TPU v7x, 32 devices: a whole 2x2x4 slice. The times are simulated.
32 devices in a mesh: cand: 4 (over y, x), hist: 8 (over z, core).
Axes of the slice: x: 2, y: 2, z: 4, core: 2. Of those that a mesh axis runs over, the one named last changes fastest.
Arguments:
- cand_x: bfloat16 [2, 1024, 1024], P(None, ('cand', 'hist')), may hold values from -6 to 6
- qu_weight: bfloat16 [1024, 2048], replicated, may hold values from -0.1875 to 0.1875
- out_weight: bfloat16 [1024, 1024], replicated, may hold values from -0.1875 to 0.1875
- k_cache: bfloat16 [131072, 1024], P('hist', 'cand'), may hold values from -1.5 to 1.5
- v_cache: bfloat16 [131072, 1024], P('hist', 'cand'), may hold values from -6 to 6
- hist_len: int32 [16], replicated, may hold values from 1 to 32768, as said below
- cand_count: int32 [2, 16], replicated, may hold values from 1 to 128, 1024 in all within a row
- tile_user: int32 [1024], P('hist'), may hold values from 0 to 16, as said below
- tile_rank: int32 [1024], P('hist'), may hold values from 0 to 255, as said below
Outputs:
- ranked: bfloat16 [2, 1024, 1024], P(None, ('cand', 'hist'))
Inputs may be any that keep to these rules, and one draw needn't show every extreme that they name: A user's history fills exactly ceil(hist_len / 128) tile slots; one user's history is 32768 rows long. `tile_user`: slot owner, 16 for an empty slot; within each hist index's 128 slots the occupied ones come first; every user owns at least one slot. `tile_rank`: each tile position 0 to ceil(hist_len[u] / 128) - 1 of every user u stands in exactly one slot; empty slots hold 0. `cand_count`: row m gives the candidates of each user in micro-batch m, numbered user by user; they sum to 1024 and one user has exactly 128.
All inputs are finite; a program needn't handle non-finite values.
Results may differ from a plain program's by a relative error of at most 0.0051.
Values may be sent and summed in bfloat16 or wider, within the bound.
No kernel may reach another device: no remote copies, remote signals or barrier semaphores. Data moves between devices by JAX's collectives and lax.ppermute only.
A program may use at most 128 MiB of HBM per device.

v0:
```python
import functools

import jax
import jax.numpy as jnp
from jax import lax
from jax.experimental import pallas as pl
from jax.experimental.pallas import tpu as pltpu
from jax.sharding import PartitionSpec as P

HEAD_DIM = 128
TILE = 128
USERS = 16
MICRO = 2
BLOCK_TILES = 8


EPSILON = 1e-06


def silu_f32(x):
    return 0.5 * x * (1.0 + jnp.tanh(0.5 * x))


def attend_kernel(
    owner_ref, rank_ref, len_ref, user_ref, last_ref, row_ref,
    q_ref, k_ref, v_ref, out_ref, user_q, user_acc, *, window, heads_here, micro,
):
    block = pl.program_id(0)
    row_ids = lax.broadcasted_iota(jnp.int32, (window, 1), 0)
    pad = jnp.zeros((8, out_ref.shape[2]), jnp.float32)

    @pl.when(block == 0)
    def _():
        user_acc[...] = jnp.zeros_like(user_acc)
        for m in range(micro):
            def fill(user, carry):
                entry = (m * USERS + user) * 4
                span = pl.ds(pl.multiple_of(user_ref[entry], 8), window + 8)
                shift = user_ref[entry + 1]
                rows = pltpu.roll(q_ref[m, span, :], (window + 8 - shift) % (window + 8), 0)
                keep = (row_ids >= user_ref[entry + 2]) & (row_ids < user_ref[entry + 3])
                user_q[pl.ds(pl.multiple_of(user * (micro * window) + m * window, window), window), :] = jnp.where(
                    keep, rows[:window], 0.0
                )
                return carry

            lax.fori_loop(0, USERS, fill, 0)

    key_ids = lax.broadcasted_iota(jnp.int32, (TILE, 1), 0)

    def one_tile(j):
        if True:
            slot = block * BLOCK_TILES + j
            user = owner_ref[slot]
            klen = jnp.where(
                user < USERS, len_ref[jnp.minimum(user, USERS - 1)] - rank_ref[slot] * TILE, 0
            )
            rows = slice(j * TILE, (j + 1) * TILE)
            keys = jnp.where(key_ids < klen, k_ref[rows, :], 0)
            values = v_ref[rows, :]
            user_rows = pl.ds(pl.multiple_of(row_ref[slot], micro * window), micro * window)
            queries = user_q[user_rows, :].astype(jnp.bfloat16)
            if heads_here == 2:
                lanes = lax.broadcasted_iota(jnp.int32, (1, 2 * HEAD_DIM), 1)
                first = lanes < HEAD_DIM

                def diagonal(tile):
                    return jnp.concatenate(
                        [jnp.where(first, tile, 0), jnp.where(first, 0, tile)], axis=0
                    )

                scores = lax.dot_general(
                    queries,
                    diagonal(keys),
                    (((1,), (1,)), ((), ())),
                    preferred_element_type=jnp.float32,
                )
                weights = silu_f32(scores).astype(jnp.bfloat16)
                user_acc[user_rows, :] += jnp.dot(
                    weights, diagonal(values), preferred_element_type=jnp.float32
                )
            else:
                parts = []
                for h in range(heads_here):
                    cols = slice(h * HEAD_DIM, (h + 1) * HEAD_DIM)
                    scores = lax.dot_general(
                        queries[:, cols],
                        keys[:, cols],
                        (((1,), (1,)), ((), ())),
                        preferred_element_type=jnp.float32,
                    )
                    weights = silu_f32(scores).astype(jnp.bfloat16)
                    parts.append(
                        jnp.dot(weights, values[:, cols], preferred_element_type=jnp.float32)
                    )
                user_acc[user_rows, :] += jnp.concatenate(parts, axis=1) if heads_here > 1 else parts[0]


    @pl.when(block <= last_ref[0])
    def _():
        for j in range(BLOCK_TILES):
            one_tile(j)

    @pl.when(block == pl.num_programs(0) - 1)
    def _():
        out_ref[...] = jnp.zeros_like(out_ref)
        for m in range(micro):
            def place(user, carry):
                entry = (m * USERS + user) * 4
                span = pl.ds(pl.multiple_of(user_ref[entry], 8), window + 8)
                first = pl.multiple_of(user * (micro * window) + m * window, window)
                sums = jnp.concatenate([user_acc[pl.ds(first, window), :], pad])
                out_ref[m, span, :] += pltpu.roll(sums, user_ref[entry + 1], 0)
                return carry

            lax.fori_loop(0, USERS, place, 0)


def reduce_over_hist(partial):
    micro, n_cand, n_hist, rows, cols = partial.shape
    chips = n_hist // 2
    me = lax.axis_index("hist")
    chip, core = me // 2, me % 2
    halves = partial.reshape(micro, n_cand, chips, 2, rows, cols)
    mine = lax.dynamic_index_in_dim(halves, core, axis=3, keepdims=False)
    theirs = lax.dynamic_index_in_dim(halves, 1 - core, axis=3, keepdims=False)
    swapped = lax.ppermute(
        theirs.astype(jnp.bfloat16), "hist", perm=[(i, i ^ 1) for i in range(n_hist)]
    )
    chip_sums = mine + swapped.astype(jnp.float32)

    def block_of(index):
        index = jnp.clip(index, 0, chips - 1)
        return lax.dynamic_index_in_dim(chip_sums, index, axis=2, keepdims=False)

    rightward = jnp.zeros_like(block_of(0))
    leftward = jnp.zeros_like(rightward)
    for step in range(1, chips):
        send_right = (block_of(chip + chips - step) + rightward).astype(jnp.bfloat16)
        send_left = (block_of(chip - chips + step) + leftward).astype(jnp.bfloat16)
        to_right = [(2 * c + k, 2 * (c + 1) + k) for c in range(step) for k in range(2)]
        to_left = [(2 * c + k, 2 * (c - 1) + k) for c in range(chips - step, chips) for k in range(2)]
        rightward = lax.ppermute(send_right, "hist", perm=to_right).astype(jnp.float32)
        leftward = lax.ppermute(send_left, "hist", perm=to_left).astype(jnp.float32)
    return block_of(chip) + rightward + leftward


def body(
    cand_x, qu_weight, out_weight, k_cache, v_cache, hist_len, cand_count, tile_user, tile_rank
):
    n_cand = lax.axis_size("cand")
    n_hist = lax.axis_size("hist")
    micro, local_rows, model_width = cand_x.shape
    head_cols = k_cache.shape[1]
    heads_here = head_cols // HEAD_DIM
    tiles_here = k_cache.shape[0] // TILE

    cand_rows = cand_x.reshape(micro * local_rows, model_width)
    projected = jax.nn.silu(jnp.dot(cand_rows, qu_weight, preferred_element_type=jnp.float32))
    queries = projected[:, :model_width].astype(jnp.bfloat16).reshape(micro, local_rows, model_width)
    gate_vals = projected[:, model_width:].astype(jnp.bfloat16)
    gathered = lax.all_gather(queries, "hist", axis=1, tiled=True)
    queries_all = lax.all_to_all(gathered, "cand", split_axis=2, concat_axis=1, tiled=True)
    all_cands = queries_all.shape[1]
    window = 2 * all_cands // USERS

    starts = jnp.cumsum(cand_count, axis=1) - cand_count
    offsets = jnp.minimum(starts, all_cands - window)
    base_rows = jnp.minimum(offsets // 8 * 8, all_cands - window - 8)
    shifts = offsets - base_rows
    lows = starts - offsets
    highs = lows + cand_count
    user_info = jnp.stack([base_rows, shifts, lows, highs], axis=2).astype(jnp.int32).reshape(-1)
    block_ids = jnp.arange(tiles_here, dtype=jnp.int32) // BLOCK_TILES
    last_block = jnp.max(jnp.where(tile_user < USERS, block_ids, 0)).reshape(1).astype(jnp.int32)

    first_rows = (jnp.minimum(tile_user, USERS - 1) * (micro * window)).astype(jnp.int32)
    rows_per_block = BLOCK_TILES * TILE
    n_blocks = tiles_here // BLOCK_TILES
    whole = pl.BlockSpec((micro, all_cands, head_cols), lambda b, *_: (0, 0, 0))
    tiles = pl.BlockSpec(
        (rows_per_block, head_cols), lambda b, *_: (jnp.minimum(b, _[4][0]), 0)
    )
    per_user = pl.BlockSpec((USERS * micro * window, head_cols), lambda b, *_: (0, 0))
    partial_value, _, _ = pl.pallas_call(
        functools.partial(attend_kernel, window=window, heads_here=heads_here, micro=micro),
        grid_spec=pltpu.PrefetchScalarGridSpec(
            num_scalar_prefetch=6,
            grid=(n_blocks,),
            in_specs=[whole, tiles, tiles],
            out_specs=[whole, per_user, per_user],
        ),
        out_shape=[
            jax.ShapeDtypeStruct((micro, all_cands, head_cols), jnp.float32),
            jax.ShapeDtypeStruct((USERS * micro * window, head_cols), jnp.float32),
            jax.ShapeDtypeStruct((USERS * micro * window, head_cols), jnp.float32),
        ],
        compiler_params=pltpu.CompilerParams(dimension_semantics=("arbitrary",)),
    )(tile_user, tile_rank, hist_len, user_info, last_block, first_rows, queries_all.astype(jnp.float32), k_cache, v_cache)

    reduced = reduce_over_hist(partial_value.reshape(micro, n_cand, n_hist, local_rows, head_cols))
    attended = lax.all_to_all(reduced, "cand", split_axis=1, concat_axis=3, tiled=True)
    attended = attended.reshape(micro * local_rows, model_width)
    average = jnp.mean(attended, axis=-1, keepdims=True)
    centered = attended - average
    spread_sq = jnp.mean(centered * centered, axis=-1, keepdims=True)
    normed = centered * lax.rsqrt(spread_sq + EPSILON)
    mixed_rows = (normed * gate_vals.astype(jnp.float32)).astype(jnp.bfloat16)
    ranked = jnp.dot(
        mixed_rows, out_weight, preferred_element_type=jnp.float32
    ) + cand_rows.astype(jnp.float32)
    return ranked.astype(jnp.bfloat16).reshape(micro, local_rows, model_width)


def solution(mesh):
    return jax.shard_map(
        body,
        mesh=mesh,
        in_specs=(
            P(None, ("cand", "hist"), None),
            P(),
            P(),
            P("hist", "cand"),
            P("hist", "cand"),
            P(),
            P(),
            P("hist"),
            P("hist"),
        ),
        out_specs=P(None, ("cand", "hist"), None),
        check_vma=False,
    )
```

profile of v0, /device:TPU:0, one launch (start us, length us, event | category | flops | bytes accessed | tf_op | source)
XLA Modules:
  0.0 146.5 jit_solution(3949613441260802577)
XLA Ops:
  6.5 0.0 copy-start
  6.5 0.0 all-gather.2.cloned.1.call-start
  6.5 3.3 %multiply_convert_fusion = bf16[64,2048]{1,0:T(8,128)(2,1)S(1)} fusion(bf16[64,1024]{1,0:T(8,128)(2,1)} %bitcast.65, bf16[1024,2048]{1,0:T(8,128)(2,1)} %param.10), kind=kOutput, calls=%fused_computation.6 | convolution fusion | flops 269090816 | bytes 4587520 | tf_op jit(solution)/shard_map/dot_general | solution.py:159
  9.8 0.8 copy.19
  10.6 0.0 all-gather.2.cloned.1.call-update
  10.7 0.0 copy-start.2
  10.7 0.0 copy-start.3
  10.7 24.9 %all-gather.2.cloned.1.call-done = bf16[2,256,1024]{2,0,1:T(2,128)(2,1)} async-done(((bf16[2,32,1024]{2,0,1:T(2,128)(2,1)}), bf16[2,256,1024]{2,0,1:T(2,128)(2,1)}) %all-gather.2.cloned.1.call-update) | async-done | bytes 1048592 | tf_op jit(solution)/shard_map/all_gather | solution.py:162
  35.6 4.9 %copy.20 = bf16[2,256,1024]{1,0,2:T(2,128)(2,1)} copy(bf16[2,256,1024]{2,0,1:T(2,128)(2,1)} %all-gather.2.cloned.1.call-done) | data formatting | bytes 2097152 | tf_op jit(solution)/shard_map/all_gather | solution.py:162
  40.5 3.6 %all-to-all-start = ((bf16[2,256,1024]{1,0,2:T(2,128)(2,1)}), bf16[2,256,1024]{1,0,2:T(2,128)(2,1)S(1)}, u32[]{:S(2)}, u32[]{:S(2)}) async-start(bf16[2,256,1024]{1,0,2:T(2,128)(2,1)} %copy.20), calls=%async_computation | async-start | bytes 2097152 | tf_op jit(solution)/shard_map/all_to_all | solution.py:163
  44.1 0.0 copy-done.2
  44.1 0.2 reduce_window_sum.11
  44.4 0.1 copy.18
  44.5 0.6 reshape.66.user_ref
  45.1 0.0 copy-done.3
  45.1 1.1 minimum_multiply_fusion
  46.2 12.1 %all-to-all-done = bf16[2,256,1024]{1,0,2:T(2,128)(2,1)S(1)} async-done(((bf16[2,256,1024]{1,0,2:T(2,128)(2,1)}), bf16[2,256,1024]{1,0,2:T(2,128)(2,1)S(1)}, u32[]{:S(2)}, u32[]{:S(2)}) %all-to-all-start) | async-done | bytes 1048608 | tf_op jit(solution)/shard_map/all_to_all | solution.py:163
  58.3 0.1 copy.21
  58.5 1.5 %convert_bitcast_fusion = f32[2,4,256,256]{2,3,1,0:T(8,128)} fusion(bf16[2,256,4,256]{1,3,2,0:T(8,128)(2,1)S(1)} %bitcast.58), kind=kLoop, calls=%fused_computation | loop fusion | flops 524288 | bytes 3145728 | tf_op jit(solution)/shard_map/convert_element_type | solution.py:199
  60.0 2.9 %copy.22 = f32[2,4,256,256]{3,2,1,0:T(8,128)} copy(f32[2,4,256,256]{2,3,1,0:T(8,128)} %convert_bitcast_fusion) | data formatting | bytes 4194304 | tf_op jit(solution)/shard_map/convert_element_type | solution.py:199
  62.9 29.0 %shard_map.91 = (f32[2,1024,256]{2,1,0:T(8,128)}, f32[4096,256]{1,0:T(8,128)}, f32[4096,256]{1,0:T(8,128)}) custom-call(s32[128]{0:T(128)} %owner_ref.1, s32[128]{0:T(128)} %rank_ref.1, s32[16]{0:T(128)} %len_ref.1, s32[128]{0:T(128)} %reshape.66.user_ref, s32[1]{0:T(128)} %bitcast.4.last_ref, s32[128]{0:T(128)} %get-tuple-element.15.row_ref, ...), custom_call_target="tpu_custom_call" | custom-call | tf_op jit(solution)/shard_map/pallas_call | solution.py:185
  91.9 1.3 fusion.1
  93.2 0.1 collective-permute-start
  93.3 2.0 %collective-permute-done = bf16[2,4,4,32,256]{4,3,0,1,2:T(8,128)(2,1)} collective-permute-done((bf16[2,4,4,32,256]{4,3,0,1,2:T(8,128)(2,1)S(1)}, bf16[2,4,4,32,256]{4,3,0,1,2:T(8,128)(2,1)}, u32[]{:S(2)}, u32[]{:S(2)}) %collective-permute-start) | collective-permute-done | bytes 524320 | tf_op jit(solution)/shard_map/ppermute | solution.py:127
  95.3 1.5 %bitcast_add_fusion = f32[2,4,4,32,256]{4,3,0,1,2:T(8,128)S(1)} fusion(bf16[2,4,4,32,256]{4,3,0,1,2:T(8,128)(2,1)} %collective-permute-done, f32[2,4,4,2,32,256]{5,4,3,2,1,0:T(8,128)} %bitcast.61, s32[]{:T(128)S(6)} %select_n.44), kind=kLoop, calls=%fused_computation.4 | loop fusion | flops 524288 | bytes 2621444 | tf_op jit(solution)/shard_map/add | solution.py:130
  96.8 0.7 fusion.7
  97.6 1.3 collective-permute-start.1
  98.9 1.3 collective-permute-start.4
  100.2 2.3 %collective-permute-done.1 = bf16[2,4,32,256]{3,2,0,1:T(8,128)(2,1)S(1)} collective-permute-done((bf16[2,4,32,256]{3,2,0,1:T(8,128)(2,1)}, bf16[2,4,32,256]{3,2,0,1:T(8,128)(2,1)S(1)}, u32[]{:S(2)}, u32[]{:S(2)}) %collective-permute-start.1) | collective-permute-done | bytes 131104 | tf_op jit(solution)/shard_map/ppermute | solution.py:143
  102.5 0.7 fusion.4
  103.2 4.9 %collective-permute-start.2 = (bf16[2,4,32,256]{3,2,0,1:T(8,128)(2,1)}, bf16[2,4,32,256]{3,2,0,1:T(8,128)(2,1)}, u32[]{:S(2)}, u32[]{:S(2)}) collective-permute-start(bf16[2,4,32,256]{3,2,0,1:T(8,128)(2,1)} %fusion.4), channel_id=1, source_target_pairs={{0,2},{1,3},{2,4},{3,5},{8,10},{9,11},{10,12},{11,13},{16,18},{17,... | collective-permute-start | bytes 393224 | tf_op jit(solution)/shard_map/ppermute | solution.py:143
  108.1 0.0 copy-start.1
  108.1 0.0 collective-permute-done.4
  108.1 2.2 %collective-permute-done.2 = bf16[2,4,32,256]{3,2,0,1:T(8,128)(2,1)} collective-permute-done((bf16[2,4,32,256]{3,2,0,1:T(8,128)(2,1)}, bf16[2,4,32,256]{3,2,0,1:T(8,128)(2,1)}, u32[]{:S(2)}, u32[]{:S(2)}) %collective-permute-start.2) | collective-permute-done | bytes 131104 | tf_op jit(solution)/shard_map/ppermute | solution.py:143
  110.3 1.7 %fusion.5 = (bf16[2,4,32,256]{3,2,0,1:T(8,128)(2,1)}, bf16[2,4,32,256]{3,2,0,1:T(8,128)(2,1)}) fusion(bf16[2,4,32,256]{3,2,0,1:T(8,128)(2,1)} %collective-permute-done.2, f32[2,4,4,32,256]{4,3,0,1,2:T(8,128)S(1)} %bitcast_add_fusion, s32[]{:T(128)S(6)} %min.47, bf16[2,4,32,256]{3,2,0,1:T(8,128)(2,1)} %collective-permute-done.4, s32[]{:T(128)S(6)} %min.51), kind=kLoop, calls=%fused_computation.14 | loop fusion | flops 393216 | bytes 1048584 | tf_op jit(solution)/shard_map/convert_element_type | solution.py:139
  112.1 1.3 collective-permute-start.5
  113.4 5.0 %collective-permute-start.3 = (bf16[2,4,32,256]{3,2,0,1:T(8,128)(2,1)}, bf16[2,4,32,256]{3,2,0,1:T(8,128)(2,1)}, u32[]{:S(2)}, u32[]{:S(2)}) collective-permute-start(bf16[2,4,32,256]{3,2,0,1:T(8,128)(2,1)} %get-tuple-element.9), channel_id=1, source_target_pairs={{0,2},{1,3},{2,4},{3,5},{4,6},{5,7},{8,10},{9,11},{10,12},{11,13},... | collective-permute-start | bytes 393224 | tf_op jit(solution)/shard_map/ppermute | solution.py:143
  118.4 0.0 collective-permute-done.5
  118.4 1.6 %fusion.3 = bf16[2,4,32,256]{3,2,0,1:T(8,128)(2,1)} fusion(bf16[2,4,32,256]{3,2,0,1:T(8,128)(2,1)} %collective-permute-done.5, f32[2,4,4,32,256]{4,3,0,1,2:T(8,128)S(1)} %bitcast_add_fusion, s32[]{:T(128)S(6)} %min.50), kind=kLoop, calls=%fused_computation.10 | loop fusion | flops 196608 | bytes 524292 | tf_op jit(solution)/shard_map/convert_element_type | solution.py:140
  120.0 1.3 collective-permute-start.6
  121.3 0.0 collective-permute-done.3
  121.3 7.2 %collective-permute-done.6 = bf16[2,4,32,256]{3,2,0,1:T(8,128)(2,1)} collective-permute-done((bf16[2,4,32,256]{3,2,0,1:T(8,128)(2,1)}, bf16[2,4,32,256]{3,2,0,1:T(8,128)(2,1)}, u32[]{:S(2)}, u32[]{:S(2)}) %collective-permute-start.6) | collective-permute-done | bytes 131104 | tf_op jit(solution)/shard_map/ppermute | solution.py:144
  128.4 1.0 fusion.6
  129.5 8.3 %all_to_all.24 = f32[2,4,32,256]{3,2,0,1:T(8,128)S(1)} all-to-all(f32[2,4,32,256]{3,2,0,1:T(8,128)S(1)} %fusion.6), channel_id=1, replica_groups=mesh['cand'=4,'hist'=8] {'cand'}, dimensions={1} | all-to-all | bytes 524288 | tf_op jit(solution)/shard_map/all_to_all | solution.py:202
  137.7 0.2 copy.25
  137.9 0.1 bitcast_reduce_fusion
  138.1 0.1 div.51
  138.1 0.2 multiply_reduce_fusion
  138.3 0.1 rsqrt.12
  138.4 0.0 copy-done
  138.4 0.0 copy-done.1
  138.4 1.2 fusion
  (6 shorter events, 0.1 us)
Async XLA Ops:
  6.5 131.9 %copy-start = (bf16[1024,1024]{1,0:T(8,128)(2,1)S(1)}, bf16[1024,1024]{1,0:T(8,128)(2,1)}, u32[]{:S(2)}) copy-start(bf16[1024,1024]{1,0:T(8,128)(2,1)} %param.11) | copy-start | bytes 6291460
  6.5 29.1 %all-gather.2.cloned.1.call-start = ((), (), s32[]{:S(2)}) async-start(), calls=%async_computation.2 | async-start | bytes 1179648 | tf_op jit(solution)/shard_map/all_gather | solution.py:162
  10.7 33.5 %copy-start.2 = (s32[2,16]{1,0:T(2,128)S(1)}, s32[2,16]{1,0:T(2,128)}, u32[]{:S(2)}) copy-start(s32[2,16]{1,0:T(2,128)} %param.15) | copy-start | bytes 388
  10.7 34.4 %copy-start.3 = (s32[128]{0:T(128)S(1)}, s32[128]{0:T(128)}, u32[]{:S(2)}) copy-start(s32[128]{0:T(128)} %owner_ref.1) | copy-start | bytes 1540
  40.5 17.8 %all-to-all-start = ((bf16[2,256,1024]{1,0,2:T(2,128)(2,1)}), bf16[2,256,1024]{1,0,2:T(2,128)(2,1)S(1)}, u32[]{:S(2)}, u32[]{:S(2)}) async-start(bf16[2,256,1024]{1,0,2:T(2,128)(2,1)} %copy.20), calls=%async_computation | async-start | bytes 2097152 | tf_op jit(solution)/shard_map/all_to_all | solution.py:163
  93.2 2.1 %collective-permute-start = (bf16[2,4,4,32,256]{4,3,0,1,2:T(8,128)(2,1)S(1)}, bf16[2,4,4,32,256]{4,3,0,1,2:T(8,128)(2,1)}, u32[]{:S(2)}, u32[]{:S(2)}) collective-permute-start(bf16[2,4,4,32,256]{4,3,0,1,2:T(8,128)(2,1)S(1)} %fusion.1), channel_id=1, source_target_pairs={{0,1},{1,0},{2,3},{3,2},{4,5},{5,4},{6,7},{7,6},{8,9},{9,8},{10,11... | collective-permute-start | bytes 1572872 | tf_op jit(solution)/shard_map/ppermute | solution.py:127
  97.6 4.9 %collective-permute-start.1 = (bf16[2,4,32,256]{3,2,0,1:T(8,128)(2,1)}, bf16[2,4,32,256]{3,2,0,1:T(8,128)(2,1)S(1)}, u32[]{:S(2)}, u32[]{:S(2)}) collective-permute-start(bf16[2,4,32,256]{3,2,0,1:T(8,128)(2,1)} %get-tuple-element.11), channel_id=1, source_target_pairs={{0,2},{1,3},{8,10},{9,11},{16,18},{17,19},{24,26},{25,27}} | collective-permute-start | bytes 393224 | tf_op jit(solution)/shard_map/ppermute | solution.py:143
  98.9 9.2 %collective-permute-start.4 = (bf16[2,4,32,256]{3,2,0,1:T(8,128)(2,1)}, bf16[2,4,32,256]{3,2,0,1:T(8,128)(2,1)}, u32[]{:S(2)}, u32[]{:S(2)}) collective-permute-start(bf16[2,4,32,256]{3,2,0,1:T(8,128)(2,1)} %get-tuple-element.12), channel_id=1, source_target_pairs={{6,4},{7,5},{14,12},{15,13},{22,20},{23,21},{30,28},{31,29}} | collective-permute-start | bytes 393224 | tf_op jit(solution)/shard_map/ppermute | solution.py:144
  103.2 7.1 %collective-permute-start.2 = (bf16[2,4,32,256]{3,2,0,1:T(8,128)(2,1)}, bf16[2,4,32,256]{3,2,0,1:T(8,128)(2,1)}, u32[]{:S(2)}, u32[]{:S(2)}) collective-permute-start(bf16[2,4,32,256]{3,2,0,1:T(8,128)(2,1)} %fusion.4), channel_id=1, source_target_pairs={{0,2},{1,3},{2,4},{3,5},{8,10},{9,11},{10,12},{11,13},{16,18},{17,... | collective-permute-start | bytes 393224 | tf_op jit(solution)/shard_map/ppermute | solution.py:143
  108.1 30.3 %copy-start.1 = (bf16[2,32,1024]{2,1,0:T(8,128)(2,1)S(1)}, bf16[2,32,1024]{2,1,0:T(8,128)(2,1)}, u32[]{:S(2)}) copy-start(bf16[2,32,1024]{2,1,0:T(8,128)(2,1)} %param.9) | copy-start | bytes 393220
  112.1 6.3 %collective-permute-start.5 = (bf16[2,4,32,256]{3,2,0,1:T(8,128)(2,1)}, bf16[2,4,32,256]{3,2,0,1:T(8,128)(2,1)}, u32[]{:S(2)}, u32[]{:S(2)}) collective-permute-start(bf16[2,4,32,256]{3,2,0,1:T(8,128)(2,1)} %get-tuple-element.10), channel_id=1, source_target_pairs={{4,2},{5,3},{6,4},{7,5},{12,10},{13,11},{14,12},{15,13},{20,18},{2... | collective-permute-start | bytes 393224 | tf_op jit(solution)/shard_map/ppermute | solution.py:144
  113.4 7.9 %collective-permute-start.3 = (bf16[2,4,32,256]{3,2,0,1:T(8,128)(2,1)}, bf16[2,4,32,256]{3,2,0,1:T(8,128)(2,1)}, u32[]{:S(2)}, u32[]{:S(2)}) collective-permute-start(bf16[2,4,32,256]{3,2,0,1:T(8,128)(2,1)} %get-tuple-element.9), channel_id=1, source_target_pairs={{0,2},{1,3},{2,4},{3,5},{4,6},{5,7},{8,10},{9,11},{10,12},{11,13},... | collective-permute-start | bytes 393224 | tf_op jit(solution)/shard_map/ppermute | solution.py:143
  120.0 8.5 %collective-permute-start.6 = (bf16[2,4,32,256]{3,2,0,1:T(8,128)(2,1)}, bf16[2,4,32,256]{3,2,0,1:T(8,128)(2,1)}, u32[]{:S(2)}, u32[]{:S(2)}) collective-permute-start(bf16[2,4,32,256]{3,2,0,1:T(8,128)(2,1)} %fusion.3), channel_id=1, source_target_pairs={{2,0},{3,1},{4,2},{5,3},{6,4},{7,5},{10,8},{11,9},{12,10},{13,11},... | collective-permute-start | bytes 393224 | tf_op jit(solution)/shard_map/ppermute | solution.py:144
Sparse Core Ops, SparseCore 0:
  10.8 24.7 all-gather.1
where the time goes:
time: 149 us; the launch traced here: 146 us
  waiting for transfers between devices  50.7 us (34%)
  Pallas kernels  29 us (19%)
  starting transfers between devices  18.8 us (13%)
  between operations  13.6 us (9%)
  local copies, waits for them, and re-layouts  11.9 us (8%)
  other arithmetic  9.74 us (7%)
  blocking collectives  8.26 us (6%)
  matrix products  4.47 us (3%)
    pallas_call x1, Pallas kernels, body(): pl.pallas_call(functools.partial(attend_kernel, window=window, heads_here...  29 us
    all_gather x1, waiting for transfers between devices, body(): gathered = lax.all_gather(queries, 'hist', axis=1, tiled=True)  24.9 us
    all_to_all x1, waiting for transfers between devices, body(): lax.all_to_all(gathered, 'cand', split_axis=2, concat_axis=1, tiled=True)  12.1 us
    ppermute x3, starting transfers between devices, reduce_over_hist(): lax.ppermute(send_right, 'hist', perm=to_right).astype(jnp.float32)  11.2 us
    all_to_all x1, blocking collectives, body(): lax.all_to_all(reduced, 'cand', split_axis=1, concat_axis=3, tiled=True)  8.26 us
    ppermute x3, waiting for transfers between devices, reduce_over_hist(): leftward = lax.ppermute(send_left, 'hist', perm=to_left).astype(jnp.float32)  7.16 us
    all_gather x1, local copies, waits for them, and re-layouts, body(): gathered = lax.all_gather(queries, 'hist', axis=1, tiled=True)  4.9 us
    ppermute x3, waiting for transfers between devices, reduce_over_hist(): lax.ppermute(send_right, 'hist', perm=to_right).astype(jnp.float32)  4.51 us
  transfers between devices with their start and end apart: 9, of which 6 were waited for; matrix products, arithmetic and copies ran while one was open for 3% of the time, Pallas kernels for 0%

commit v1 on v0

--- a/solution.py
+++ b/solution.py
@@ -145,6 +145,52 @@
     return block_of(chip) + rightward + leftward
 
 
+def gather_queries(queries, n_cand, n_hist):
+    micro, rows, width = queries.shape
+    group = width // n_cand
+    me_cand = lax.axis_index("cand")
+    chunks = queries.reshape(micro, rows, n_cand, group)
+    received = []
+    for shift in range(n_cand):
+        target = (me_cand + shift) % n_cand
+        piece = lax.dynamic_index_in_dim(chunks, target, axis=2, keepdims=False)
+        if shift:
+            piece = lax.ppermute(
+                piece, "cand", perm=[(i, (i + shift) % n_cand) for i in range(n_cand)]
+            )
+        received.append(piece)
+    by_offset = jnp.stack(received)
+    sources = jnp.stack(
+        [
+            lax.dynamic_index_in_dim(by_offset, (me_cand - c) % n_cand, axis=0, keepdims=False)
+            for c in range(n_cand)
+        ]
+    )
+    chips = n_hist // 2
+    me = lax.axis_index("hist")
+    chip, core = me // 2, me % 2
+    rightward, leftward = [], []
+    send_right = send_left = sources
+    for step in range(1, chips):
+        to_right = [(2 * c + k, 2 * (c + 1) + k) for c in range(step - 1, chips - 1) for k in range(2)]
+        to_left = [(2 * c + k, 2 * (c - 1) + k) for c in range(1, chips - step + 1) for k in range(2)]
+        send_right = lax.ppermute(send_right, "hist", perm=to_right)
+        send_left = lax.ppermute(send_left, "hist", perm=to_left)
+        rightward.append(send_right)
+        leftward.append(send_left)
+    by_distance = jnp.stack(leftward[::-1] + [sources] + rightward)
+    mine = jnp.stack(
+        [
+            lax.dynamic_index_in_dim(by_distance, chips - 1 + chip - c, axis=0, keepdims=False)
+            for c in range(chips)
+        ]
+    )
+    theirs = lax.ppermute(mine, "hist", perm=[(i, i ^ 1) for i in range(n_hist)])
+    both = jnp.where(core == 0, jnp.stack([mine, theirs], axis=1), jnp.stack([theirs, mine], axis=1))
+    both = both.reshape(n_hist, n_cand, micro, rows, group)
+    return jnp.transpose(both, (2, 1, 0, 3, 4)).reshape(micro, n_cand * n_hist * rows, group)
+
+
 def body(
     cand_x, qu_weight, out_weight, k_cache, v_cache, hist_len, cand_count, tile_user, tile_rank
 ):
@@ -159,8 +205,7 @@
     projected = jax.nn.silu(jnp.dot(cand_rows, qu_weight, preferred_element_type=jnp.float32))
     queries = projected[:, :model_width].astype(jnp.bfloat16).reshape(micro, local_rows, model_width)
     gate_vals = projected[:, model_width:].astype(jnp.bfloat16)
-    gathered = lax.all_gather(queries, "hist", axis=1, tiled=True)
-    queries_all = lax.all_to_all(gathered, "cand", split_axis=2, concat_axis=1, tiled=True)
+    queries_all = gather_queries(queries, n_cand, n_hist)
     all_cands = queries_all.shape[1]
     window = 2 * all_cands // USERS
 

time: 149 us -> 118 us (0.79); the launches traced: 146 us -> 117 us
  waiting for transfers between devices: 50.7 us -> 28.3 us
  between operations: 13.6 us -> 0.43 us
  starting transfers between devices: 18.8 us -> 30.4 us
  local copies, waits for them, and re-layouts: 11.9 us -> 5.4 us
    all_gather x1 -> x0, waiting for transfers between devices: 24.9 us -> none  [body(): gathered = lax.all_gather(queries, 'hist', axis=1, tiled=True)]
    ppermute x0 -> x10, starting transfers between devices: none -> 14.9 us  [the longest x3 5.87 us: gather_queries(): send_right = lax.ppermute(send_right, 'hist', perm=to_right)]
    ppermute x0 -> x10, waiting for transfers between devices: none -> 14.8 us  [the longest x3 10.3 us: gather_queries(): send_left = lax.ppermute(send_left, 'hist', perm=to_left)]
    all_to_all x1 -> x0, waiting for transfers between devices: 12.1 us -> none  [body(): lax.all_to_all(gathered, 'cand', split_axis=2, concat_axis=1, tiled=True)]
    all_gather x1 -> x0, local copies, waits for them, and re-layouts: 4.9 us -> none  [body(): gathered = lax.all_gather(queries, 'hist', axis=1, tiled=True)]
    all_to_all x1 -> x0, starting transfers between devices: 3.64 us -> none  [body(): lax.all_to_all(gathered, 'cand', split_axis=2, concat_axis=1, tiled=True)]
  transfers between devices with their start and end apart: 9 -> 17, of which waited for: 6 -> 10; matrix products, arithmetic and copies ran while one was open for 3% -> 4% of each run, Pallas kernels for 0% -> 0%
where the time goes in v1:
time: 118 us; the launch traced here: 117 us
  starting transfers between devices  30.4 us (26%)
  Pallas kernels  30.3 us (26%)
  waiting for transfers between devices  28.3 us (24%)
  other arithmetic  9.89 us (8%)
  blocking collectives  8.31 us (7%)
  local copies, waits for them, and re-layouts  5.4 us (5%)
  matrix products  4.46 us (4%)
    pallas_call x1, Pallas kernels, body(): pl.pallas_call(functools.partial(attend_kernel, window=window, heads_here...  30.3 us
    ppermute x3, starting transfers between devices, reduce_over_hist(): lax.ppermute(send_right, 'hist', perm=to_right).astype(jnp.float32)  11.6 us
    ppermute x3, waiting for transfers between devices, gather_queries(): send_left = lax.ppermute(send_left, 'hist', perm=to_left)  10.3 us
    all_to_all x1, blocking collectives, body(): lax.all_to_all(reduced, 'cand', split_axis=1, concat_axis=3, tiled=True)  8.31 us
    ppermute x3, waiting for transfers between devices, reduce_over_hist(): leftward = lax.ppermute(send_left, 'hist', perm=to_left).astype(jnp.float32)  7.14 us
    ppermute x3, starting transfers between devices, gather_queries(): send_right = lax.ppermute(send_right, 'hist', perm=to_right)  5.87 us
    ppermute x3, starting transfers between devices, gather_queries(): lax.ppermute(piece, 'cand', perm=[(i, (i + shift) % n_cand) for i in rang...  5.06 us
    ppermute x3, waiting for transfers between devices, reduce_over_hist(): lax.ppermute(send_right, 'hist', perm=to_right).astype(jnp.float32)  4.4 us
  transfers between devices with their start and end apart: 17, of which 10 were waited for; matrix products, arithmetic and copies ran while one was open for 4% of the time, Pallas kernels for 0%

profile of v1, /device:TPU:0, one launch (start us, length us, event | category | flops | bytes accessed | tf_op | source)
XLA Modules:
  0.0 117.5 jit_solution(9430468358686781236)
XLA Ops:
  0.0 0.0 copy-start
  0.0 3.3 %multiply_convert_fusion = bf16[64,2048]{1,0:T(8,128)(2,1)S(1)} fusion(bf16[64,1024]{1,0:T(8,128)(2,1)} %bitcast.94, bf16[1024,2048]{1,0:T(8,128)(2,1)} %param.10), kind=kOutput, calls=%fused_computation.8 | convolution fusion | flops 269090816 | bytes 4587520 | tf_op jit(solution)/shard_map/dot_general | solution.py:205
  3.3 0.0 copy-start.2
  3.3 0.1 reshape_reshape.6
  3.4 0.3 constant_dynamic-slice_fusion.13
  3.7 3.0 %collective-permute-start.1 = (bf16[2,32,256]{2,1,0:T(8,128)(2,1)S(1)}, bf16[2,32,256]{2,1,0:T(8,128)(2,1)S(1)}, u32[]{:S(2)}, u32[]{:S(2)}) collective-permute-start(bf16[2,32,256]{2,1,0:T(8,128)(2,1)S(1)} %bitcast.97), channel_id=1, source_target_pairs={{0,16},{8,24},{16,0},{24,8},{1,17},{9,25},{17,1},{25,9},{2,18},{10... | collective-permute-start | bytes 98312 | tf_op jit(solution)/shard_map/ppermute | solution.py:158
  6.8 1.4 %collective-permute-start.2 = (bf16[2,32,256]{2,1,0:T(8,128)(2,1)S(1)}, bf16[2,32,256]{2,1,0:T(8,128)(2,1)S(1)}, u32[]{:S(2)}, u32[]{:S(2)}) collective-permute-start(bf16[2,32,256]{2,1,0:T(8,128)(2,1)S(1)} %bitcast.98), channel_id=1, source_target_pairs={{0,24},{8,0},{16,8},{24,16},{1,25},{9,1},{17,9},{25,17},{2,26},{10... | collective-permute-start | bytes 98312 | tf_op jit(solution)/shard_map/ppermute | solution.py:158
  8.2 0.6 collective-permute-start
  8.8 0.0 collective-permute-done.1
  8.8 1.9 %collective-permute-done.2 = bf16[2,32,256]{2,1,0:T(8,128)(2,1)S(1)} collective-permute-done((bf16[2,32,256]{2,1,0:T(8,128)(2,1)S(1)}, bf16[2,32,256]{2,1,0:T(8,128)(2,1)S(1)}, u32[]{:S(2)}, u32[]{:S(2)}) %collective-permute-start.2) | collective-permute-done | bytes 32800 | tf_op jit(solution)/shard_map/ppermute | solution.py:158
  10.7 2.3 %collective-permute-done = bf16[2,32,256]{2,1,0:T(8,128)(2,1)S(1)} collective-permute-done((bf16[2,32,256]{2,1,0:T(8,128)(2,1)S(1)}, bf16[2,32,256]{2,1,0:T(8,128)(2,1)S(1)}, u32[]{:S(2)}, u32[]{:S(2)}) %collective-permute-start) | collective-permute-done | bytes 32800 | tf_op jit(solution)/shard_map/ppermute | solution.py:158
  13.1 1.3 %collective-permute-start.3 = (bf16[4,2,32,256]{3,2,1,0:T(8,128)(2,1)S(1)}, bf16[4,2,32,256]{3,2,1,0:T(8,128)(2,1)S(1)}, u32[]{:S(2)}, u32[]{:S(2)}) collective-permute-start(bf16[4,2,32,256]{3,2,1,0:T(8,128)(2,1)S(1)} %pad_maximum_fusion.2), channel_id=1, source_target_pairs={{2,0},{3,1},{4,2},{5,3},{6,4},{7,5},{10,8},{11,9},{12,10},{13,11},... | collective-permute-start | bytes 393224 | tf_op jit(solution)/shard_map/ppermute | solution.py:178
  14.4 4.6 %collective-permute-start.6 = (bf16[4,2,32,256]{3,2,1,0:T(8,128)(2,1)S(1)}, bf16[4,2,32,256]{3,2,1,0:T(8,128)(2,1)S(1)}, u32[]{:S(2)}, u32[]{:S(2)}) collective-permute-start(bf16[4,2,32,256]{3,2,1,0:T(8,128)(2,1)S(1)} %pad_maximum_fusion.2), channel_id=1, source_target_pairs={{0,2},{1,3},{2,4},{3,5},{4,6},{5,7},{8,10},{9,11},{10,12},{11,13},... | collective-permute-start | bytes 393224 | tf_op jit(solution)/shard_map/ppermute | solution.py:177
  19.0 1.0 collective-permute-done.3
  20.0 1.3 %collective-permute-start.4 = (bf16[4,2,32,256]{3,2,1,0:T(8,128)(2,1)S(1)}, bf16[4,2,32,256]{3,2,1,0:T(8,128)(2,1)S(1)}, u32[]{:S(2)}, u32[]{:S(2)}) collective-permute-start(bf16[4,2,32,256]{3,2,1,0:T(8,128)(2,1)S(1)} %collective-permute-done.3), channel_id=1, source_target_pairs={{2,0},{3,1},{4,2},{5,3},{10,8},{11,9},{12,10},{13,11},{18,16},{19,... | collective-permute-start | bytes 393224 | tf_op jit(solution)/shard_map/ppermute | solution.py:178
  21.2 0.2 collective-permute-done.6
  21.5 0.7 collective-permute-start.7
  22.1 4.7 %collective-permute-done.4 = bf16[4,2,32,256]{3,2,1,0:T(8,128)(2,1)S(1)} collective-permute-done((bf16[4,2,32,256]{3,2,1,0:T(8,128)(2,1)S(1)}, bf16[4,2,32,256]{3,2,1,0:T(8,128)(2,1)S(1)}, u32[]{:S(2)}, u32[]{:S(2)}) %collective-permute-start.4) | collective-permute-done | bytes 131104 | tf_op jit(solution)/shard_map/ppermute | solution.py:178
  26.8 1.3 %collective-permute-start.5 = (bf16[4,2,32,256]{3,2,1,0:T(8,128)(2,1)S(1)}, bf16[4,2,32,256]{3,2,1,0:T(8,128)(2,1)S(1)}, u32[]{:S(2)}, u32[]{:S(2)}) collective-permute-start(bf16[4,2,32,256]{3,2,1,0:T(8,128)(2,1)S(1)} %collective-permute-done.4), channel_id=1, source_target_pairs={{2,0},{3,1},{10,8},{11,9},{18,16},{19,17},{26,24},{27,25}} | collective-permute-start | bytes 393224 | tf_op jit(solution)/shard_map/ppermute | solution.py:178
  28.1 0.0 copy-done.2
  28.1 0.2 reduce_window_sum.11
  28.3 0.0 collective-permute-done.7
  28.3 0.7 collective-permute-start.8
  29.0 4.7 %collective-permute-done.5 = bf16[4,2,32,256]{3,2,1,0:T(8,128)(2,1)S(1)} collective-permute-done((bf16[4,2,32,256]{3,2,1,0:T(8,128)(2,1)S(1)}, bf16[4,2,32,256]{3,2,1,0:T(8,128)(2,1)S(1)}, u32[]{:S(2)}, u32[]{:S(2)}) %collective-permute-start.5) | collective-permute-done | bytes 131104 | tf_op jit(solution)/shard_map/ppermute | solution.py:178
  33.7 0.0 copy-start.3
  33.8 0.0 collective-permute-done.8
  33.9 0.1 fusion.15
  34.0 0.1 collective-permute-start.9
  34.1 0.1 copy.35
  34.2 0.6 reshape.70.user_ref
  34.8 1.3 %minimum_multiply_fusion = (s32[128]{0:T(128)}, s32[]{:T(128)}) fusion(s32[128]{0:T(128)S(1)} %copy-done.3), kind=kLoop, calls=%fused_computation.73 | loop fusion | flops 1663 | bytes 1028 | tf_op jit(solution)/shard_map/mul | solution.py:222
  36.1 0.0 collective-permute-done.9
  36.1 1.4 %fusion.1 = f32[4,2,4,2,32,256]{5,4,3,2,0,1:T(8,128)S(1)} fusion(bf16[4,1,4,2,32,256]{5,4,3,2,0,1:T(8,128)(2,1)} %bitcast.21, bf16[4,1,4,2,32,256]{5,4,3,2,0,1:T(8,128)(2,1)S(1)} %get-tuple-element.17, pred[]{:T(512)S(6)} %eq.14), kind=kLoop, calls=%fused_computation.3 | loop fusion | flops 2097152 | bytes 3145729 | tf_op jit(solution)/shard_map/convert_element_type | solution.py:244
  37.5 0.2 copy.40
  37.7 1.5 %copy.41 = f32[2,4,8,32,256]{4,3,2,1,0:T(8,128)} copy(f32[2,4,8,32,256]{4,3,0,1,2:T(8,128)S(1)} %bitcast.88) | data formatting | bytes 4194304 | tf_op jit(solution)/shard_map/convert_element_type | solution.py:244
  39.2 30.3 %shard_map.91 = (f32[2,1024,256]{2,1,0:T(8,128)}, f32[4096,256]{1,0:T(8,128)}, f32[4096,256]{1,0:T(8,128)}) custom-call(s32[128]{0:T(128)} %owner_ref.1, s32[128]{0:T(128)} %rank_ref.1, s32[16]{0:T(128)} %len_ref.1, s32[128]{0:T(128)} %reshape.70.user_ref, s32[1]{0:T(128)} %bitcast.4.last_ref, s32[128]{0:T(128)} %get-tuple-element.29.row_ref, ...), custom_call_target="tpu_custom_call" | custom-call | tf_op jit(solution)/shard_map/pallas_call | solution.py:230
  69.5 1.3 %fusion.2 = bf16[2,4,4,32,256]{4,3,0,1,2:T(8,128)(2,1)S(1)} fusion(f32[2,4,4,2,32,256]{5,4,3,2,1,0:T(8,128)} %bitcast.90, s32[]{:T(128)S(6)} %select_n.146), kind=kLoop, calls=%fused_computation.6 | loop fusion | bytes 1048580 | tf_op jit(solution)/shard_map/convert_element_type | solution.py:128
  70.8 0.1 collective-permute-start.10
  70.9 2.0 %collective-permute-done.10 = bf16[2,4,4,32,256]{4,3,0,1,2:T(8,128)(2,1)} collective-permute-done((bf16[2,4,4,32,256]{4,3,0,1,2:T(8,128)(2,1)S(1)}, bf16[2,4,4,32,256]{4,3,0,1,2:T(8,128)(2,1)}, u32[]{:S(2)}, u32[]{:S(2)}) %collective-permute-start.10) | collective-permute-done | bytes 524320 | tf_op jit(solution)/shard_map/ppermute | solution.py:127
  72.9 1.5 %bitcast_add_fusion = f32[2,4,4,32,256]{4,3,0,1,2:T(8,128)S(1)} fusion(bf16[2,4,4,32,256]{4,3,0,1,2:T(8,128)(2,1)} %collective-permute-done.10, f32[2,4,4,2,32,256]{5,4,3,2,1,0:T(8,128)} %bitcast.91, s32[]{:T(128)S(6)} %select_n.145), kind=kLoop, calls=%fused_computation.5 | loop fusion | flops 524288 | bytes 2621444 | tf_op jit(solution)/shard_map/add | solution.py:130
  74.4 0.7 fusion.8
  75.2 1.6 %collective-permute-start.11 = (bf16[2,4,32,256]{3,2,0,1:T(8,128)(2,1)}, bf16[2,4,32,256]{3,2,0,1:T(8,128)(2,1)S(1)}, u32[]{:S(2)}, u32[]{:S(2)}) collective-permute-start(bf16[2,4,32,256]{3,2,0,1:T(8,128)(2,1)} %get-tuple-element.11), channel_id=1, source_target_pairs={{0,2},{1,3},{8,10},{9,11},{16,18},{17,19},{24,26},{25,27}} | collective-permute-start | bytes 393224 | tf_op jit(solution)/shard_map/ppermute | solution.py:143
  76.8 1.3 %collective-permute-start.14 = (bf16[2,4,32,256]{3,2,0,1:T(8,128)(2,1)}, bf16[2,4,32,256]{3,2,0,1:T(8,128)(2,1)}, u32[]{:S(2)}, u32[]{:S(2)}) collective-permute-start(bf16[2,4,32,256]{3,2,0,1:T(8,128)(2,1)} %get-tuple-element.12), channel_id=1, source_target_pairs={{6,4},{7,5},{14,12},{15,13},{22,20},{23,21},{30,28},{31,29}} | collective-permute-start | bytes 393224 | tf_op jit(solution)/shard_map/ppermute | solution.py:144
  78.1 2.2 %collective-permute-done.11 = bf16[2,4,32,256]{3,2,0,1:T(8,128)(2,1)S(1)} collective-permute-done((bf16[2,4,32,256]{3,2,0,1:T(8,128)(2,1)}, bf16[2,4,32,256]{3,2,0,1:T(8,128)(2,1)S(1)}, u32[]{:S(2)}, u32[]{:S(2)}) %collective-permute-start.11) | collective-permute-done | bytes 131104 | tf_op jit(solution)/shard_map/ppermute | solution.py:143
  80.4 0.7 fusion.5
  81.1 4.9 %collective-permute-start.12 = (bf16[2,4,32,256]{3,2,0,1:T(8,128)(2,1)}, bf16[2,4,32,256]{3,2,0,1:T(8,128)(2,1)}, u32[]{:S(2)}, u32[]{:S(2)}) collective-permute-start(bf16[2,4,32,256]{3,2,0,1:T(8,128)(2,1)} %fusion.5), channel_id=1, source_target_pairs={{0,2},{1,3},{2,4},{3,5},{8,10},{9,11},{10,12},{11,13},{16,18},{17,... | collective-permute-start | bytes 393224 | tf_op jit(solution)/shard_map/ppermute | solution.py:143
  86.0 0.0 collective-permute-done.14
  86.0 2.1 %collective-permute-done.12 = bf16[2,4,32,256]{3,2,0,1:T(8,128)(2,1)} collective-permute-done((bf16[2,4,32,256]{3,2,0,1:T(8,128)(2,1)}, bf16[2,4,32,256]{3,2,0,1:T(8,128)(2,1)}, u32[]{:S(2)}, u32[]{:S(2)}) %collective-permute-start.12) | collective-permute-done | bytes 131104 | tf_op jit(solution)/shard_map/ppermute | solution.py:143
  88.2 1.7 %fusion.6 = (bf16[2,4,32,256]{3,2,0,1:T(8,128)(2,1)}, bf16[2,4,32,256]{3,2,0,1:T(8,128)(2,1)}) fusion(bf16[2,4,32,256]{3,2,0,1:T(8,128)(2,1)} %collective-permute-done.12, f32[2,4,4,32,256]{4,3,0,1,2:T(8,128)S(1)} %bitcast_add_fusion, s32[]{:T(128)S(6)} %min.47, bf16[2,4,32,256]{3,2,0,1:T(8,128)(2,1)} %collective-permute-done.14, s32[]{:T(128)S(6)} %min.51), kind=kLoop, calls=%fused_computation.16 | loop fusion | flops 393216 | bytes 1048584 | tf_op jit(solution)/shard_map/convert_element_type | solution.py:139
  89.9 1.3 %collective-permute-start.15 = (bf16[2,4,32,256]{3,2,0,1:T(8,128)(2,1)}, bf16[2,4,32,256]{3,2,0,1:T(8,128)(2,1)}, u32[]{:S(2)}, u32[]{:S(2)}) collective-permute-start(bf16[2,4,32,256]{3,2,0,1:T(8,128)(2,1)} %get-tuple-element.10), channel_id=1, source_target_pairs={{4,2},{5,3},{6,4},{7,5},{12,10},{13,11},{14,12},{15,13},{20,18},{2... | collective-permute-start | bytes 393224 | tf_op jit(solution)/shard_map/ppermute | solution.py:144
  91.2 5.0 %collective-permute-start.13 = (bf16[2,4,32,256]{3,2,0,1:T(8,128)(2,1)}, bf16[2,4,32,256]{3,2,0,1:T(8,128)(2,1)}, u32[]{:S(2)}, u32[]{:S(2)}) collective-permute-start(bf16[2,4,32,256]{3,2,0,1:T(8,128)(2,1)} %get-tuple-element.9), channel_id=1, source_target_pairs={{0,2},{1,3},{2,4},{3,5},{4,6},{5,7},{8,10},{9,11},{10,12},{11,13},... | collective-permute-start | bytes 393224 | tf_op jit(solution)/shard_map/ppermute | solution.py:143
  96.2 0.0 collective-permute-done.15
  96.2 1.6 %fusion.4 = bf16[2,4,32,256]{3,2,0,1:T(8,128)(2,1)} fusion(bf16[2,4,32,256]{3,2,0,1:T(8,128)(2,1)} %collective-permute-done.15, f32[2,4,4,32,256]{4,3,0,1,2:T(8,128)S(1)} %bitcast_add_fusion, s32[]{:T(128)S(6)} %min.50), kind=kLoop, calls=%fused_computation.12 | loop fusion | flops 196608 | bytes 524292 | tf_op jit(solution)/shard_map/convert_element_type | solution.py:140
  97.8 1.3 %collective-permute-start.16 = (bf16[2,4,32,256]{3,2,0,1:T(8,128)(2,1)}, bf16[2,4,32,256]{3,2,0,1:T(8,128)(2,1)}, u32[]{:S(2)}, u32[]{:S(2)}) collective-permute-start(bf16[2,4,32,256]{3,2,0,1:T(8,128)(2,1)} %fusion.4), channel_id=1, source_target_pairs={{2,0},{3,1},{4,2},{5,3},{6,4},{7,5},{10,8},{11,9},{12,10},{13,11},... | collective-permute-start | bytes 393224 | tf_op jit(solution)/shard_map/ppermute | solution.py:144
  99.1 0.0 collective-permute-done.13
  99.1 7.1 %collective-permute-done.16 = bf16[2,4,32,256]{3,2,0,1:T(8,128)(2,1)} collective-permute-done((bf16[2,4,32,256]{3,2,0,1:T(8,128)(2,1)}, bf16[2,4,32,256]{3,2,0,1:T(8,128)(2,1)}, u32[]{:S(2)}, u32[]{:S(2)}) %collective-permute-start.16) | collective-permute-done | bytes 131104 | tf_op jit(solution)/shard_map/ppermute | solution.py:144
  106.3 1.0 fusion.7
  107.3 8.3 %all_to_all.15 = f32[2,4,32,256]{3,2,0,1:T(8,128)S(1)} all-to-all(f32[2,4,32,256]{3,2,0,1:T(8,128)S(1)} %fusion.7), channel_id=1, replica_groups=mesh['cand'=4,'hist'=8] {'cand'}, dimensions={1} | all-to-all | bytes 524288 | tf_op jit(solution)/shard_map/all_to_all | solution.py:247
  115.6 0.1 bitcast_reduce_fusion
  115.7 0.1 div.52
  115.8 0.2 multiply_reduce_fusion
  116.0 0.1 rsqrt.12
  116.0 0.2 copy.44
  116.3 1.2 %fusion = bf16[64,1024]{1,0:T(8,128)(2,1)} fusion(bf16[1024,1024]{1,0:T(8,128)(2,1)S(1)} %copy-done, bf16[64,1024]{1,0:T(8,128)(2,1)S(1)} %bitcast.95, f32[64,1024]{1,0:T(8,128)S(1)} %bitcast.92, bf16[64,2048]{1,0:T(8,128)(2,1)S(1)} %multiply_convert_fusion, f32[64]{0:T(128)S(1)} %rsqrt.12, f32[64]{0:T(128)S(1)} %div.52), kind=kOutput, calls=%fused_computation.1 | convolution fusion | flops 134742016 | bytes 2753536 | tf_op jit(solution)/shard_map/dot_general | solution.py:254
  (25 shorter events, 0.3 us)
Async XLA Ops:
  0.0 116.3 %copy-start = (bf16[1024,1024]{1,0:T(8,128)(2,1)S(1)}, bf16[1024,1024]{1,0:T(8,128)(2,1)}, u32[]{:S(2)}) copy-start(bf16[1024,1024]{1,0:T(8,128)(2,1)} %param.11) | copy-start | bytes 6291460
  3.3 24.9 %copy-start.2 = (s32[2,16]{1,0:T(2,128)S(1)}, s32[2,16]{1,0:T(2,128)}, u32[]{:S(2)}) copy-start(s32[2,16]{1,0:T(2,128)} %param.15) | copy-start | bytes 388
  3.7 5.1 %collective-permute-start.1 = (bf16[2,32,256]{2,1,0:T(8,128)(2,1)S(1)}, bf16[2,32,256]{2,1,0:T(8,128)(2,1)S(1)}, u32[]{:S(2)}, u32[]{:S(2)}) collective-permute-start(bf16[2,32,256]{2,1,0:T(8,128)(2,1)S(1)} %bitcast.97), channel_id=1, source_target_pairs={{0,16},{8,24},{16,0},{24,8},{1,17},{9,25},{17,1},{25,9},{2,18},{10... | collective-permute-start | bytes 98312 | tf_op jit(solution)/shard_map/ppermute | solution.py:158
  6.8 3.9 %collective-permute-start.2 = (bf16[2,32,256]{2,1,0:T(8,128)(2,1)S(1)}, bf16[2,32,256]{2,1,0:T(8,128)(2,1)S(1)}, u32[]{:S(2)}, u32[]{:S(2)}) collective-permute-start(bf16[2,32,256]{2,1,0:T(8,128)(2,1)S(1)} %bitcast.98), channel_id=1, source_target_pairs={{0,24},{8,0},{16,8},{24,16},{1,25},{9,1},{17,9},{25,17},{2,26},{10... | collective-permute-start | bytes 98312 | tf_op jit(solution)/shard_map/ppermute | solution.py:158
  8.2 4.8 %collective-permute-start = (bf16[2,32,256]{2,1,0:T(8,128)(2,1)S(1)}, bf16[2,32,256]{2,1,0:T(8,128)(2,1)S(1)}, u32[]{:S(2)}, u32[]{:S(2)}) collective-permute-start(bf16[2,32,256]{2,1,0:T(8,128)(2,1)S(1)} %bitcast.99), channel_id=1, source_target_pairs={{0,8},{8,16},{16,24},{24,0},{1,9},{9,17},{17,25},{25,1},{2,10},{10... | collective-permute-start | bytes 98312 | tf_op jit(solution)/shard_map/ppermute | solution.py:158
  13.1 6.9 %collective-permute-start.3 = (bf16[4,2,32,256]{3,2,1,0:T(8,128)(2,1)S(1)}, bf16[4,2,32,256]{3,2,1,0:T(8,128)(2,1)S(1)}, u32[]{:S(2)}, u32[]{:S(2)}) collective-permute-start(bf16[4,2,32,256]{3,2,1,0:T(8,128)(2,1)S(1)} %pad_maximum_fusion.2), channel_id=1, source_target_pairs={{2,0},{3,1},{4,2},{5,3},{6,4},{7,5},{10,8},{11,9},{12,10},{13,11},... | collective-permute-start | bytes 393224 | tf_op jit(solution)/shard_map/ppermute | solution.py:178
  14.4 7.1 %collective-permute-start.6 = (bf16[4,2,32,256]{3,2,1,0:T(8,128)(2,1)S(1)}, bf16[4,2,32,256]{3,2,1,0:T(8,128)(2,1)S(1)}, u32[]{:S(2)}, u32[]{:S(2)}) collective-permute-start(bf16[4,2,32,256]{3,2,1,0:T(8,128)(2,1)S(1)} %pad_maximum_fusion.2), channel_id=1, source_target_pairs={{0,2},{1,3},{2,4},{3,5},{4,6},{5,7},{8,10},{9,11},{10,12},{11,13},... | collective-permute-start | bytes 393224 | tf_op jit(solution)/shard_map/ppermute | solution.py:177
  20.0 6.8 %collective-permute-start.4 = (bf16[4,2,32,256]{3,2,1,0:T(8,128)(2,1)S(1)}, bf16[4,2,32,256]{3,2,1,0:T(8,128)(2,1)S(1)}, u32[]{:S(2)}, u32[]{:S(2)}) collective-permute-start(bf16[4,2,32,256]{3,2,1,0:T(8,128)(2,1)S(1)} %collective-permute-done.3), channel_id=1, source_target_pairs={{2,0},{3,1},{4,2},{5,3},{10,8},{11,9},{12,10},{13,11},{18,16},{19,... | collective-permute-start | bytes 393224 | tf_op jit(solution)/shard_map/ppermute | solution.py:178
  21.5 6.9 %collective-permute-start.7 = (bf16[4,2,32,256]{3,2,1,0:T(8,128)(2,1)S(1)}, bf16[4,2,32,256]{3,2,1,0:T(8,128)(2,1)S(1)}, u32[]{:S(2)}, u32[]{:S(2)}) collective-permute-start(bf16[4,2,32,256]{3,2,1,0:T(8,128)(2,1)S(1)} %collective-permute-done.6), channel_id=1, source_target_pairs={{2,4},{3,5},{4,6},{5,7},{10,12},{11,13},{12,14},{13,15},{18,20},{1... | collective-permute-start | bytes 393224 | tf_op jit(solution)/shard_map/ppermute | solution.py:177
  26.8 6.8 %collective-permute-start.5 = (bf16[4,2,32,256]{3,2,1,0:T(8,128)(2,1)S(1)}, bf16[4,2,32,256]{3,2,1,0:T(8,128)(2,1)S(1)}, u32[]{:S(2)}, u32[]{:S(2)}) collective-permute-start(bf16[4,2,32,256]{3,2,1,0:T(8,128)(2,1)S(1)} %collective-permute-done.4), channel_id=1, source_target_pairs={{2,0},{3,1},{10,8},{11,9},{18,16},{19,17},{26,24},{27,25}} | collective-permute-start | bytes 393224 | tf_op jit(solution)/shard_map/ppermute | solution.py:178
  28.3 5.4 %collective-permute-start.8 = (bf16[4,2,32,256]{3,2,1,0:T(8,128)(2,1)S(1)}, bf16[4,2,32,256]{3,2,1,0:T(8,128)(2,1)S(1)}, u32[]{:S(2)}, u32[]{:S(2)}) collective-permute-start(bf16[4,2,32,256]{3,2,1,0:T(8,128)(2,1)S(1)} %collective-permute-done.7), channel_id=1, source_target_pairs={{4,6},{5,7},{12,14},{13,15},{20,22},{21,23},{28,30},{29,31}} | collective-permute-start | bytes 393224 | tf_op jit(solution)/shard_map/ppermute | solution.py:177
  33.7 1.1 copy-start.3
  34.0 2.1 %collective-permute-start.9 = (bf16[4,4,2,32,256]{4,3,2,1,0:T(8,128)(2,1)S(1)}, bf16[4,4,2,32,256]{4,3,2,1,0:T(8,128)(2,1)}, u32[]{:S(2)}, u32[]{:S(2)}) collective-permute-start(bf16[4,4,2,32,256]{4,3,2,1,0:T(8,128)(2,1)S(1)} %get-tuple-element.18), channel_id=1, source_target_pairs={{0,1},{1,0},{2,3},{3,2},{4,5},{5,4},{6,7},{7,6},{8,9},{9,8},{10,11... | collective-permute-start | bytes 1572872 | tf_op jit(solution)/shard_map/ppermute | solution.py:188
  70.8 2.1 %collective-permute-start.10 = (bf16[2,4,4,32,256]{4,3,0,1,2:T(8,128)(2,1)S(1)}, bf16[2,4,4,32,256]{4,3,0,1,2:T(8,128)(2,1)}, u32[]{:S(2)}, u32[]{:S(2)}) collective-permute-start(bf16[2,4,4,32,256]{4,3,0,1,2:T(8,128)(2,1)S(1)} %fusion.2), channel_id=1, source_target_pairs={{0,1},{1,0},{2,3},{3,2},{4,5},{5,4},{6,7},{7,6},{8,9},{9,8},{10,11... | collective-permute-start | bytes 1572872 | tf_op jit(solution)/shard_map/ppermute | solution.py:127
  75.2 5.2 %collective-permute-start.11 = (bf16[2,4,32,256]{3,2,0,1:T(8,128)(2,1)}, bf16[2,4,32,256]{3,2,0,1:T(8,128)(2,1)S(1)}, u32[]{:S(2)}, u32[]{:S(2)}) collective-permute-start(bf16[2,4,32,256]{3,2,0,1:T(8,128)(2,1)} %get-tuple-element.11), channel_id=1, source_target_pairs={{0,2},{1,3},{8,10},{9,11},{16,18},{17,19},{24,26},{25,27}} | collective-permute-start | bytes 393224 | tf_op jit(solution)/shard_map/ppermute | solution.py:143
  76.8 9.2 %collective-permute-start.14 = (bf16[2,4,32,256]{3,2,0,1:T(8,128)(2,1)}, bf16[2,4,32,256]{3,2,0,1:T(8,128)(2,1)}, u32[]{:S(2)}, u32[]{:S(2)}) collective-permute-start(bf16[2,4,32,256]{3,2,0,1:T(8,128)(2,1)} %get-tuple-element.12), channel_id=1, source_target_pairs={{6,4},{7,5},{14,12},{15,13},{22,20},{23,21},{30,28},{31,29}} | collective-permute-start | bytes 393224 | tf_op jit(solution)/shard_map/ppermute | solution.py:144
  81.1 7.1 %collective-permute-start.12 = (bf16[2,4,32,256]{3,2,0,1:T(8,128)(2,1)}, bf16[2,4,32,256]{3,2,0,1:T(8,128)(2,1)}, u32[]{:S(2)}, u32[]{:S(2)}) collective-permute-start(bf16[2,4,32,256]{3,2,0,1:T(8,128)(2,1)} %fusion.5), channel_id=1, source_target_pairs={{0,2},{1,3},{2,4},{3,5},{8,10},{9,11},{10,12},{11,13},{16,18},{17,... | collective-permute-start | bytes 393224 | tf_op jit(solution)/shard_map/ppermute | solution.py:143
  86.0 30.3 %copy-start.1 = (bf16[2,32,1024]{2,1,0:T(8,128)(2,1)S(1)}, bf16[2,32,1024]{2,1,0:T(8,128)(2,1)}, u32[]{:S(2)}) copy-start(bf16[2,32,1024]{2,1,0:T(8,128)(2,1)} %param.9) | copy-start | bytes 393220
  89.9 6.3 %collective-permute-start.15 = (bf16[2,4,32,256]{3,2,0,1:T(8,128)(2,1)}, bf16[2,4,32,256]{3,2,0,1:T(8,128)(2,1)}, u32[]{:S(2)}, u32[]{:S(2)}) collective-permute-start(bf16[2,4,32,256]{3,2,0,1:T(8,128)(2,1)} %get-tuple-element.10), channel_id=1, source_target_pairs={{4,2},{5,3},{6,4},{7,5},{12,10},{13,11},{14,12},{15,13},{20,18},{2... | collective-permute-start | bytes 393224 | tf_op jit(solution)/shard_map/ppermute | solution.py:144
  91.2 7.9 %collective-permute-start.13 = (bf16[2,4,32,256]{3,2,0,1:T(8,128)(2,1)}, bf16[2,4,32,256]{3,2,0,1:T(8,128)(2,1)}, u32[]{:S(2)}, u32[]{:S(2)}) collective-permute-start(bf16[2,4,32,256]{3,2,0,1:T(8,128)(2,1)} %get-tuple-element.9), channel_id=1, source_target_pairs={{0,2},{1,3},{2,4},{3,5},{4,6},{5,7},{8,10},{9,11},{10,12},{11,13},... | collective-permute-start | bytes 393224 | tf_op jit(solution)/shard_map/ppermute | solution.py:143
  97.8 8.4 %collective-permute-start.16 = (bf16[2,4,32,256]{3,2,0,1:T(8,128)(2,1)}, bf16[2,4,32,256]{3,2,0,1:T(8,128)(2,1)}, u32[]{:S(2)}, u32[]{:S(2)}) collective-permute-start(bf16[2,4,32,256]{3,2,0,1:T(8,128)(2,1)} %fusion.4), channel_id=1, source_target_pairs={{2,0},{3,1},{4,2},{5,3},{6,4},{7,5},{10,8},{11,9},{12,10},{13,11},... | collective-permute-start | bytes 393224 | tf_op jit(solution)/shard_map/ppermute | solution.py:144

commit v2 on v1

--- a/solution.py
+++ b/solution.py
@@ -191,6 +191,27 @@
     return jnp.transpose(both, (2, 1, 0, 3, 4)).reshape(micro, n_cand * n_hist * rows, group)
 
 
+def spread_over_cand(reduced):
+    micro, n_cand, rows, group = reduced.shape
+    me = lax.axis_index("cand")
+    received = []
+    for shift in range(n_cand):
+        piece = lax.dynamic_index_in_dim(reduced, (me + shift) % n_cand, axis=1, keepdims=False)
+        if shift:
+            piece = lax.ppermute(
+                piece, "cand", perm=[(i, (i + shift) % n_cand) for i in range(n_cand)]
+            )
+        received.append(piece)
+    by_offset = jnp.stack(received)
+    return jnp.concatenate(
+        [
+            lax.dynamic_index_in_dim(by_offset, (me - c) % n_cand, axis=0, keepdims=False)
+            for c in range(n_cand)
+        ],
+        axis=-1,
+    )
+
+
 def body(
     cand_x, qu_weight, out_weight, k_cache, v_cache, hist_len, cand_count, tile_user, tile_rank
 ):
@@ -244,7 +265,7 @@
     )(tile_user, tile_rank, hist_len, user_info, last_block, first_rows, queries_all.astype(jnp.float32), k_cache, v_cache)
 
     reduced = reduce_over_hist(partial_value.reshape(micro, n_cand, n_hist, local_rows, head_cols))
-    attended = lax.all_to_all(reduced, "cand", split_axis=1, concat_axis=3, tiled=True)
+    attended = spread_over_cand(reduced)
     attended = attended.reshape(micro * local_rows, model_width)
     average = jnp.mean(attended, axis=-1, keepdims=True)
     centered = attended - average

time: 118 us -> 114 us (0.966)
  blocking collectives: 8.31 us -> 0 us
  starting transfers between devices: 30.4 us -> 34.6 us
  waiting for transfers between devices: 28.3 us -> 30.4 us
    all_to_all x1 -> x0, blocking collectives: 8.31 us -> none  [body(): lax.all_to_all(reduced, 'cand', split_axis=1, concat_axis=3, tiled=True)]
    ppermute x0 -> x3, starting transfers between devices: none -> 4.5 us  [spread_over_cand(): lax.ppermute(piece, 'cand', perm=[(i, (i + shift) % n_cand) for i in rang...]
    ppermute x0 -> x3, waiting for transfers between devices: none -> 1.9 us  [spread_over_cand(): lax.ppermute(piece, 'cand', perm=[(i, (i + shift) % n_cand) for i in rang...]
  transfers between devices with their start and end apart: 17 -> 20, of which waited for: 10 -> 12; matrix products, arithmetic and copies ran while one was open for 4% -> 4% of each run, Pallas kernels for 0% -> 0%
where the time goes in v2:
time: 114 us
  starting transfers between devices  34.6 us (30%)
  waiting for transfers between devices  30.4 us (27%)
  Pallas kernels  29.2 us (26%)
  other arithmetic  9.91 us (9%)
  local copies, waits for them, and re-layouts  5.11 us (4%)
  matrix products  4.46 us (4%)
    pallas_call x1, Pallas kernels, body(): pl.pallas_call(functools.partial(attend_kernel, window=window, heads_here...  29.2 us
    ppermute x3, starting transfers between devices, reduce_over_hist(): lax.ppermute(send_right, 'hist', perm=to_right).astype(jnp.float32)  11.2 us
    ppermute x3, waiting for transfers between devices, gather_queries(): send_left = lax.ppermute(send_left, 'hist', perm=to_left)  10.3 us
    ppermute x3, waiting for transfers between devices, reduce_over_hist(): leftward = lax.ppermute(send_left, 'hist', perm=to_left).astype(jnp.float32)  7.16 us
    ppermute x3, starting transfers between devices, gather_queries(): send_right = lax.ppermute(send_right, 'hist', perm=to_right)  5.87 us
    ppermute x3, starting transfers between devices, gather_queries(): lax.ppermute(piece, 'cand', perm=[(i, (i + shift) % n_cand) for i in rang...  5.06 us
    ppermute x3, waiting for transfers between devices, reduce_over_hist(): lax.ppermute(send_right, 'hist', perm=to_right).astype(jnp.float32)  4.5 us
    ppermute x3, starting transfers between devices, spread_over_cand(): lax.ppermute(piece, 'cand', perm=[(i, (i + shift) % n_cand) for i in rang...  4.5 us
  transfers between devices with their start and end apart: 20, of which 12 were waited for; matrix products, arithmetic and copies ran while one was open for 4% of the time, Pallas kernels for 0%

profile of v2, /device:TPU:0, one launch (start us, length us, event | category | flops | bytes accessed | tf_op | source)
XLA Modules:
  0.0 114.0 jit_solution(1783549885963203122)
XLA Ops:
  0.0 3.3 %multiply_convert_fusion = bf16[64,2048]{1,0:T(8,128)(2,1)S(1)} fusion(bf16[64,1024]{1,0:T(8,128)(2,1)} %bitcast.109, bf16[1024,2048]{1,0:T(8,128)(2,1)} %param.10), kind=kOutput, calls=%fused_computation.8 | convolution fusion | flops 269090816 | bytes 4587520 | tf_op jit(solution)/shard_map/dot_general | solution.py:226
  3.3 0.0 copy-start.2
  3.3 0.1 reshape_reshape.6
  3.4 0.3 constant_dynamic-slice_fusion.15
  3.7 3.0 %collective-permute-start.1 = (bf16[2,32,256]{2,1,0:T(8,128)(2,1)S(1)}, bf16[2,32,256]{2,1,0:T(8,128)(2,1)S(1)}, u32[]{:S(2)}, u32[]{:S(2)}) collective-permute-start(bf16[2,32,256]{2,1,0:T(8,128)(2,1)S(1)} %bitcast.115), channel_id=1, source_target_pairs={{0,16},{8,24},{16,0},{24,8},{1,17},{9,25},{17,1},{25,9},{2,18},{10... | collective-permute-start | bytes 98312 | tf_op jit(solution)/shard_map/ppermute | solution.py:158
  6.8 1.4 %collective-permute-start.2 = (bf16[2,32,256]{2,1,0:T(8,128)(2,1)S(1)}, bf16[2,32,256]{2,1,0:T(8,128)(2,1)S(1)}, u32[]{:S(2)}, u32[]{:S(2)}) collective-permute-start(bf16[2,32,256]{2,1,0:T(8,128)(2,1)S(1)} %bitcast.116), channel_id=1, source_target_pairs={{0,24},{8,0},{16,8},{24,16},{1,25},{9,1},{17,9},{25,17},{2,26},{10... | collective-permute-start | bytes 98312 | tf_op jit(solution)/shard_map/ppermute | solution.py:158
  8.2 0.6 collective-permute-start
  8.8 0.0 collective-permute-done.1
  8.8 1.9 %collective-permute-done.2 = bf16[2,32,256]{2,1,0:T(8,128)(2,1)S(1)} collective-permute-done((bf16[2,32,256]{2,1,0:T(8,128)(2,1)S(1)}, bf16[2,32,256]{2,1,0:T(8,128)(2,1)S(1)}, u32[]{:S(2)}, u32[]{:S(2)}) %collective-permute-start.2) | collective-permute-done | bytes 32800 | tf_op jit(solution)/shard_map/ppermute | solution.py:158
  10.7 2.3 %collective-permute-done = bf16[2,32,256]{2,1,0:T(8,128)(2,1)S(1)} collective-permute-done((bf16[2,32,256]{2,1,0:T(8,128)(2,1)S(1)}, bf16[2,32,256]{2,1,0:T(8,128)(2,1)S(1)}, u32[]{:S(2)}, u32[]{:S(2)}) %collective-permute-start) | collective-permute-done | bytes 32800 | tf_op jit(solution)/shard_map/ppermute | solution.py:158
  13.1 1.3 %collective-permute-start.3 = (bf16[4,2,32,256]{3,2,1,0:T(8,128)(2,1)S(1)}, bf16[4,2,32,256]{3,2,1,0:T(8,128)(2,1)S(1)}, u32[]{:S(2)}, u32[]{:S(2)}) collective-permute-start(bf16[4,2,32,256]{3,2,1,0:T(8,128)(2,1)S(1)} %pad_maximum_fusion.3), channel_id=1, source_target_pairs={{2,0},{3,1},{4,2},{5,3},{6,4},{7,5},{10,8},{11,9},{12,10},{13,11},... | collective-permute-start | bytes 393224 | tf_op jit(solution)/shard_map/ppermute | solution.py:178
  14.4 4.6 %collective-permute-start.6 = (bf16[4,2,32,256]{3,2,1,0:T(8,128)(2,1)S(1)}, bf16[4,2,32,256]{3,2,1,0:T(8,128)(2,1)S(1)}, u32[]{:S(2)}, u32[]{:S(2)}) collective-permute-start(bf16[4,2,32,256]{3,2,1,0:T(8,128)(2,1)S(1)} %pad_maximum_fusion.3), channel_id=1, source_target_pairs={{0,2},{1,3},{2,4},{3,5},{4,6},{5,7},{8,10},{9,11},{10,12},{11,13},... | collective-permute-start | bytes 393224 | tf_op jit(solution)/shard_map/ppermute | solution.py:177
  19.0 1.0 collective-permute-done.3
  20.0 1.3 %collective-permute-start.4 = (bf16[4,2,32,256]{3,2,1,0:T(8,128)(2,1)S(1)}, bf16[4,2,32,256]{3,2,1,0:T(8,128)(2,1)S(1)}, u32[]{:S(2)}, u32[]{:S(2)}) collective-permute-start(bf16[4,2,32,256]{3,2,1,0:T(8,128)(2,1)S(1)} %collective-permute-done.3), channel_id=1, source_target_pairs={{2,0},{3,1},{4,2},{5,3},{10,8},{11,9},{12,10},{13,11},{18,16},{19,... | collective-permute-start | bytes 393224 | tf_op jit(solution)/shard_map/ppermute | solution.py:178
  21.2 0.2 collective-permute-done.6
  21.5 0.7 collective-permute-start.7
  22.1 4.7 %collective-permute-done.4 = bf16[4,2,32,256]{3,2,1,0:T(8,128)(2,1)S(1)} collective-permute-done((bf16[4,2,32,256]{3,2,1,0:T(8,128)(2,1)S(1)}, bf16[4,2,32,256]{3,2,1,0:T(8,128)(2,1)S(1)}, u32[]{:S(2)}, u32[]{:S(2)}) %collective-permute-start.4) | collective-permute-done | bytes 131104 | tf_op jit(solution)/shard_map/ppermute | solution.py:178
  26.8 1.3 %collective-permute-start.5 = (bf16[4,2,32,256]{3,2,1,0:T(8,128)(2,1)S(1)}, bf16[4,2,32,256]{3,2,1,0:T(8,128)(2,1)S(1)}, u32[]{:S(2)}, u32[]{:S(2)}) collective-permute-start(bf16[4,2,32,256]{3,2,1,0:T(8,128)(2,1)S(1)} %collective-permute-done.4), channel_id=1, source_target_pairs={{2,0},{3,1},{10,8},{11,9},{18,16},{19,17},{26,24},{27,25}} | collective-permute-start | bytes 393224 | tf_op jit(solution)/shard_map/ppermute | solution.py:178
  28.1 0.2 reduce_window_sum.11
  28.3 0.0 collective-permute-done.7
  28.3 0.7 collective-permute-start.8
  29.0 4.7 %collective-permute-done.5 = bf16[4,2,32,256]{3,2,1,0:T(8,128)(2,1)S(1)} collective-permute-done((bf16[4,2,32,256]{3,2,1,0:T(8,128)(2,1)S(1)}, bf16[4,2,32,256]{3,2,1,0:T(8,128)(2,1)S(1)}, u32[]{:S(2)}, u32[]{:S(2)}) %collective-permute-start.5) | collective-permute-done | bytes 131104 | tf_op jit(solution)/shard_map/ppermute | solution.py:178
  33.7 0.0 copy-start.3
  33.8 0.0 collective-permute-done.8
  33.9 0.1 fusion.16
  34.0 0.1 collective-permute-start.9
  34.1 0.1 copy.24
  34.2 0.6 reshape.60.user_ref
  34.8 1.3 %minimum_multiply_fusion = (s32[128]{0:T(128)}, s32[]{:T(128)}) fusion(s32[128]{0:T(128)S(1)} %copy-done.3), kind=kLoop, calls=%fused_computation.81 | loop fusion | flops 1663 | bytes 1028 | tf_op jit(solution)/shard_map/mul | solution.py:243
  36.0 0.0 collective-permute-done.9
  36.1 1.4 %fusion.1 = f32[4,2,4,2,32,256]{5,4,3,2,0,1:T(8,128)S(1)} fusion(bf16[4,1,4,2,32,256]{5,4,3,2,0,1:T(8,128)(2,1)} %bitcast.21, bf16[4,1,4,2,32,256]{5,4,3,2,0,1:T(8,128)(2,1)S(1)} %get-tuple-element.25, pred[]{:T(512)S(6)} %eq.22), kind=kLoop, calls=%fused_computation.3 | loop fusion | flops 2097152 | bytes 3145729 | tf_op jit(solution)/shard_map/convert_element_type | solution.py:265
  37.5 0.2 copy.29
  37.7 1.5 %copy.30 = f32[2,4,8,32,256]{4,3,2,1,0:T(8,128)} copy(f32[2,4,8,32,256]{4,3,0,1,2:T(8,128)S(1)} %bitcast.98) | data formatting | bytes 4194304 | tf_op jit(solution)/shard_map/convert_element_type | solution.py:265
  39.2 29.2 %shard_map.91 = (f32[2,1024,256]{2,1,0:T(8,128)}, f32[4096,256]{1,0:T(8,128)}, f32[4096,256]{1,0:T(8,128)}) custom-call(s32[128]{0:T(128)} %owner_ref.1, s32[128]{0:T(128)} %rank_ref.1, s32[16]{0:T(128)} %len_ref.1, s32[128]{0:T(128)} %reshape.60.user_ref, s32[1]{0:T(128)} %bitcast.4.last_ref, s32[128]{0:T(128)} %get-tuple-element.47.row_ref, ...), custom_call_target="tpu_custom_call" | custom-call | tf_op jit(solution)/shard_map/pallas_call | solution.py:251
  68.4 1.3 %fusion.2 = bf16[2,4,4,32,256]{4,3,2,1,0:T(8,128)(2,1)S(1)} fusion(f32[2,4,4,2,32,256]{5,4,3,2,1,0:T(8,128)} %bitcast.99, s32[]{:T(128)S(6)} %select_n.172), kind=kLoop, calls=%fused_computation.6 | loop fusion | bytes 1048580 | tf_op jit(solution)/shard_map/convert_element_type | solution.py:128
  69.7 0.1 collective-permute-start.10
  69.8 2.0 %collective-permute-done.10 = bf16[2,4,4,32,256]{4,3,2,1,0:T(8,128)(2,1)} collective-permute-done((bf16[2,4,4,32,256]{4,3,2,1,0:T(8,128)(2,1)S(1)}, bf16[2,4,4,32,256]{4,3,2,1,0:T(8,128)(2,1)}, u32[]{:S(2)}, u32[]{:S(2)}) %collective-permute-start.10) | collective-permute-done | bytes 524320 | tf_op jit(solution)/shard_map/ppermute | solution.py:127
  71.8 1.5 %bitcast_add_fusion = f32[2,4,4,32,256]{4,3,2,1,0:T(8,128)S(1)} fusion(bf16[2,4,4,32,256]{4,3,2,1,0:T(8,128)(2,1)} %collective-permute-done.10, f32[2,4,4,2,32,256]{5,4,3,2,1,0:T(8,128)} %bitcast.100, s32[]{:T(128)S(6)} %select_n.171), kind=kLoop, calls=%fused_computation.4 | loop fusion | flops 524288 | bytes 2621444 | tf_op jit(solution)/shard_map/add | solution.py:130
  73.3 0.7 fusion.9
  74.1 1.3 %collective-permute-start.11 = (bf16[2,4,32,256]{3,2,1,0:T(8,128)(2,1)}, bf16[2,4,32,256]{3,2,1,0:T(8,128)(2,1)S(1)}, u32[]{:S(2)}, u32[]{:S(2)}) collective-permute-start(bf16[2,4,32,256]{3,2,1,0:T(8,128)(2,1)} %get-tuple-element.19), channel_id=1, source_target_pairs={{0,2},{1,3},{8,10},{9,11},{16,18},{17,19},{24,26},{25,27}} | collective-permute-start | bytes 393224 | tf_op jit(solution)/shard_map/ppermute | solution.py:143
  75.4 1.3 %collective-permute-start.14 = (bf16[2,4,32,256]{3,2,1,0:T(8,128)(2,1)}, bf16[2,4,32,256]{3,2,1,0:T(8,128)(2,1)}, u32[]{:S(2)}, u32[]{:S(2)}) collective-permute-start(bf16[2,4,32,256]{3,2,1,0:T(8,128)(2,1)} %get-tuple-element.20), channel_id=1, source_target_pairs={{6,4},{7,5},{14,12},{15,13},{22,20},{23,21},{30,28},{31,29}} | collective-permute-start | bytes 393224 | tf_op jit(solution)/shard_map/ppermute | solution.py:144
  76.7 2.3 %collective-permute-done.11 = bf16[2,4,32,256]{3,2,1,0:T(8,128)(2,1)S(1)} collective-permute-done((bf16[2,4,32,256]{3,2,1,0:T(8,128)(2,1)}, bf16[2,4,32,256]{3,2,1,0:T(8,128)(2,1)S(1)}, u32[]{:S(2)}, u32[]{:S(2)}) %collective-permute-start.11) | collective-permute-done | bytes 131104 | tf_op jit(solution)/shard_map/ppermute | solution.py:143
  79.0 0.7 fusion.5
  79.7 4.9 %collective-permute-start.12 = (bf16[2,4,32,256]{3,2,1,0:T(8,128)(2,1)}, bf16[2,4,32,256]{3,2,1,0:T(8,128)(2,1)}, u32[]{:S(2)}, u32[]{:S(2)}) collective-permute-start(bf16[2,4,32,256]{3,2,1,0:T(8,128)(2,1)} %fusion.5), channel_id=1, source_target_pairs={{0,2},{1,3},{2,4},{3,5},{8,10},{9,11},{10,12},{11,13},{16,18},{17,... | collective-permute-start | bytes 393224 | tf_op jit(solution)/shard_map/ppermute | solution.py:143
  84.6 0.0 collective-permute-done.14
  84.6 2.2 %collective-permute-done.12 = bf16[2,4,32,256]{3,2,1,0:T(8,128)(2,1)} collective-permute-done((bf16[2,4,32,256]{3,2,1,0:T(8,128)(2,1)}, bf16[2,4,32,256]{3,2,1,0:T(8,128)(2,1)}, u32[]{:S(2)}, u32[]{:S(2)}) %collective-permute-start.12) | collective-permute-done | bytes 131104 | tf_op jit(solution)/shard_map/ppermute | solution.py:143
  86.8 1.7 %fusion.6 = (bf16[2,4,32,256]{3,2,1,0:T(8,128)(2,1)}, bf16[2,4,32,256]{3,2,1,0:T(8,128)(2,1)}) fusion(bf16[2,4,32,256]{3,2,1,0:T(8,128)(2,1)} %collective-permute-done.12, f32[2,4,4,32,256]{4,3,2,1,0:T(8,128)S(1)} %bitcast_add_fusion, s32[]{:T(128)S(6)} %min.47, bf16[2,4,32,256]{3,2,1,0:T(8,128)(2,1)} %collective-permute-done.14, s32[]{:T(128)S(6)} %min.51), kind=kLoop, calls=%fused_computation.19 | loop fusion | flops 393216 | bytes 1048584 | tf_op jit(solution)/shard_map/convert_element_type | solution.py:139
  88.5 1.3 %collective-permute-start.15 = (bf16[2,4,32,256]{3,2,1,0:T(8,128)(2,1)}, bf16[2,4,32,256]{3,2,1,0:T(8,128)(2,1)}, u32[]{:S(2)}, u32[]{:S(2)}) collective-permute-start(bf16[2,4,32,256]{3,2,1,0:T(8,128)(2,1)} %get-tuple-element.18), channel_id=1, source_target_pairs={{4,2},{5,3},{6,4},{7,5},{12,10},{13,11},{14,12},{15,13},{20,18},{2... | collective-permute-start | bytes 393224 | tf_op jit(solution)/shard_map/ppermute | solution.py:144
  89.9 5.0 %collective-permute-start.13 = (bf16[2,4,32,256]{3,2,1,0:T(8,128)(2,1)}, bf16[2,4,32,256]{3,2,1,0:T(8,128)(2,1)}, u32[]{:S(2)}, u32[]{:S(2)}) collective-permute-start(bf16[2,4,32,256]{3,2,1,0:T(8,128)(2,1)} %get-tuple-element.17), channel_id=1, source_target_pairs={{0,2},{1,3},{2,4},{3,5},{4,6},{5,7},{8,10},{9,11},{10,12},{11,13},... | collective-permute-start | bytes 393224 | tf_op jit(solution)/shard_map/ppermute | solution.py:143
  94.9 0.0 collective-permute-done.15
  94.9 1.6 %fusion.4 = bf16[2,4,32,256]{3,2,1,0:T(8,128)(2,1)} fusion(bf16[2,4,32,256]{3,2,1,0:T(8,128)(2,1)} %collective-permute-done.15, f32[2,4,4,32,256]{4,3,2,1,0:T(8,128)S(1)} %bitcast_add_fusion, s32[]{:T(128)S(6)} %min.50), kind=kLoop, calls=%fused_computation.15 | loop fusion | flops 196608 | bytes 524292 | tf_op jit(solution)/shard_map/convert_element_type | solution.py:140
  96.5 1.3 %collective-permute-start.16 = (bf16[2,4,32,256]{3,2,1,0:T(8,128)(2,1)}, bf16[2,4,32,256]{3,2,1,0:T(8,128)(2,1)}, u32[]{:S(2)}, u32[]{:S(2)}) collective-permute-start(bf16[2,4,32,256]{3,2,1,0:T(8,128)(2,1)} %fusion.4), channel_id=1, source_target_pairs={{2,0},{3,1},{4,2},{5,3},{6,4},{7,5},{10,8},{11,9},{12,10},{13,11},... | collective-permute-start | bytes 393224 | tf_op jit(solution)/shard_map/ppermute | solution.py:144
  97.8 7.2 %collective-permute-done.16 = bf16[2,4,32,256]{3,2,1,0:T(8,128)(2,1)} collective-permute-done((bf16[2,4,32,256]{3,2,1,0:T(8,128)(2,1)}, bf16[2,4,32,256]{3,2,1,0:T(8,128)(2,1)}, u32[]{:S(2)}, u32[]{:S(2)}) %collective-permute-start.16) | collective-permute-done | bytes 131104 | tf_op jit(solution)/shard_map/ppermute | solution.py:144
  104.9 1.0 fusion.7
  106.0 0.1 collective-permute-start.17
  106.1 1.5 %collective-permute-start.18 = (f32[2,32,256]{2,1,0:T(8,128)S(1)}, f32[2,32,256]{2,1,0:T(8,128)S(1)}, u32[]{:S(2)}, u32[]{:S(2)}) collective-permute-start(f32[2,32,256]{2,1,0:T(8,128)S(1)} %get-tuple-element.35), channel_id=1, source_target_pairs={{0,16},{8,24},{16,0},{24,8},{1,17},{9,25},{17,1},{25,9},{2,18},{10... | collective-permute-start | bytes 196616 | tf_op jit(solution)/shard_map/ppermute | solution.py:201
  107.6 2.8 %collective-permute-start.19 = (f32[2,32,256]{2,1,0:T(8,128)S(1)}, f32[2,32,256]{2,1,0:T(8,128)S(1)}, u32[]{:S(2)}, u32[]{:S(2)}) collective-permute-start(f32[2,32,256]{2,1,0:T(8,128)S(1)} %get-tuple-element.34), channel_id=1, source_target_pairs={{0,24},{8,0},{16,8},{24,16},{1,25},{9,1},{17,9},{25,17},{2,26},{10... | collective-permute-start | bytes 196616 | tf_op jit(solution)/shard_map/ppermute | solution.py:201
  110.5 0.7 collective-permute-done.17
  111.2 0.0 collective-permute-done.18
  111.2 1.2 %collective-permute-done.19 = f32[2,32,256]{2,1,0:T(8,128)S(1)} collective-permute-done((f32[2,32,256]{2,1,0:T(8,128)S(1)}, f32[2,32,256]{2,1,0:T(8,128)S(1)}, u32[]{:S(2)}, u32[]{:S(2)}) %collective-permute-start.19) | collective-permute-done | bytes 65568 | tf_op jit(solution)/shard_map/ppermute | solution.py:201
  112.4 0.1 fusion.18
  112.5 0.1 div.52
  112.6 0.2 multiply_reduce_fusion
  112.9 1.2 %fusion = bf16[64,1024]{1,0:T(8,128)(2,1)} fusion(bf16[1024,1024]{1,0:T(8,128)(2,1)S(1)} %copy-done, bf16[64,1024]{1,0:T(8,128)(2,1)S(1)} %bitcast.110, f32[64,256]{1,0:T(8,128)S(1)} %bitcast.104, f32[64,256]{1,0:T(8,128)S(1)} %bitcast.106, f32[64,256]{1,0:T(8,128)S(1)} %bitcast.108, f32[64,256]{1,0:T(8,128)S(1)} %bitcast.102, ...), kind=kOutput, calls=%fused_computation.1 | convolution fusion | flops 134938624 | bytes 2753536 | tf_op jit(solution)/shard_map/dot_general | solution.py:275
  (29 shorter events, 0.3 us)
Async XLA Ops:
  0.0 112.8 %copy-start = (bf16[1024,1024]{1,0:T(8,128)(2,1)S(1)}, bf16[1024,1024]{1,0:T(8,128)(2,1)}, u32[]{:S(2)}) copy-start(bf16[1024,1024]{1,0:T(8,128)(2,1)} %param.11) | copy-start | bytes 6291460
  3.3 24.9 %copy-start.2 = (s32[2,16]{1,0:T(2,128)S(1)}, s32[2,16]{1,0:T(2,128)}, u32[]{:S(2)}) copy-start(s32[2,16]{1,0:T(2,128)} %param.15) | copy-start | bytes 388
  3.7 5.1 %collective-permute-start.1 = (bf16[2,32,256]{2,1,0:T(8,128)(2,1)S(1)}, bf16[2,32,256]{2,1,0:T(8,128)(2,1)S(1)}, u32[]{:S(2)}, u32[]{:S(2)}) collective-permute-start(bf16[2,32,256]{2,1,0:T(8,128)(2,1)S(1)} %bitcast.115), channel_id=1, source_target_pairs={{0,16},{8,24},{16,0},{24,8},{1,17},{9,25},{17,1},{25,9},{2,18},{10... | collective-permute-start | bytes 98312 | tf_op jit(solution)/shard_map/ppermute | solution.py:158
  6.8 3.9 %collective-permute-start.2 = (bf16[2,32,256]{2,1,0:T(8,128)(2,1)S(1)}, bf16[2,32,256]{2,1,0:T(8,128)(2,1)S(1)}, u32[]{:S(2)}, u32[]{:S(2)}) collective-permute-start(bf16[2,32,256]{2,1,0:T(8,128)(2,1)S(1)} %bitcast.116), channel_id=1, source_target_pairs={{0,24},{8,0},{16,8},{24,16},{1,25},{9,1},{17,9},{25,17},{2,26},{10... | collective-permute-start | bytes 98312 | tf_op jit(solution)/shard_map/ppermute | solution.py:158
  8.2 4.8 %collective-permute-start = (bf16[2,32,256]{2,1,0:T(8,128)(2,1)S(1)}, bf16[2,32,256]{2,1,0:T(8,128)(2,1)S(1)}, u32[]{:S(2)}, u32[]{:S(2)}) collective-permute-start(bf16[2,32,256]{2,1,0:T(8,128)(2,1)S(1)} %bitcast.117), channel_id=1, source_target_pairs={{0,8},{8,16},{16,24},{24,0},{1,9},{9,17},{17,25},{25,1},{2,10},{10... | collective-permute-start | bytes 98312 | tf_op jit(solution)/shard_map/ppermute | solution.py:158
  13.1 6.9 %collective-permute-start.3 = (bf16[4,2,32,256]{3,2,1,0:T(8,128)(2,1)S(1)}, bf16[4,2,32,256]{3,2,1,0:T(8,128)(2,1)S(1)}, u32[]{:S(2)}, u32[]{:S(2)}) collective-permute-start(bf16[4,2,32,256]{3,2,1,0:T(8,128)(2,1)S(1)} %pad_maximum_fusion.3), channel_id=1, source_target_pairs={{2,0},{3,1},{4,2},{5,3},{6,4},{7,5},{10,8},{11,9},{12,10},{13,11},... | collective-permute-start | bytes 393224 | tf_op jit(solution)/shard_map/ppermute | solution.py:178
  14.4 7.1 %collective-permute-start.6 = (bf16[4,2,32,256]{3,2,1,0:T(8,128)(2,1)S(1)}, bf16[4,2,32,256]{3,2,1,0:T(8,128)(2,1)S(1)}, u32[]{:S(2)}, u32[]{:S(2)}) collective-permute-start(bf16[4,2,32,256]{3,2,1,0:T(8,128)(2,1)S(1)} %pad_maximum_fusion.3), channel_id=1, source_target_pairs={{0,2},{1,3},{2,4},{3,5},{4,6},{5,7},{8,10},{9,11},{10,12},{11,13},... | collective-permute-start | bytes 393224 | tf_op jit(solution)/shard_map/ppermute | solution.py:177
  20.0 6.8 %collective-permute-start.4 = (bf16[4,2,32,256]{3,2,1,0:T(8,128)(2,1)S(1)}, bf16[4,2,32,256]{3,2,1,0:T(8,128)(2,1)S(1)}, u32[]{:S(2)}, u32[]{:S(2)}) collective-permute-start(bf16[4,2,32,256]{3,2,1,0:T(8,128)(2,1)S(1)} %collective-permute-done.3), channel_id=1, source_target_pairs={{2,0},{3,1},{4,2},{5,3},{10,8},{11,9},{12,10},{13,11},{18,16},{19,... | collective-permute-start | bytes 393224 | tf_op jit(solution)/shard_map/ppermute | solution.py:178
  21.5 6.9 %collective-permute-start.7 = (bf16[4,2,32,256]{3,2,1,0:T(8,128)(2,1)S(1)}, bf16[4,2,32,256]{3,2,1,0:T(8,128)(2,1)S(1)}, u32[]{:S(2)}, u32[]{:S(2)}) collective-permute-start(bf16[4,2,32,256]{3,2,1,0:T(8,128)(2,1)S(1)} %collective-permute-done.6), channel_id=1, source_target_pairs={{2,4},{3,5},{4,6},{5,7},{10,12},{11,13},{12,14},{13,15},{18,20},{1... | collective-permute-start | bytes 393224 | tf_op jit(solution)/shard_map/ppermute | solution.py:177
  26.8 6.8 %collective-permute-start.5 = (bf16[4,2,32,256]{3,2,1,0:T(8,128)(2,1)S(1)}, bf16[4,2,32,256]{3,2,1,0:T(8,128)(2,1)S(1)}, u32[]{:S(2)}, u32[]{:S(2)}) collective-permute-start(bf16[4,2,32,256]{3,2,1,0:T(8,128)(2,1)S(1)} %collective-permute-done.4), channel_id=1, source_target_pairs={{2,0},{3,1},{10,8},{11,9},{18,16},{19,17},{26,24},{27,25}} | collective-permute-start | bytes 393224 | tf_op jit(solution)/shard_map/ppermute | solution.py:178
  28.3 5.4 %collective-permute-start.8 = (bf16[4,2,32,256]{3,2,1,0:T(8,128)(2,1)S(1)}, bf16[4,2,32,256]{3,2,1,0:T(8,128)(2,1)S(1)}, u32[]{:S(2)}, u32[]{:S(2)}) collective-permute-start(bf16[4,2,32,256]{3,2,1,0:T(8,128)(2,1)S(1)} %collective-permute-done.7), channel_id=1, source_target_pairs={{4,6},{5,7},{12,14},{13,15},{20,22},{21,23},{28,30},{29,31}} | collective-permute-start | bytes 393224 | tf_op jit(solution)/shard_map/ppermute | solution.py:177
  33.7 1.1 copy-start.3
  34.0 2.1 %collective-permute-start.9 = (bf16[4,4,2,32,256]{4,3,2,1,0:T(8,128)(2,1)S(1)}, bf16[4,4,2,32,256]{4,3,2,1,0:T(8,128)(2,1)}, u32[]{:S(2)}, u32[]{:S(2)}) collective-permute-start(bf16[4,4,2,32,256]{4,3,2,1,0:T(8,128)(2,1)S(1)} %get-tuple-element.26), channel_id=1, source_target_pairs={{0,1},{1,0},{2,3},{3,2},{4,5},{5,4},{6,7},{7,6},{8,9},{9,8},{10,11... | collective-permute-start | bytes 1572872 | tf_op jit(solution)/shard_map/ppermute | solution.py:188
  69.7 2.1 %collective-permute-start.10 = (bf16[2,4,4,32,256]{4,3,2,1,0:T(8,128)(2,1)S(1)}, bf16[2,4,4,32,256]{4,3,2,1,0:T(8,128)(2,1)}, u32[]{:S(2)}, u32[]{:S(2)}) collective-permute-start(bf16[2,4,4,32,256]{4,3,2,1,0:T(8,128)(2,1)S(1)} %fusion.2), channel_id=1, source_target_pairs={{0,1},{1,0},{2,3},{3,2},{4,5},{5,4},{6,7},{7,6},{8,9},{9,8},{10,11... | collective-permute-start | bytes 1572872 | tf_op jit(solution)/shard_map/ppermute | solution.py:127
  74.1 4.9 %collective-permute-start.11 = (bf16[2,4,32,256]{3,2,1,0:T(8,128)(2,1)}, bf16[2,4,32,256]{3,2,1,0:T(8,128)(2,1)S(1)}, u32[]{:S(2)}, u32[]{:S(2)}) collective-permute-start(bf16[2,4,32,256]{3,2,1,0:T(8,128)(2,1)} %get-tuple-element.19), channel_id=1, source_target_pairs={{0,2},{1,3},{8,10},{9,11},{16,18},{17,19},{24,26},{25,27}} | collective-permute-start | bytes 393224 | tf_op jit(solution)/shard_map/ppermute | solution.py:143
  75.4 9.2 %collective-permute-start.14 = (bf16[2,4,32,256]{3,2,1,0:T(8,128)(2,1)}, bf16[2,4,32,256]{3,2,1,0:T(8,128)(2,1)}, u32[]{:S(2)}, u32[]{:S(2)}) collective-permute-start(bf16[2,4,32,256]{3,2,1,0:T(8,128)(2,1)} %get-tuple-element.20), channel_id=1, source_target_pairs={{6,4},{7,5},{14,12},{15,13},{22,20},{23,21},{30,28},{31,29}} | collective-permute-start | bytes 393224 | tf_op jit(solution)/shard_map/ppermute | solution.py:144
  79.7 7.1 %collective-permute-start.12 = (bf16[2,4,32,256]{3,2,1,0:T(8,128)(2,1)}, bf16[2,4,32,256]{3,2,1,0:T(8,128)(2,1)}, u32[]{:S(2)}, u32[]{:S(2)}) collective-permute-start(bf16[2,4,32,256]{3,2,1,0:T(8,128)(2,1)} %fusion.5), channel_id=1, source_target_pairs={{0,2},{1,3},{2,4},{3,5},{8,10},{9,11},{10,12},{11,13},{16,18},{17,... | collective-permute-start | bytes 393224 | tf_op jit(solution)/shard_map/ppermute | solution.py:143
  84.6 28.2 %copy-start.1 = (bf16[2,32,1024]{2,1,0:T(8,128)(2,1)S(1)}, bf16[2,32,1024]{2,1,0:T(8,128)(2,1)}, u32[]{:S(2)}) copy-start(bf16[2,32,1024]{2,1,0:T(8,128)(2,1)} %param.9) | copy-start | bytes 393220
  88.5 6.3 %collective-permute-start.15 = (bf16[2,4,32,256]{3,2,1,0:T(8,128)(2,1)}, bf16[2,4,32,256]{3,2,1,0:T(8,128)(2,1)}, u32[]{:S(2)}, u32[]{:S(2)}) collective-permute-start(bf16[2,4,32,256]{3,2,1,0:T(8,128)(2,1)} %get-tuple-element.18), channel_id=1, source_target_pairs={{4,2},{5,3},{6,4},{7,5},{12,10},{13,11},{14,12},{15,13},{20,18},{2... | collective-permute-start | bytes 393224 | tf_op jit(solution)/shard_map/ppermute | solution.py:144
  89.9 7.9 %collective-permute-start.13 = (bf16[2,4,32,256]{3,2,1,0:T(8,128)(2,1)}, bf16[2,4,32,256]{3,2,1,0:T(8,128)(2,1)}, u32[]{:S(2)}, u32[]{:S(2)}) collective-permute-start(bf16[2,4,32,256]{3,2,1,0:T(8,128)(2,1)} %get-tuple-element.17), channel_id=1, source_target_pairs={{0,2},{1,3},{2,4},{3,5},{4,6},{5,7},{8,10},{9,11},{10,12},{11,13},... | collective-permute-start | bytes 393224 | tf_op jit(solution)/shard_map/ppermute | solution.py:143
  96.5 8.5 %collective-permute-start.16 = (bf16[2,4,32,256]{3,2,1,0:T(8,128)(2,1)}, bf16[2,4,32,256]{3,2,1,0:T(8,128)(2,1)}, u32[]{:S(2)}, u32[]{:S(2)}) collective-permute-start(bf16[2,4,32,256]{3,2,1,0:T(8,128)(2,1)} %fusion.4), channel_id=1, source_target_pairs={{2,0},{3,1},{4,2},{5,3},{6,4},{7,5},{10,8},{11,9},{12,10},{13,11},... | collective-permute-start | bytes 393224 | tf_op jit(solution)/shard_map/ppermute | solution.py:144
  106.0 5.2 %collective-permute-start.17 = (f32[2,32,256]{2,1,0:T(8,128)S(1)}, f32[2,32,256]{2,1,0:T(8,128)S(1)}, u32[]{:S(2)}, u32[]{:S(2)}) collective-permute-start(f32[2,32,256]{2,1,0:T(8,128)S(1)} %get-tuple-element.36), channel_id=1, source_target_pairs={{0,8},{8,16},{16,24},{24,0},{1,9},{9,17},{17,25},{25,1},{2,10},{10... | collective-permute-start | bytes 196616 | tf_op jit(solution)/shard_map/ppermute | solution.py:201
  106.1 5.1 %collective-permute-start.18 = (f32[2,32,256]{2,1,0:T(8,128)S(1)}, f32[2,32,256]{2,1,0:T(8,128)S(1)}, u32[]{:S(2)}, u32[]{:S(2)}) collective-permute-start(f32[2,32,256]{2,1,0:T(8,128)S(1)} %get-tuple-element.35), channel_id=1, source_target_pairs={{0,16},{8,24},{16,0},{24,8},{1,17},{9,25},{17,1},{25,9},{2,18},{10... | collective-permute-start | bytes 196616 | tf_op jit(solution)/shard_map/ppermute | solution.py:201
  107.6 4.8 %collective-permute-start.19 = (f32[2,32,256]{2,1,0:T(8,128)S(1)}, f32[2,32,256]{2,1,0:T(8,128)S(1)}, u32[]{:S(2)}, u32[]{:S(2)}) collective-permute-start(f32[2,32,256]{2,1,0:T(8,128)S(1)} %get-tuple-element.34), channel_id=1, source_target_pairs={{0,24},{8,0},{16,8},{24,16},{1,25},{9,1},{17,9},{25,17},{2,26},{10... | collective-permute-start | bytes 196616 | tf_op jit(solution)/shard_map/ppermute | solution.py:201

commit v3 on v2

--- a/solution.py
+++ b/solution.py
@@ -133,16 +133,12 @@
         index = jnp.clip(index, 0, chips - 1)
         return lax.dynamic_index_in_dim(chip_sums, index, axis=2, keepdims=False)
 
-    rightward = jnp.zeros_like(block_of(0))
-    leftward = jnp.zeros_like(rightward)
-    for step in range(1, chips):
-        send_right = (block_of(chip + chips - step) + rightward).astype(jnp.bfloat16)
-        send_left = (block_of(chip - chips + step) + leftward).astype(jnp.bfloat16)
-        to_right = [(2 * c + k, 2 * (c + 1) + k) for c in range(step) for k in range(2)]
-        to_left = [(2 * c + k, 2 * (c - 1) + k) for c in range(chips - step, chips) for k in range(2)]
-        rightward = lax.ppermute(send_right, "hist", perm=to_right).astype(jnp.float32)
-        leftward = lax.ppermute(send_left, "hist", perm=to_left).astype(jnp.float32)
-    return block_of(chip) + rightward + leftward
+    total = block_of(chip)
+    for shift in range(1, chips):
+        send = block_of((chip + shift) % chips).astype(jnp.bfloat16)
+        perm = [(2 * c + k, 2 * ((c + shift) % chips) + k) for c in range(chips) for k in range(2)]
+        total = total + lax.ppermute(send, "hist", perm=perm).astype(jnp.float32)
+    return total
 
 
 def gather_queries(queries, n_cand, n_hist):
@@ -169,19 +165,14 @@
     chips = n_hist // 2
     me = lax.axis_index("hist")
     chip, core = me // 2, me % 2
-    rightward, leftward = [], []
-    send_right = send_left = sources
-    for step in range(1, chips):
-        to_right = [(2 * c + k, 2 * (c + 1) + k) for c in range(step - 1, chips - 1) for k in range(2)]
-        to_left = [(2 * c + k, 2 * (c - 1) + k) for c in range(1, chips - step + 1) for k in range(2)]
-        send_right = lax.ppermute(send_right, "hist", perm=to_right)
-        send_left = lax.ppermute(send_left, "hist", perm=to_left)
-        rightward.append(send_right)
-        leftward.append(send_left)
-    by_distance = jnp.stack(leftward[::-1] + [sources] + rightward)
+    by_offset = [sources]
+    for shift in range(1, chips):
+        perm = [(2 * c + k, 2 * ((c + shift) % chips) + k) for c in range(chips) for k in range(2)]
+        by_offset.append(lax.ppermute(sources, "hist", perm=perm))
+    by_offset = jnp.stack(by_offset)
     mine = jnp.stack(
         [
-            lax.dynamic_index_in_dim(by_distance, chips - 1 + chip - c, axis=0, keepdims=False)
+            lax.dynamic_index_in_dim(by_offset, (chip - c) % chips, axis=0, keepdims=False)
             for c in range(chips)
         ]
     )

time: 114 us -> 90.3 us (0.79); the launches traced: 114 us -> 91.5 us
  Pallas kernels: 29.2 us -> 21.6 us
  starting transfers between devices: 34.6 us -> 28.5 us
  waiting for transfers between devices: 30.4 us -> 25.7 us
  other arithmetic: 9.91 us -> 5.96 us
    pallas_call x1, Pallas kernels: 29.2 us -> 21.6 us  [body(): pl.pallas_call(functools.partial(attend_kernel, window=window, heads_here...]
    ppermute x12 -> x6, starting transfers between devices: 24.9 us -> 18.8 us  [the longest x3 13.2 us: reduce_over_hist(): total = total + lax.ppermute(send, 'hist', perm=perm).astype(jnp.float32)]
    ppermute x12 -> x6, waiting for transfers between devices: 22.2 us -> 17.5 us  [the longest x3 11.7 us: reduce_over_hist(): total = total + lax.ppermute(send, 'hist', perm=perm).astype(jnp.float32)]
    convert_element_type x3 -> x0, other arithmetic: 4 us -> none  [the longest x2 2.42 us: reduce_over_hist(): (block_of(chip + chips - step) + rightward).astype(jnp.bfloat16)]
  transfers between devices with their start and end apart: 20 -> 14, of which waited for: 12 -> 11; matrix products, arithmetic and copies ran while one was open for 4% -> 2% of each run, Pallas kernels for 0% -> 0%
where the time goes in v3:
time: 90.3 us; the launch traced here: 91.5 us
  starting transfers between devices  28.5 us (32%)
  waiting for transfers between devices  25.7 us (28%)
  Pallas kernels  21.6 us (24%)
  other arithmetic  5.96 us (7%)
  local copies, waits for them, and re-layouts  5.07 us (6%)
  matrix products  4.46 us (5%)
    pallas_call x1, Pallas kernels, body(): pl.pallas_call(functools.partial(attend_kernel, window=window, heads_here...  21.6 us
    ppermute x3, starting transfers between devices, reduce_over_hist(): total = total + lax.ppermute(send, 'hist', perm=perm).astype(jnp.float32)  13.2 us
    ppermute x3, waiting for transfers between devices, reduce_over_hist(): total = total + lax.ppermute(send, 'hist', perm=perm).astype(jnp.float32)  11.7 us
    ppermute x3, waiting for transfers between devices, gather_queries(): by_offset.append(lax.ppermute(sources, 'hist', perm=perm))  5.73 us
    ppermute x3, starting transfers between devices, gather_queries(): by_offset.append(lax.ppermute(sources, 'hist', perm=perm))  5.57 us
    ppermute x3, starting transfers between devices, gather_queries(): lax.ppermute(piece, 'cand', perm=[(i, (i + shift) % n_cand) for i in rang...  5.06 us
    ppermute x3, starting transfers between devices, spread_over_cand(): lax.ppermute(piece, 'cand', perm=[(i, (i + shift) % n_cand) for i in rang...  4.5 us
    ppermute x3, waiting for transfers between devices, gather_queries(): lax.ppermute(piece, 'cand', perm=[(i, (i + shift) % n_cand) for i in rang...  4.21 us
  transfers between devices with their start and end apart: 14, of which 11 were waited for; matrix products, arithmetic and copies ran while one was open for 2% of the time, Pallas kernels for 0%

profile of v3, /device:TPU:0, one launch (start us, length us, event | category | flops | bytes accessed | tf_op | source)
XLA Modules:
  0.0 91.5 jit_solution(10148886024213187449)
XLA Ops:
  0.0 0.0 copy-start
  0.0 3.3 %multiply_convert_fusion = bf16[64,2048]{1,0:T(8,128)(2,1)S(1)} fusion(bf16[64,1024]{1,0:T(8,128)(2,1)} %bitcast.92, bf16[1024,2048]{1,0:T(8,128)(2,1)} %param.10), kind=kOutput, calls=%fused_computation.9 | convolution fusion | flops 269090816 | bytes 4587520 | tf_op jit(solution)/shard_map/dot_general | solution.py:217
  3.3 0.0 copy-start.2
  3.3 0.1 reshape_reshape.6
  3.4 0.3 constant_dynamic-slice_fusion.15
  3.7 3.0 %collective-permute-start.1 = (bf16[2,32,256]{2,1,0:T(8,128)(2,1)S(1)}, bf16[2,32,256]{2,1,0:T(8,128)(2,1)S(1)}, u32[]{:S(2)}, u32[]{:S(2)}) collective-permute-start(bf16[2,32,256]{2,1,0:T(8,128)(2,1)S(1)} %bitcast.101), channel_id=1, source_target_pairs={{0,16},{8,24},{16,0},{24,8},{1,17},{9,25},{17,1},{25,9},{2,18},{10... | collective-permute-start | bytes 98312 | tf_op jit(solution)/shard_map/ppermute | solution.py:154
  6.8 1.4 %collective-permute-start.2 = (bf16[2,32,256]{2,1,0:T(8,128)(2,1)S(1)}, bf16[2,32,256]{2,1,0:T(8,128)(2,1)S(1)}, u32[]{:S(2)}, u32[]{:S(2)}) collective-permute-start(bf16[2,32,256]{2,1,0:T(8,128)(2,1)S(1)} %bitcast.102), channel_id=1, source_target_pairs={{0,24},{8,0},{16,8},{24,16},{1,25},{9,1},{17,9},{25,17},{2,26},{10... | collective-permute-start | bytes 98312 | tf_op jit(solution)/shard_map/ppermute | solution.py:154
  8.2 0.6 collective-permute-start
  8.8 0.0 collective-permute-done.1
  8.8 1.9 %collective-permute-done.2 = bf16[2,32,256]{2,1,0:T(8,128)(2,1)S(1)} collective-permute-done((bf16[2,32,256]{2,1,0:T(8,128)(2,1)S(1)}, bf16[2,32,256]{2,1,0:T(8,128)(2,1)S(1)}, u32[]{:S(2)}, u32[]{:S(2)}) %collective-permute-start.2) | collective-permute-done | bytes 32800 | tf_op jit(solution)/shard_map/ppermute | solution.py:154
  10.7 2.3 %collective-permute-done = bf16[2,32,256]{2,1,0:T(8,128)(2,1)S(1)} collective-permute-done((bf16[2,32,256]{2,1,0:T(8,128)(2,1)S(1)}, bf16[2,32,256]{2,1,0:T(8,128)(2,1)S(1)}, u32[]{:S(2)}, u32[]{:S(2)}) %collective-permute-start) | collective-permute-done | bytes 32800 | tf_op jit(solution)/shard_map/ppermute | solution.py:154
  13.1 0.0 copy-start.3
  13.1 1.6 %collective-permute-start.3 = (bf16[4,2,32,256]{3,2,1,0:T(8,128)(2,1)S(1)}, bf16[4,2,32,256]{3,2,1,0:T(8,128)(2,1)S(1)}, u32[]{:S(2)}, u32[]{:S(2)}) collective-permute-start(bf16[4,2,32,256]{3,2,1,0:T(8,128)(2,1)S(1)} %get-tuple-element.37), channel_id=1, source_target_pairs={{0,2},{1,3},{2,4},{3,5},{4,6},{5,7},{6,0},{7,1},{8,10},{9,11},{10,... | collective-permute-start | bytes 393224 | tf_op jit(solution)/shard_map/ppermute | solution.py:171
  14.7 2.6 %collective-permute-start.4 = (bf16[4,2,32,256]{3,2,1,0:T(8,128)(2,1)S(1)}, bf16[4,2,32,256]{3,2,1,0:T(8,128)(2,1)S(1)}, u32[]{:S(2)}, u32[]{:S(2)}) collective-permute-start(bf16[4,2,32,256]{3,2,1,0:T(8,128)(2,1)S(1)} %get-tuple-element.37), channel_id=1, source_target_pairs={{0,4},{1,5},{2,6},{3,7},{4,0},{5,1},{6,2},{7,3},{8,12},{9,13},{10,... | collective-permute-start | bytes 393224 | tf_op jit(solution)/shard_map/ppermute | solution.py:171
  17.3 1.3 %collective-permute-start.5 = (bf16[4,2,32,256]{3,2,1,0:T(8,128)(2,1)S(1)}, bf16[4,2,32,256]{3,2,1,0:T(8,128)(2,1)S(1)}, u32[]{:S(2)}, u32[]{:S(2)}) collective-permute-start(bf16[4,2,32,256]{3,2,1,0:T(8,128)(2,1)S(1)} %get-tuple-element.37), channel_id=1, source_target_pairs={{0,6},{1,7},{2,0},{3,1},{4,2},{5,3},{6,4},{7,5},{8,14},{9,15},{10,... | collective-permute-start | bytes 393224 | tf_op jit(solution)/shard_map/ppermute | solution.py:171
  18.7 0.0 copy-done.2
  18.7 0.2 reduce_window_sum.11
  18.9 2.6 %collective-permute-done.3 = bf16[4,2,32,256]{3,2,1,0:T(8,128)(2,1)S(1)} collective-permute-done((bf16[4,2,32,256]{3,2,1,0:T(8,128)(2,1)S(1)}, bf16[4,2,32,256]{3,2,1,0:T(8,128)(2,1)S(1)}, u32[]{:S(2)}, u32[]{:S(2)}) %collective-permute-start.3) | collective-permute-done | bytes 131104 | tf_op jit(solution)/shard_map/ppermute | solution.py:171
  21.5 3.1 %collective-permute-done.4 = bf16[4,2,32,256]{3,2,1,0:T(8,128)(2,1)S(1)} collective-permute-done((bf16[4,2,32,256]{3,2,1,0:T(8,128)(2,1)S(1)}, bf16[4,2,32,256]{3,2,1,0:T(8,128)(2,1)S(1)}, u32[]{:S(2)}, u32[]{:S(2)}) %collective-permute-start.4) | collective-permute-done | bytes 131104 | tf_op jit(solution)/shard_map/ppermute | solution.py:171
  24.6 0.0 collective-permute-done.5
  24.6 0.1 pad_maximum_fusion
  24.7 0.1 fusion.15
  24.8 0.1 collective-permute-start.6
  24.9 0.1 copy.23
  25.0 0.6 reshape.61.user_ref
  25.7 0.0 copy-done.3
  25.7 1.1 %minimum_multiply_fusion = (s32[128]{0:T(128)}, s32[]{:T(128)}) fusion(s32[128]{0:T(128)S(1)} %copy-done.3), kind=kLoop, calls=%fused_computation.70 | loop fusion | flops 1663 | bytes 1028 | tf_op jit(solution)/shard_map/mul | solution.py:234
  26.8 0.1 collective-permute-done.6
  26.9 1.4 %fusion.1 = f32[4,2,4,2,32,256]{5,4,3,2,0,1:T(8,128)S(1)} fusion(bf16[4,1,4,2,32,256]{5,4,3,2,0,1:T(8,128)(2,1)} %bitcast.18, bf16[4,1,4,2,32,256]{5,4,3,2,0,1:T(8,128)(2,1)S(1)} %get-tuple-element.20, pred[]{:T(512)S(6)} %eq.29), kind=kLoop, calls=%fused_computation.3 | loop fusion | flops 2097152 | bytes 3145729 | tf_op jit(solution)/shard_map/convert_element_type | solution.py:256
  28.4 0.2 copy.28
  28.6 1.5 %copy.29 = f32[2,4,8,32,256]{4,3,2,1,0:T(8,128)} copy(f32[2,4,8,32,256]{4,3,0,1,2:T(8,128)S(1)} %bitcast.81) | data formatting | bytes 4194304 | tf_op jit(solution)/shard_map/convert_element_type | solution.py:256
  30.1 21.6 %shard_map.91 = (f32[2,1024,256]{2,1,0:T(8,128)}, f32[4096,256]{1,0:T(8,128)}, f32[4096,256]{1,0:T(8,128)}) custom-call(s32[128]{0:T(128)} %owner_ref.1, s32[128]{0:T(128)} %rank_ref.1, s32[16]{0:T(128)} %len_ref.1, s32[128]{0:T(128)} %reshape.61.user_ref, s32[1]{0:T(128)} %bitcast.4.last_ref, s32[128]{0:T(128)} %get-tuple-element.48.row_ref, ...), custom_call_target="tpu_custom_call" | custom-call | tf_op jit(solution)/shard_map/pallas_call | solution.py:242
  51.7 1.3 %fusion.2 = bf16[2,4,4,32,256]{4,3,2,1,0:T(8,128)(2,1)S(1)} fusion(f32[2,4,4,2,32,256]{5,4,3,2,1,0:T(8,128)} %bitcast.82, s32[]{:T(128)S(6)} %select_n.201), kind=kLoop, calls=%fused_computation.6 | loop fusion | bytes 1048580 | tf_op jit(solution)/shard_map/convert_element_type | solution.py:128
  53.0 0.1 collective-permute-start.7
  53.1 2.0 %collective-permute-done.7 = bf16[2,4,4,32,256]{4,3,2,1,0:T(8,128)(2,1)} collective-permute-done((bf16[2,4,4,32,256]{4,3,2,1,0:T(8,128)(2,1)S(1)}, bf16[2,4,4,32,256]{4,3,2,1,0:T(8,128)(2,1)}, u32[]{:S(2)}, u32[]{:S(2)}) %collective-permute-start.7) | collective-permute-done | bytes 524320 | tf_op jit(solution)/shard_map/ppermute | solution.py:127
  55.1 1.5 %bitcast_add_fusion = f32[2,4,4,32,256]{4,3,2,1,0:T(8,128)S(1)} fusion(bf16[2,4,4,32,256]{4,3,2,1,0:T(8,128)(2,1)} %collective-permute-done.7, f32[2,4,4,2,32,256]{5,4,3,2,1,0:T(8,128)} %bitcast.83, s32[]{:T(128)S(6)} %select_n.200), kind=kLoop, calls=%fused_computation.4 | loop fusion | flops 524288 | bytes 2621444 | tf_op jit(solution)/shard_map/add | solution.py:130
  56.6 0.0 copy-start.1
  56.6 0.8 fusion.6
  57.4 12.6 %collective-permute-start.10 = (bf16[2,4,32,256]{3,2,1,0:T(8,128)(2,1)}, bf16[2,4,32,256]{3,2,1,0:T(8,128)(2,1)}, u32[]{:S(2)}, u32[]{:S(2)}) collective-permute-start(bf16[2,4,32,256]{3,2,1,0:T(8,128)(2,1)} %get-tuple-element.18), channel_id=1, source_target_pairs={{0,6},{1,7},{2,0},{3,1},{4,2},{5,3},{6,4},{7,5},{8,14},{9,15},{10,... | collective-permute-start | bytes 393224 | tf_op jit(solution)/shard_map/ppermute | solution.py:140
  70.0 0.0 collective-permute-start.8
  70.0 0.6 collective-permute-start.9
  70.6 3.6 %collective-permute-done.10 = bf16[2,4,32,256]{3,2,1,0:T(8,128)(2,1)} collective-permute-done((bf16[2,4,32,256]{3,2,1,0:T(8,128)(2,1)}, bf16[2,4,32,256]{3,2,1,0:T(8,128)(2,1)}, u32[]{:S(2)}, u32[]{:S(2)}) %collective-permute-start.10) | collective-permute-done | bytes 131104 | tf_op jit(solution)/shard_map/ppermute | solution.py:140
  74.2 4.4 %collective-permute-done.8 = bf16[2,4,32,256]{3,2,1,0:T(8,128)(2,1)} collective-permute-done((bf16[2,4,32,256]{3,2,1,0:T(8,128)(2,1)}, bf16[2,4,32,256]{3,2,1,0:T(8,128)(2,1)}, u32[]{:S(2)}, u32[]{:S(2)}) %collective-permute-start.8) | collective-permute-done | bytes 131104 | tf_op jit(solution)/shard_map/ppermute | solution.py:140
  78.6 3.7 %collective-permute-done.9 = bf16[2,4,32,256]{3,2,1,0:T(8,128)(2,1)} collective-permute-done((bf16[2,4,32,256]{3,2,1,0:T(8,128)(2,1)}, bf16[2,4,32,256]{3,2,1,0:T(8,128)(2,1)}, u32[]{:S(2)}, u32[]{:S(2)}) %collective-permute-start.9) | collective-permute-done | bytes 131104 | tf_op jit(solution)/shard_map/ppermute | solution.py:140
  82.4 1.1 %fusion.4 = f32[2,4,32,256]{3,2,1,0:T(8,128)S(1)} fusion(bf16[2,4,32,256]{3,2,1,0:T(8,128)(2,1)} %collective-permute-done.10, bf16[2,4,32,256]{3,2,1,0:T(8,128)(2,1)} %collective-permute-done.9, bf16[2,4,32,256]{3,2,1,0:T(8,128)(2,1)} %collective-permute-done.8, f32[2,4,4,32,256]{4,3,2,1,0:T(8,128)S(1)} %bitcast_add_fusion, s32[]{:T(128)S(6)} %min.37), kind=kLoop, calls=%fused_computation.16 | loop fusion | flops 393216 | bytes 917508 | tf_op jit(solution)/shard_map/add | solution.py:140
  83.5 0.4 collective-permute-start.11
  83.9 1.3 %collective-permute-start.12 = (f32[2,32,256]{2,1,0:T(8,128)S(1)}, f32[2,32,256]{2,1,0:T(8,128)S(1)}, u32[]{:S(2)}, u32[]{:S(2)}) collective-permute-start(f32[2,32,256]{2,1,0:T(8,128)S(1)} %get-tuple-element.34), channel_id=1, source_target_pairs={{0,16},{8,24},{16,0},{24,8},{1,17},{9,25},{17,1},{25,9},{2,18},{10... | collective-permute-start | bytes 196616 | tf_op jit(solution)/shard_map/ppermute | solution.py:192
  85.1 2.8 %collective-permute-start.13 = (f32[2,32,256]{2,1,0:T(8,128)S(1)}, f32[2,32,256]{2,1,0:T(8,128)S(1)}, u32[]{:S(2)}, u32[]{:S(2)}) collective-permute-start(f32[2,32,256]{2,1,0:T(8,128)S(1)} %get-tuple-element.33), channel_id=1, source_target_pairs={{0,24},{8,0},{16,8},{24,16},{1,25},{9,1},{17,9},{25,17},{2,26},{10... | collective-permute-start | bytes 196616 | tf_op jit(solution)/shard_map/ppermute | solution.py:192
  88.0 0.9 %collective-permute-done.11 = f32[2,32,256]{2,1,0:T(8,128)S(1)} collective-permute-done((f32[2,32,256]{2,1,0:T(8,128)S(1)}, f32[2,32,256]{2,1,0:T(8,128)S(1)}, u32[]{:S(2)}, u32[]{:S(2)}) %collective-permute-start.11) | collective-permute-done | bytes 65568 | tf_op jit(solution)/shard_map/ppermute | solution.py:192
  88.9 0.0 collective-permute-done.12
  88.9 1.0 %collective-permute-done.13 = f32[2,32,256]{2,1,0:T(8,128)S(1)} collective-permute-done((f32[2,32,256]{2,1,0:T(8,128)S(1)}, f32[2,32,256]{2,1,0:T(8,128)S(1)}, u32[]{:S(2)}, u32[]{:S(2)}) %collective-permute-start.13) | collective-permute-done | bytes 65568 | tf_op jit(solution)/shard_map/ppermute | solution.py:192
  89.9 0.1 fusion.17
  90.1 0.1 div.52
  90.1 0.2 multiply_reduce_fusion
  90.3 0.0 copy-done
  90.4 0.0 copy-done.1
  90.4 1.2 %fusion = bf16[64,1024]{1,0:T(8,128)(2,1)} fusion(bf16[1024,1024]{1,0:T(8,128)(2,1)S(1)} %copy-done, bf16[64,1024]{1,0:T(8,128)(2,1)S(1)} %bitcast.93, f32[64,256]{1,0:T(8,128)S(1)} %bitcast.87, f32[64,256]{1,0:T(8,128)S(1)} %bitcast.89, f32[64,256]{1,0:T(8,128)S(1)} %bitcast.91, f32[64,256]{1,0:T(8,128)S(1)} %bitcast.85, ...), kind=kOutput, calls=%fused_computation.1 | convolution fusion | flops 134938624 | bytes 2753536 | tf_op jit(solution)/shard_map/dot_general | solution.py:266
  (15 shorter events, 0.2 us)
Async XLA Ops:
  0.0 90.3 %copy-start = (bf16[1024,1024]{1,0:T(8,128)(2,1)S(1)}, bf16[1024,1024]{1,0:T(8,128)(2,1)}, u32[]{:S(2)}) copy-start(bf16[1024,1024]{1,0:T(8,128)(2,1)} %param.11) | copy-start | bytes 6291460
  3.3 15.4 %copy-start.2 = (s32[2,16]{1,0:T(2,128)S(1)}, s32[2,16]{1,0:T(2,128)}, u32[]{:S(2)}) copy-start(s32[2,16]{1,0:T(2,128)} %param.15) | copy-start | bytes 388
  3.7 5.1 %collective-permute-start.1 = (bf16[2,32,256]{2,1,0:T(8,128)(2,1)S(1)}, bf16[2,32,256]{2,1,0:T(8,128)(2,1)S(1)}, u32[]{:S(2)}, u32[]{:S(2)}) collective-permute-start(bf16[2,32,256]{2,1,0:T(8,128)(2,1)S(1)} %bitcast.101), channel_id=1, source_target_pairs={{0,16},{8,24},{16,0},{24,8},{1,17},{9,25},{17,1},{25,9},{2,18},{10... | collective-permute-start | bytes 98312 | tf_op jit(solution)/shard_map/ppermute | solution.py:154
  6.8 3.9 %collective-permute-start.2 = (bf16[2,32,256]{2,1,0:T(8,128)(2,1)S(1)}, bf16[2,32,256]{2,1,0:T(8,128)(2,1)S(1)}, u32[]{:S(2)}, u32[]{:S(2)}) collective-permute-start(bf16[2,32,256]{2,1,0:T(8,128)(2,1)S(1)} %bitcast.102), channel_id=1, source_target_pairs={{0,24},{8,0},{16,8},{24,16},{1,25},{9,1},{17,9},{25,17},{2,26},{10... | collective-permute-start | bytes 98312 | tf_op jit(solution)/shard_map/ppermute | solution.py:154
  8.2 4.8 %collective-permute-start = (bf16[2,32,256]{2,1,0:T(8,128)(2,1)S(1)}, bf16[2,32,256]{2,1,0:T(8,128)(2,1)S(1)}, u32[]{:S(2)}, u32[]{:S(2)}) collective-permute-start(bf16[2,32,256]{2,1,0:T(8,128)(2,1)S(1)} %bitcast.103), channel_id=1, source_target_pairs={{0,8},{8,16},{16,24},{24,0},{1,9},{9,17},{17,25},{25,1},{2,10},{10... | collective-permute-start | bytes 98312 | tf_op jit(solution)/shard_map/ppermute | solution.py:154
  13.1 12.6 %copy-start.3 = (s32[128]{0:T(128)S(1)}, s32[128]{0:T(128)}, u32[]{:S(2)}) copy-start(s32[128]{0:T(128)} %owner_ref.1) | copy-start | bytes 1540
  13.1 8.3 %collective-permute-start.3 = (bf16[4,2,32,256]{3,2,1,0:T(8,128)(2,1)S(1)}, bf16[4,2,32,256]{3,2,1,0:T(8,128)(2,1)S(1)}, u32[]{:S(2)}, u32[]{:S(2)}) collective-permute-start(bf16[4,2,32,256]{3,2,1,0:T(8,128)(2,1)S(1)} %get-tuple-element.37), channel_id=1, source_target_pairs={{0,2},{1,3},{2,4},{3,5},{4,6},{5,7},{6,0},{7,1},{8,10},{9,11},{10,... | collective-permute-start | bytes 393224 | tf_op jit(solution)/shard_map/ppermute | solution.py:171
  14.7 9.9 %collective-permute-start.4 = (bf16[4,2,32,256]{3,2,1,0:T(8,128)(2,1)S(1)}, bf16[4,2,32,256]{3,2,1,0:T(8,128)(2,1)S(1)}, u32[]{:S(2)}, u32[]{:S(2)}) collective-permute-start(bf16[4,2,32,256]{3,2,1,0:T(8,128)(2,1)S(1)} %get-tuple-element.37), channel_id=1, source_target_pairs={{0,4},{1,5},{2,6},{3,7},{4,0},{5,1},{6,2},{7,3},{8,12},{9,13},{10,... | collective-permute-start | bytes 393224 | tf_op jit(solution)/shard_map/ppermute | solution.py:171
  17.3 7.3 %collective-permute-start.5 = (bf16[4,2,32,256]{3,2,1,0:T(8,128)(2,1)S(1)}, bf16[4,2,32,256]{3,2,1,0:T(8,128)(2,1)S(1)}, u32[]{:S(2)}, u32[]{:S(2)}) collective-permute-start(bf16[4,2,32,256]{3,2,1,0:T(8,128)(2,1)S(1)} %get-tuple-element.37), channel_id=1, source_target_pairs={{0,6},{1,7},{2,0},{3,1},{4,2},{5,3},{6,4},{7,5},{8,14},{9,15},{10,... | collective-permute-start | bytes 393224 | tf_op jit(solution)/shard_map/ppermute | solution.py:171
  24.8 2.1 %collective-permute-start.6 = (bf16[4,4,2,32,256]{4,3,2,1,0:T(8,128)(2,1)S(1)}, bf16[4,4,2,32,256]{4,3,2,1,0:T(8,128)(2,1)}, u32[]{:S(2)}, u32[]{:S(2)}) collective-permute-start(bf16[4,4,2,32,256]{4,3,2,1,0:T(8,128)(2,1)S(1)} %get-tuple-element.21), channel_id=1, source_target_pairs={{0,1},{1,0},{2,3},{3,2},{4,5},{5,4},{6,7},{7,6},{8,9},{9,8},{10,11... | collective-permute-start | bytes 1572872 | tf_op jit(solution)/shard_map/ppermute | solution.py:179
  53.0 2.1 %collective-permute-start.7 = (bf16[2,4,4,32,256]{4,3,2,1,0:T(8,128)(2,1)S(1)}, bf16[2,4,4,32,256]{4,3,2,1,0:T(8,128)(2,1)}, u32[]{:S(2)}, u32[]{:S(2)}) collective-permute-start(bf16[2,4,4,32,256]{4,3,2,1,0:T(8,128)(2,1)S(1)} %fusion.2), channel_id=1, source_target_pairs={{0,1},{1,0},{2,3},{3,2},{4,5},{5,4},{6,7},{7,6},{8,9},{9,8},{10,11... | collective-permute-start | bytes 1572872 | tf_op jit(solution)/shard_map/ppermute | solution.py:127
  56.6 33.7 %copy-start.1 = (bf16[2,32,1024]{2,1,0:T(8,128)(2,1)S(1)}, bf16[2,32,1024]{2,1,0:T(8,128)(2,1)}, u32[]{:S(2)}) copy-start(bf16[2,32,1024]{2,1,0:T(8,128)(2,1)} %param.9) | copy-start | bytes 393220
  57.4 16.8 %collective-permute-start.10 = (bf16[2,4,32,256]{3,2,1,0:T(8,128)(2,1)}, bf16[2,4,32,256]{3,2,1,0:T(8,128)(2,1)}, u32[]{:S(2)}, u32[]{:S(2)}) collective-permute-start(bf16[2,4,32,256]{3,2,1,0:T(8,128)(2,1)} %get-tuple-element.18), channel_id=1, source_target_pairs={{0,6},{1,7},{2,0},{3,1},{4,2},{5,3},{6,4},{7,5},{8,14},{9,15},{10,... | collective-permute-start | bytes 393224 | tf_op jit(solution)/shard_map/ppermute | solution.py:140
  70.0 8.6 %collective-permute-start.8 = (bf16[2,4,32,256]{3,2,1,0:T(8,128)(2,1)}, bf16[2,4,32,256]{3,2,1,0:T(8,128)(2,1)}, u32[]{:S(2)}, u32[]{:S(2)}) collective-permute-start(bf16[2,4,32,256]{3,2,1,0:T(8,128)(2,1)} %get-tuple-element.17), channel_id=1, source_target_pairs={{0,2},{1,3},{2,4},{3,5},{4,6},{5,7},{6,0},{7,1},{8,10},{9,11},{10,... | collective-permute-start | bytes 393224 | tf_op jit(solution)/shard_map/ppermute | solution.py:140
  70.0 12.3 %collective-permute-start.9 = (bf16[2,4,32,256]{3,2,1,0:T(8,128)(2,1)}, bf16[2,4,32,256]{3,2,1,0:T(8,128)(2,1)}, u32[]{:S(2)}, u32[]{:S(2)}) collective-permute-start(bf16[2,4,32,256]{3,2,1,0:T(8,128)(2,1)} %get-tuple-element.19), channel_id=1, source_target_pairs={{0,4},{1,5},{2,6},{3,7},{4,0},{5,1},{6,2},{7,3},{8,12},{9,13},{10,... | collective-permute-start | bytes 393224 | tf_op jit(solution)/shard_map/ppermute | solution.py:140
  83.5 5.4 %collective-permute-start.11 = (f32[2,32,256]{2,1,0:T(8,128)S(1)}, f32[2,32,256]{2,1,0:T(8,128)S(1)}, u32[]{:S(2)}, u32[]{:S(2)}) collective-permute-start(f32[2,32,256]{2,1,0:T(8,128)S(1)} %get-tuple-element.35), channel_id=1, source_target_pairs={{0,8},{8,16},{16,24},{24,0},{1,9},{9,17},{17,25},{25,1},{2,10},{10... | collective-permute-start | bytes 196616 | tf_op jit(solution)/shard_map/ppermute | solution.py:192
  83.9 5.0 %collective-permute-start.12 = (f32[2,32,256]{2,1,0:T(8,128)S(1)}, f32[2,32,256]{2,1,0:T(8,128)S(1)}, u32[]{:S(2)}, u32[]{:S(2)}) collective-permute-start(f32[2,32,256]{2,1,0:T(8,128)S(1)} %get-tuple-element.34), channel_id=1, source_target_pairs={{0,16},{8,24},{16,0},{24,8},{1,17},{9,25},{17,1},{25,9},{2,18},{10... | collective-permute-start | bytes 196616 | tf_op jit(solution)/shard_map/ppermute | solution.py:192
  85.1 4.8 %collective-permute-start.13 = (f32[2,32,256]{2,1,0:T(8,128)S(1)}, f32[2,32,256]{2,1,0:T(8,128)S(1)}, u32[]{:S(2)}, u32[]{:S(2)}) collective-permute-start(f32[2,32,256]{2,1,0:T(8,128)S(1)} %get-tuple-element.33), channel_id=1, source_target_pairs={{0,24},{8,0},{16,8},{24,16},{1,25},{9,1},{17,9},{25,17},{2,26},{10... | collective-permute-start | bytes 196616 | tf_op jit(solution)/shard_map/ppermute | solution.py:192

commit v4 on v3

--- a/solution.py
+++ b/solution.py
@@ -238,20 +238,19 @@
     tiles = pl.BlockSpec(
         (rows_per_block, head_cols), lambda b, *_: (jnp.minimum(b, _[4][0]), 0)
     )
-    per_user = pl.BlockSpec((USERS * micro * window, head_cols), lambda b, *_: (0, 0))
-    partial_value, _, _ = pl.pallas_call(
+    partial_value = pl.pallas_call(
         functools.partial(attend_kernel, window=window, heads_here=heads_here, micro=micro),
         grid_spec=pltpu.PrefetchScalarGridSpec(
             num_scalar_prefetch=6,
             grid=(n_blocks,),
             in_specs=[whole, tiles, tiles],
-            out_specs=[whole, per_user, per_user],
+            out_specs=whole,
+            scratch_shapes=[
+                pltpu.VMEM((USERS * micro * window, head_cols), jnp.float32),
+                pltpu.VMEM((USERS * micro * window, head_cols), jnp.float32),
+            ],
         ),
-        out_shape=[
-            jax.ShapeDtypeStruct((micro, all_cands, head_cols), jnp.float32),
-            jax.ShapeDtypeStruct((USERS * micro * window, head_cols), jnp.float32),
-            jax.ShapeDtypeStruct((USERS * micro * window, head_cols), jnp.float32),
-        ],
+        out_shape=jax.ShapeDtypeStruct((micro, all_cands, head_cols), jnp.float32),
         compiler_params=pltpu.CompilerParams(dimension_semantics=("arbitrary",)),
     )(tile_user, tile_rank, hist_len, user_info, last_block, first_rows, queries_all.astype(jnp.float32), k_cache, v_cache)
 

time: 90.3 us -> 87.5 us (0.969); the launches traced: 91.5 us -> 86.7 us
  Pallas kernels: 21.6 us -> 18.9 us
  starting transfers between devices: 28.5 us -> 26.7 us
    ppermute x3, starting transfers between devices: 13.2 us -> 3.51 us  [reduce_over_hist(): total = total + lax.ppermute(send, 'hist', perm=perm).astype(jnp.float32)]
    ppermute x1, starting transfers between devices: 0.07 us -> 8.03 us  [reduce_over_hist(): lax.ppermute(theirs.astype(jnp.bfloat16), 'hist', perm=[(i, i ^ 1) for i...]
    pallas_call x1, Pallas kernels: 21.6 us -> 18.9 us  [body(): pl.pallas_call(functools.partial(attend_kernel, window=window, heads_here...]
where the time goes in v4:
time: 87.5 us; the launch traced here: 86.7 us
  starting transfers between devices  26.7 us (31%)
  waiting for transfers between devices  25.4 us (29%)
  Pallas kernels  18.9 us (22%)
  other arithmetic  6.02 us (7%)
  local copies, waits for them, and re-layouts  5.06 us (6%)
  matrix products  4.46 us (5%)
    pallas_call x1, Pallas kernels, body(): pl.pallas_call(functools.partial(attend_kernel, window=window, heads_here...  18.9 us
    ppermute x3, waiting for transfers between devices, reduce_over_hist(): total = total + lax.ppermute(send, 'hist', perm=perm).astype(jnp.float32)  11.7 us
    ppermute x1, starting transfers between devices, reduce_over_hist(): lax.ppermute(theirs.astype(jnp.bfloat16), 'hist', perm=[(i, i ^ 1) for i...  8.03 us
    ppermute x3, waiting for transfers between devices, gather_queries(): by_offset.append(lax.ppermute(sources, 'hist', perm=perm))  5.73 us
    ppermute x3, starting transfers between devices, gather_queries(): by_offset.append(lax.ppermute(sources, 'hist', perm=perm))  5.57 us
    ppermute x3, starting transfers between devices, gather_queries(): lax.ppermute(piece, 'cand', perm=[(i, (i + shift) % n_cand) for i in rang...  5.06 us
    ppermute x3, starting transfers between devices, spread_over_cand(): lax.ppermute(piece, 'cand', perm=[(i, (i + shift) % n_cand) for i in rang...  4.5 us
    ppermute x3, waiting for transfers between devices, gather_queries(): lax.ppermute(piece, 'cand', perm=[(i, (i + shift) % n_cand) for i in rang...  4.21 us
  transfers between devices with their start and end apart: 14, of which 11 were waited for; matrix products, arithmetic and copies ran while one was open for 2% of the time, Pallas kernels for 0%

profile of v4, /device:TPU:0, one launch (start us, length us, event | category | flops | bytes accessed | tf_op | source)
XLA Modules:
  0.0 86.7 jit_solution(3554091773357427365)
XLA Ops:
  0.0 0.0 copy-start
  0.0 3.3 %multiply_convert_fusion = bf16[64,2048]{1,0:T(8,128)(2,1)S(1)} fusion(bf16[64,1024]{1,0:T(8,128)(2,1)} %bitcast.92, bf16[1024,2048]{1,0:T(8,128)(2,1)} %param.10), kind=kOutput, calls=%fused_computation.9 | convolution fusion | flops 269090816 | bytes 4587520 | tf_op jit(solution)/shard_map/dot_general | solution.py:217
  3.3 0.0 copy-start.2
  3.3 0.1 reshape_reshape.6
  3.4 0.3 constant_dynamic-slice_fusion.15
  3.7 3.0 %collective-permute-start.1 = (bf16[2,32,256]{2,1,0:T(8,128)(2,1)S(1)}, bf16[2,32,256]{2,1,0:T(8,128)(2,1)S(1)}, u32[]{:S(2)}, u32[]{:S(2)}) collective-permute-start(bf16[2,32,256]{2,1,0:T(8,128)(2,1)S(1)} %bitcast.101), channel_id=1, source_target_pairs={{0,16},{8,24},{16,0},{24,8},{1,17},{9,25},{17,1},{25,9},{2,18},{10... | collective-permute-start | bytes 98312 | tf_op jit(solution)/shard_map/ppermute | solution.py:154
  6.8 1.4 %collective-permute-start.2 = (bf16[2,32,256]{2,1,0:T(8,128)(2,1)S(1)}, bf16[2,32,256]{2,1,0:T(8,128)(2,1)S(1)}, u32[]{:S(2)}, u32[]{:S(2)}) collective-permute-start(bf16[2,32,256]{2,1,0:T(8,128)(2,1)S(1)} %bitcast.102), channel_id=1, source_target_pairs={{0,24},{8,0},{16,8},{24,16},{1,25},{9,1},{17,9},{25,17},{2,26},{10... | collective-permute-start | bytes 98312 | tf_op jit(solution)/shard_map/ppermute | solution.py:154
  8.2 0.6 collective-permute-start
  8.8 0.0 collective-permute-done.1
  8.8 1.9 %collective-permute-done.2 = bf16[2,32,256]{2,1,0:T(8,128)(2,1)S(1)} collective-permute-done((bf16[2,32,256]{2,1,0:T(8,128)(2,1)S(1)}, bf16[2,32,256]{2,1,0:T(8,128)(2,1)S(1)}, u32[]{:S(2)}, u32[]{:S(2)}) %collective-permute-start.2) | collective-permute-done | bytes 32800 | tf_op jit(solution)/shard_map/ppermute | solution.py:154
  10.7 2.3 %collective-permute-done = bf16[2,32,256]{2,1,0:T(8,128)(2,1)S(1)} collective-permute-done((bf16[2,32,256]{2,1,0:T(8,128)(2,1)S(1)}, bf16[2,32,256]{2,1,0:T(8,128)(2,1)S(1)}, u32[]{:S(2)}, u32[]{:S(2)}) %collective-permute-start) | collective-permute-done | bytes 32800 | tf_op jit(solution)/shard_map/ppermute | solution.py:154
  13.1 0.0 copy-start.3
  13.1 1.6 %collective-permute-start.3 = (bf16[4,2,32,256]{3,2,1,0:T(8,128)(2,1)S(1)}, bf16[4,2,32,256]{3,2,1,0:T(8,128)(2,1)S(1)}, u32[]{:S(2)}, u32[]{:S(2)}) collective-permute-start(bf16[4,2,32,256]{3,2,1,0:T(8,128)(2,1)S(1)} %get-tuple-element.35), channel_id=1, source_target_pairs={{0,2},{1,3},{2,4},{3,5},{4,6},{5,7},{6,0},{7,1},{8,10},{9,11},{10,... | collective-permute-start | bytes 393224 | tf_op jit(solution)/shard_map/ppermute | solution.py:171
  14.7 2.6 %collective-permute-start.4 = (bf16[4,2,32,256]{3,2,1,0:T(8,128)(2,1)S(1)}, bf16[4,2,32,256]{3,2,1,0:T(8,128)(2,1)S(1)}, u32[]{:S(2)}, u32[]{:S(2)}) collective-permute-start(bf16[4,2,32,256]{3,2,1,0:T(8,128)(2,1)S(1)} %get-tuple-element.35), channel_id=1, source_target_pairs={{0,4},{1,5},{2,6},{3,7},{4,0},{5,1},{6,2},{7,3},{8,12},{9,13},{10,... | collective-permute-start | bytes 393224 | tf_op jit(solution)/shard_map/ppermute | solution.py:171
  17.3 1.3 %collective-permute-start.5 = (bf16[4,2,32,256]{3,2,1,0:T(8,128)(2,1)S(1)}, bf16[4,2,32,256]{3,2,1,0:T(8,128)(2,1)S(1)}, u32[]{:S(2)}, u32[]{:S(2)}) collective-permute-start(bf16[4,2,32,256]{3,2,1,0:T(8,128)(2,1)S(1)} %get-tuple-element.35), channel_id=1, source_target_pairs={{0,6},{1,7},{2,0},{3,1},{4,2},{5,3},{6,4},{7,5},{8,14},{9,15},{10,... | collective-permute-start | bytes 393224 | tf_op jit(solution)/shard_map/ppermute | solution.py:171
  18.7 0.0 copy-done.2
  18.7 0.2 reduce_window_sum.11
  18.9 2.6 %collective-permute-done.3 = bf16[4,2,32,256]{3,2,1,0:T(8,128)(2,1)S(1)} collective-permute-done((bf16[4,2,32,256]{3,2,1,0:T(8,128)(2,1)S(1)}, bf16[4,2,32,256]{3,2,1,0:T(8,128)(2,1)S(1)}, u32[]{:S(2)}, u32[]{:S(2)}) %collective-permute-start.3) | collective-permute-done | bytes 131104 | tf_op jit(solution)/shard_map/ppermute | solution.py:171
  21.5 3.1 %collective-permute-done.4 = bf16[4,2,32,256]{3,2,1,0:T(8,128)(2,1)S(1)} collective-permute-done((bf16[4,2,32,256]{3,2,1,0:T(8,128)(2,1)S(1)}, bf16[4,2,32,256]{3,2,1,0:T(8,128)(2,1)S(1)}, u32[]{:S(2)}, u32[]{:S(2)}) %collective-permute-start.4) | collective-permute-done | bytes 131104 | tf_op jit(solution)/shard_map/ppermute | solution.py:171
  24.6 0.0 collective-permute-done.5
  24.6 0.1 pad_maximum_fusion
  24.7 0.1 fusion.15
  24.8 0.1 collective-permute-start.6
  24.9 0.1 copy.23
  25.0 0.6 reshape.61.user_ref
  25.7 0.0 copy-done.3
  25.7 1.2 %minimum_multiply_fusion = (s32[128]{0:T(128)}, s32[]{:T(128)}) fusion(s32[128]{0:T(128)S(1)} %copy-done.3), kind=kLoop, calls=%fused_computation.70 | loop fusion | flops 1663 | bytes 1028 | tf_op jit(solution)/shard_map/mul | solution.py:234
  26.8 0.1 collective-permute-done.6
  26.9 1.4 %fusion.1 = f32[4,2,4,2,32,256]{5,4,3,2,0,1:T(8,128)S(1)} fusion(bf16[4,1,4,2,32,256]{5,4,3,2,0,1:T(8,128)(2,1)} %bitcast.18, bf16[4,1,4,2,32,256]{5,4,3,2,0,1:T(8,128)(2,1)S(1)} %get-tuple-element.18, pred[]{:T(512)S(6)} %eq.29), kind=kLoop, calls=%fused_computation.3 | loop fusion | flops 2097152 | bytes 3145729 | tf_op jit(solution)/shard_map/convert_element_type | solution.py:255
  28.4 0.2 copy.28
  28.6 1.5 %copy.29 = f32[2,4,8,32,256]{4,3,2,1,0:T(8,128)} copy(f32[2,4,8,32,256]{4,3,0,1,2:T(8,128)S(1)} %bitcast.80) | data formatting | bytes 4194304 | tf_op jit(solution)/shard_map/convert_element_type | solution.py:255
  30.1 18.9 %shard_map.91 = f32[2,1024,256]{2,1,0:T(8,128)} custom-call(s32[128]{0:T(128)} %owner_ref.1, s32[128]{0:T(128)} %rank_ref.1, s32[16]{0:T(128)} %len_ref.1, s32[128]{0:T(128)} %reshape.61.user_ref, s32[1]{0:T(128)} %bitcast.4.last_ref, s32[128]{0:T(128)} %get-tuple-element.46.row_ref, f32[2,1024,256]{2,1,0:T(8,128)} %bitcast.81, bf16[16384,256]{1,0:T(8,128)(2,1)} %k_ref.1, ...), custom_call_target="tpu_custom_call" | custom-call | tf_op jit(solution)/shard_map/pallas_call | solution.py:241
  48.9 1.3 %fusion.2 = bf16[2,4,4,32,256]{4,3,2,1,0:T(8,128)(2,1)S(1)} fusion(f32[2,4,4,2,32,256]{5,4,3,2,1,0:T(8,128)} %bitcast.82, s32[]{:T(128)S(6)} %select_n.201), kind=kLoop, calls=%fused_computation.6 | loop fusion | bytes 1048580 | tf_op jit(solution)/shard_map/convert_element_type | solution.py:128
  50.2 8.0 %collective-permute-start.7 = (bf16[2,4,4,32,256]{4,3,2,1,0:T(8,128)(2,1)S(1)}, bf16[2,4,4,32,256]{4,3,2,1,0:T(8,128)(2,1)}, u32[]{:S(2)}, u32[]{:S(2)}) collective-permute-start(bf16[2,4,4,32,256]{4,3,2,1,0:T(8,128)(2,1)S(1)} %fusion.2), channel_id=1, source_target_pairs={{0,1},{1,0},{2,3},{3,2},{4,5},{5,4},{6,7},{7,6},{8,9},{9,8},{10,11... | collective-permute-start | bytes 1572872 | tf_op jit(solution)/shard_map/ppermute | solution.py:127
  58.3 1.7 %collective-permute-done.7 = bf16[2,4,4,32,256]{4,3,2,1,0:T(8,128)(2,1)} collective-permute-done((bf16[2,4,4,32,256]{4,3,2,1,0:T(8,128)(2,1)S(1)}, bf16[2,4,4,32,256]{4,3,2,1,0:T(8,128)(2,1)}, u32[]{:S(2)}, u32[]{:S(2)}) %collective-permute-start.7) | collective-permute-done | bytes 524320 | tf_op jit(solution)/shard_map/ppermute | solution.py:127
  59.9 1.5 %bitcast_add_fusion = f32[2,4,4,32,256]{4,3,2,1,0:T(8,128)S(1)} fusion(bf16[2,4,4,32,256]{4,3,2,1,0:T(8,128)(2,1)} %collective-permute-done.7, f32[2,4,4,2,32,256]{5,4,3,2,1,0:T(8,128)} %bitcast.83, s32[]{:T(128)S(6)} %select_n.200), kind=kLoop, calls=%fused_computation.4 | loop fusion | flops 524288 | bytes 2621444 | tf_op jit(solution)/shard_map/add | solution.py:130
  61.5 0.0 copy-start.1
  61.5 0.8 fusion.6
  62.3 2.9 %collective-permute-start.10 = (bf16[2,4,32,256]{3,2,1,0:T(8,128)(2,1)}, bf16[2,4,32,256]{3,2,1,0:T(8,128)(2,1)}, u32[]{:S(2)}, u32[]{:S(2)}) collective-permute-start(bf16[2,4,32,256]{3,2,1,0:T(8,128)(2,1)} %get-tuple-element.16), channel_id=1, source_target_pairs={{0,6},{1,7},{2,0},{3,1},{4,2},{5,3},{6,4},{7,5},{8,14},{9,15},{10,... | collective-permute-start | bytes 393224 | tf_op jit(solution)/shard_map/ppermute | solution.py:140
  65.2 0.0 collective-permute-start.8
  65.2 0.6 collective-permute-start.9
  65.8 3.6 %collective-permute-done.10 = bf16[2,4,32,256]{3,2,1,0:T(8,128)(2,1)} collective-permute-done((bf16[2,4,32,256]{3,2,1,0:T(8,128)(2,1)}, bf16[2,4,32,256]{3,2,1,0:T(8,128)(2,1)}, u32[]{:S(2)}, u32[]{:S(2)}) %collective-permute-start.10) | collective-permute-done | bytes 131104 | tf_op jit(solution)/shard_map/ppermute | solution.py:140
  69.4 4.4 %collective-permute-done.8 = bf16[2,4,32,256]{3,2,1,0:T(8,128)(2,1)} collective-permute-done((bf16[2,4,32,256]{3,2,1,0:T(8,128)(2,1)}, bf16[2,4,32,256]{3,2,1,0:T(8,128)(2,1)}, u32[]{:S(2)}, u32[]{:S(2)}) %collective-permute-start.8) | collective-permute-done | bytes 131104 | tf_op jit(solution)/shard_map/ppermute | solution.py:140
  73.8 3.7 %collective-permute-done.9 = bf16[2,4,32,256]{3,2,1,0:T(8,128)(2,1)} collective-permute-done((bf16[2,4,32,256]{3,2,1,0:T(8,128)(2,1)}, bf16[2,4,32,256]{3,2,1,0:T(8,128)(2,1)}, u32[]{:S(2)}, u32[]{:S(2)}) %collective-permute-start.9) | collective-permute-done | bytes 131104 | tf_op jit(solution)/shard_map/ppermute | solution.py:140
  77.5 1.1 %fusion.4 = f32[2,4,32,256]{3,2,1,0:T(8,128)S(1)} fusion(bf16[2,4,32,256]{3,2,1,0:T(8,128)(2,1)} %collective-permute-done.10, bf16[2,4,32,256]{3,2,1,0:T(8,128)(2,1)} %collective-permute-done.9, bf16[2,4,32,256]{3,2,1,0:T(8,128)(2,1)} %collective-permute-done.8, f32[2,4,4,32,256]{4,3,2,1,0:T(8,128)S(1)} %bitcast_add_fusion, s32[]{:T(128)S(6)} %min.37), kind=kLoop, calls=%fused_computation.16 | loop fusion | flops 393216 | bytes 917508 | tf_op jit(solution)/shard_map/add | solution.py:140
  78.7 0.4 collective-permute-start.11
  79.0 1.3 %collective-permute-start.12 = (f32[2,32,256]{2,1,0:T(8,128)S(1)}, f32[2,32,256]{2,1,0:T(8,128)S(1)}, u32[]{:S(2)}, u32[]{:S(2)}) collective-permute-start(f32[2,32,256]{2,1,0:T(8,128)S(1)} %get-tuple-element.32), channel_id=1, source_target_pairs={{0,16},{8,24},{16,0},{24,8},{1,17},{9,25},{17,1},{25,9},{2,18},{10... | collective-permute-start | bytes 196616 | tf_op jit(solution)/shard_map/ppermute | solution.py:192
  80.3 2.8 %collective-permute-start.13 = (f32[2,32,256]{2,1,0:T(8,128)S(1)}, f32[2,32,256]{2,1,0:T(8,128)S(1)}, u32[]{:S(2)}, u32[]{:S(2)}) collective-permute-start(f32[2,32,256]{2,1,0:T(8,128)S(1)} %get-tuple-element.31), channel_id=1, source_target_pairs={{0,24},{8,0},{16,8},{24,16},{1,25},{9,1},{17,9},{25,17},{2,26},{10... | collective-permute-start | bytes 196616 | tf_op jit(solution)/shard_map/ppermute | solution.py:192
  83.1 0.9 %collective-permute-done.11 = f32[2,32,256]{2,1,0:T(8,128)S(1)} collective-permute-done((f32[2,32,256]{2,1,0:T(8,128)S(1)}, f32[2,32,256]{2,1,0:T(8,128)S(1)}, u32[]{:S(2)}, u32[]{:S(2)}) %collective-permute-start.11) | collective-permute-done | bytes 65568 | tf_op jit(solution)/shard_map/ppermute | solution.py:192
  84.1 0.0 collective-permute-done.12
  84.1 1.0 %collective-permute-done.13 = f32[2,32,256]{2,1,0:T(8,128)S(1)} collective-permute-done((f32[2,32,256]{2,1,0:T(8,128)S(1)}, f32[2,32,256]{2,1,0:T(8,128)S(1)}, u32[]{:S(2)}, u32[]{:S(2)}) %collective-permute-start.13) | collective-permute-done | bytes 65568 | tf_op jit(solution)/shard_map/ppermute | solution.py:192
  85.1 0.1 fusion.17
  85.2 0.1 div.52
  85.3 0.2 multiply_reduce_fusion
  85.5 0.0 copy-done
  85.5 0.0 copy-done.1
  85.5 1.2 %fusion = bf16[64,1024]{1,0:T(8,128)(2,1)} fusion(bf16[1024,1024]{1,0:T(8,128)(2,1)S(1)} %copy-done, bf16[64,1024]{1,0:T(8,128)(2,1)S(1)} %bitcast.93, f32[64,256]{1,0:T(8,128)S(1)} %bitcast.87, f32[64,256]{1,0:T(8,128)S(1)} %bitcast.89, f32[64,256]{1,0:T(8,128)S(1)} %bitcast.91, f32[64,256]{1,0:T(8,128)S(1)} %bitcast.85, ...), kind=kOutput, calls=%fused_computation.1 | convolution fusion | flops 134938624 | bytes 2753536 | tf_op jit(solution)/shard_map/dot_general | solution.py:265
  (15 shorter events, 0.2 us)
Async XLA Ops:
  0.0 85.5 %copy-start = (bf16[1024,1024]{1,0:T(8,128)(2,1)S(1)}, bf16[1024,1024]{1,0:T(8,128)(2,1)}, u32[]{:S(2)}) copy-start(bf16[1024,1024]{1,0:T(8,128)(2,1)} %param.11) | copy-start | bytes 6291460
  3.3 15.4 %copy-start.2 = (s32[2,16]{1,0:T(2,128)S(1)}, s32[2,16]{1,0:T(2,128)}, u32[]{:S(2)}) copy-start(s32[2,16]{1,0:T(2,128)} %param.15) | copy-start | bytes 388
  3.7 5.1 %collective-permute-start.1 = (bf16[2,32,256]{2,1,0:T(8,128)(2,1)S(1)}, bf16[2,32,256]{2,1,0:T(8,128)(2,1)S(1)}, u32[]{:S(2)}, u32[]{:S(2)}) collective-permute-start(bf16[2,32,256]{2,1,0:T(8,128)(2,1)S(1)} %bitcast.101), channel_id=1, source_target_pairs={{0,16},{8,24},{16,0},{24,8},{1,17},{9,25},{17,1},{25,9},{2,18},{10... | collective-permute-start | bytes 98312 | tf_op jit(solution)/shard_map/ppermute | solution.py:154
  6.8 3.9 %collective-permute-start.2 = (bf16[2,32,256]{2,1,0:T(8,128)(2,1)S(1)}, bf16[2,32,256]{2,1,0:T(8,128)(2,1)S(1)}, u32[]{:S(2)}, u32[]{:S(2)}) collective-permute-start(bf16[2,32,256]{2,1,0:T(8,128)(2,1)S(1)} %bitcast.102), channel_id=1, source_target_pairs={{0,24},{8,0},{16,8},{24,16},{1,25},{9,1},{17,9},{25,17},{2,26},{10... | collective-permute-start | bytes 98312 | tf_op jit(solution)/shard_map/ppermute | solution.py:154
  8.2 4.8 %collective-permute-start = (bf16[2,32,256]{2,1,0:T(8,128)(2,1)S(1)}, bf16[2,32,256]{2,1,0:T(8,128)(2,1)S(1)}, u32[]{:S(2)}, u32[]{:S(2)}) collective-permute-start(bf16[2,32,256]{2,1,0:T(8,128)(2,1)S(1)} %bitcast.103), channel_id=1, source_target_pairs={{0,8},{8,16},{16,24},{24,0},{1,9},{9,17},{17,25},{25,1},{2,10},{10... | collective-permute-start | bytes 98312 | tf_op jit(solution)/shard_map/ppermute | solution.py:154
  13.1 12.6 %copy-start.3 = (s32[128]{0:T(128)S(1)}, s32[128]{0:T(128)}, u32[]{:S(2)}) copy-start(s32[128]{0:T(128)} %owner_ref.1) | copy-start | bytes 1540
  13.1 8.3 %collective-permute-start.3 = (bf16[4,2,32,256]{3,2,1,0:T(8,128)(2,1)S(1)}, bf16[4,2,32,256]{3,2,1,0:T(8,128)(2,1)S(1)}, u32[]{:S(2)}, u32[]{:S(2)}) collective-permute-start(bf16[4,2,32,256]{3,2,1,0:T(8,128)(2,1)S(1)} %get-tuple-element.35), channel_id=1, source_target_pairs={{0,2},{1,3},{2,4},{3,5},{4,6},{5,7},{6,0},{7,1},{8,10},{9,11},{10,... | collective-permute-start | bytes 393224 | tf_op jit(solution)/shard_map/ppermute | solution.py:171
  14.7 9.9 %collective-permute-start.4 = (bf16[4,2,32,256]{3,2,1,0:T(8,128)(2,1)S(1)}, bf16[4,2,32,256]{3,2,1,0:T(8,128)(2,1)S(1)}, u32[]{:S(2)}, u32[]{:S(2)}) collective-permute-start(bf16[4,2,32,256]{3,2,1,0:T(8,128)(2,1)S(1)} %get-tuple-element.35), channel_id=1, source_target_pairs={{0,4},{1,5},{2,6},{3,7},{4,0},{5,1},{6,2},{7,3},{8,12},{9,13},{10,... | collective-permute-start | bytes 393224 | tf_op jit(solution)/shard_map/ppermute | solution.py:171
  17.3 7.3 %collective-permute-start.5 = (bf16[4,2,32,256]{3,2,1,0:T(8,128)(2,1)S(1)}, bf16[4,2,32,256]{3,2,1,0:T(8,128)(2,1)S(1)}, u32[]{:S(2)}, u32[]{:S(2)}) collective-permute-start(bf16[4,2,32,256]{3,2,1,0:T(8,128)(2,1)S(1)} %get-tuple-element.35), channel_id=1, source_target_pairs={{0,6},{1,7},{2,0},{3,1},{4,2},{5,3},{6,4},{7,5},{8,14},{9,15},{10,... | collective-permute-start | bytes 393224 | tf_op jit(solution)/shard_map/ppermute | solution.py:171
  24.8 2.1 %collective-permute-start.6 = (bf16[4,4,2,32,256]{4,3,2,1,0:T(8,128)(2,1)S(1)}, bf16[4,4,2,32,256]{4,3,2,1,0:T(8,128)(2,1)}, u32[]{:S(2)}, u32[]{:S(2)}) collective-permute-start(bf16[4,4,2,32,256]{4,3,2,1,0:T(8,128)(2,1)S(1)} %get-tuple-element.19), channel_id=1, source_target_pairs={{0,1},{1,0},{2,3},{3,2},{4,5},{5,4},{6,7},{7,6},{8,9},{9,8},{10,11... | collective-permute-start | bytes 1572872 | tf_op jit(solution)/shard_map/ppermute | solution.py:179
  50.2 9.7 %collective-permute-start.7 = (bf16[2,4,4,32,256]{4,3,2,1,0:T(8,128)(2,1)S(1)}, bf16[2,4,4,32,256]{4,3,2,1,0:T(8,128)(2,1)}, u32[]{:S(2)}, u32[]{:S(2)}) collective-permute-start(bf16[2,4,4,32,256]{4,3,2,1,0:T(8,128)(2,1)S(1)} %fusion.2), channel_id=1, source_target_pairs={{0,1},{1,0},{2,3},{3,2},{4,5},{5,4},{6,7},{7,6},{8,9},{9,8},{10,11... | collective-permute-start | bytes 1572872 | tf_op jit(solution)/shard_map/ppermute | solution.py:127
  61.5 24.0 %copy-start.1 = (bf16[2,32,1024]{2,1,0:T(8,128)(2,1)S(1)}, bf16[2,32,1024]{2,1,0:T(8,128)(2,1)}, u32[]{:S(2)}) copy-start(bf16[2,32,1024]{2,1,0:T(8,128)(2,1)} %param.9) | copy-start | bytes 393220
  62.3 7.1 %collective-permute-start.10 = (bf16[2,4,32,256]{3,2,1,0:T(8,128)(2,1)}, bf16[2,4,32,256]{3,2,1,0:T(8,128)(2,1)}, u32[]{:S(2)}, u32[]{:S(2)}) collective-permute-start(bf16[2,4,32,256]{3,2,1,0:T(8,128)(2,1)} %get-tuple-element.16), channel_id=1, source_target_pairs={{0,6},{1,7},{2,0},{3,1},{4,2},{5,3},{6,4},{7,5},{8,14},{9,15},{10,... | collective-permute-start | bytes 393224 | tf_op jit(solution)/shard_map/ppermute | solution.py:140
  65.2 8.6 %collective-permute-start.8 = (bf16[2,4,32,256]{3,2,1,0:T(8,128)(2,1)}, bf16[2,4,32,256]{3,2,1,0:T(8,128)(2,1)}, u32[]{:S(2)}, u32[]{:S(2)}) collective-permute-start(bf16[2,4,32,256]{3,2,1,0:T(8,128)(2,1)} %get-tuple-element.15), channel_id=1, source_target_pairs={{0,2},{1,3},{2,4},{3,5},{4,6},{5,7},{6,0},{7,1},{8,10},{9,11},{10,... | collective-permute-start | bytes 393224 | tf_op jit(solution)/shard_map/ppermute | solution.py:140
  65.2 12.3 %collective-permute-start.9 = (bf16[2,4,32,256]{3,2,1,0:T(8,128)(2,1)}, bf16[2,4,32,256]{3,2,1,0:T(8,128)(2,1)}, u32[]{:S(2)}, u32[]{:S(2)}) collective-permute-start(bf16[2,4,32,256]{3,2,1,0:T(8,128)(2,1)} %get-tuple-element.17), channel_id=1, source_target_pairs={{0,4},{1,5},{2,6},{3,7},{4,0},{5,1},{6,2},{7,3},{8,12},{9,13},{10,... | collective-permute-start | bytes 393224 | tf_op jit(solution)/shard_map/ppermute | solution.py:140
  78.7 5.4 %collective-permute-start.11 = (f32[2,32,256]{2,1,0:T(8,128)S(1)}, f32[2,32,256]{2,1,0:T(8,128)S(1)}, u32[]{:S(2)}, u32[]{:S(2)}) collective-permute-start(f32[2,32,256]{2,1,0:T(8,128)S(1)} %get-tuple-element.33), channel_id=1, source_target_pairs={{0,8},{8,16},{16,24},{24,0},{1,9},{9,17},{17,25},{25,1},{2,10},{10... | collective-permute-start | bytes 196616 | tf_op jit(solution)/shard_map/ppermute | solution.py:192
  79.0 5.0 %collective-permute-start.12 = (f32[2,32,256]{2,1,0:T(8,128)S(1)}, f32[2,32,256]{2,1,0:T(8,128)S(1)}, u32[]{:S(2)}, u32[]{:S(2)}) collective-permute-start(f32[2,32,256]{2,1,0:T(8,128)S(1)} %get-tuple-element.32), channel_id=1, source_target_pairs={{0,16},{8,24},{16,0},{24,8},{1,17},{9,25},{17,1},{25,9},{2,18},{10... | collective-permute-start | bytes 196616 | tf_op jit(solution)/shard_map/ppermute | solution.py:192
  80.3 4.8 %collective-permute-start.13 = (f32[2,32,256]{2,1,0:T(8,128)S(1)}, f32[2,32,256]{2,1,0:T(8,128)S(1)}, u32[]{:S(2)}, u32[]{:S(2)}) collective-permute-start(f32[2,32,256]{2,1,0:T(8,128)S(1)} %get-tuple-element.31), channel_id=1, source_target_pairs={{0,24},{8,0},{16,8},{24,16},{1,25},{9,1},{17,9},{25,17},{2,26},{10... | collective-permute-start | bytes 196616 | tf_op jit(solution)/shard_map/ppermute | solution.py:192

commit v5 on v4

--- a/solution.py
+++ b/solution.py
@@ -11,7 +11,7 @@
 TILE = 128
 USERS = 16
 MICRO = 2
-BLOCK_TILES = 8
+BLOCK_TILES = 16
 
 
 EPSILON = 1e-06
@@ -214,9 +214,13 @@
     tiles_here = k_cache.shape[0] // TILE
 
     cand_rows = cand_x.reshape(micro * local_rows, model_width)
-    projected = jax.nn.silu(jnp.dot(cand_rows, qu_weight, preferred_element_type=jnp.float32))
-    queries = projected[:, :model_width].astype(jnp.bfloat16).reshape(micro, local_rows, model_width)
-    gate_vals = projected[:, model_width:].astype(jnp.bfloat16)
+    queries = jax.nn.silu(
+        jnp.dot(cand_rows, qu_weight[:, :model_width], preferred_element_type=jnp.float32)
+    )
+    queries = queries.astype(jnp.bfloat16).reshape(micro, local_rows, model_width)
+    gate_vals = jax.nn.silu(
+        jnp.dot(cand_rows, qu_weight[:, model_width:], preferred_element_type=jnp.float32)
+    ).astype(jnp.bfloat16)
     queries_all = gather_queries(queries, n_cand, n_hist)
     all_cands = queries_all.shape[1]
     window = 2 * all_cands // USERS

time: 87.5 us -> 83.7 us (0.957); the launches traced: 86.7 us -> 85.1 us
  Pallas kernels: 18.9 us -> 15.1 us
  starting transfers between devices: 26.7 us -> 28.3 us
  other arithmetic: 6.02 us -> 4.97 us
  matrix products: 4.46 us -> 5.46 us
    ppermute x3, starting transfers between devices: 3.51 us -> 12.7 us  [reduce_over_hist(): total = total + lax.ppermute(send, 'hist', perm=perm).astype(jnp.float32)]
    ppermute x1, starting transfers between devices: 8.03 us -> 0.46 us  [reduce_over_hist(): lax.ppermute(theirs.astype(jnp.bfloat16), 'hist', perm=[(i, i ^ 1) for i...]
    pallas_call x1, Pallas kernels: 18.9 us -> 15.1 us  [body(): pl.pallas_call(functools.partial(attend_kernel, window=window, heads_here...]
    dot_general x1, matrix products: 1.19 us -> 3.14 us  [body(): jnp.dot(mixed_rows, out_weight, preferred_element_type=jnp.float32)]
    add x1, other arithmetic: 1.09 us -> 0.06 us  [reduce_over_hist(): total = total + lax.ppermute(send, 'hist', perm=perm).astype(jnp.float32)]
    dot_general x1, matrix products: 3.27 us -> 2.31 us  [body(): jnp.dot(cand_rows, qu_weight[:, :model_width], preferred_element_type=jnp...]
where the time goes in v5:
time: 83.7 us; the launch traced here: 85.1 us
  starting transfers between devices  28.3 us (34%)
  waiting for transfers between devices  26 us (31%)
  Pallas kernels  15.1 us (18%)
  matrix products  5.46 us (7%)
  local copies, waits for them, and re-layouts  5.04 us (6%)
  other arithmetic  4.97 us (6%)
    pallas_call x1, Pallas kernels, body(): pl.pallas_call(functools.partial(attend_kernel, window=window, heads_here...  15.1 us
    ppermute x3, starting transfers between devices, reduce_over_hist(): total = total + lax.ppermute(send, 'hist', perm=perm).astype(jnp.float32)  12.7 us
    ppermute x3, waiting for transfers between devices, reduce_over_hist(): total = total + lax.ppermute(send, 'hist', perm=perm).astype(jnp.float32)  12.4 us
    ppermute x3, waiting for transfers between devices, gather_queries(): by_offset.append(lax.ppermute(sources, 'hist', perm=perm))  5.73 us
    ppermute x3, starting transfers between devices, gather_queries(): by_offset.append(lax.ppermute(sources, 'hist', perm=perm))  5.57 us
    ppermute x3, starting transfers between devices, gather_queries(): lax.ppermute(piece, 'cand', perm=[(i, (i + shift) % n_cand) for i in rang...  5.06 us
    ppermute x3, starting transfers between devices, spread_over_cand(): lax.ppermute(piece, 'cand', perm=[(i, (i + shift) % n_cand) for i in rang...  4.5 us
    ppermute x3, waiting for transfers between devices, gather_queries(): lax.ppermute(piece, 'cand', perm=[(i, (i + shift) % n_cand) for i in rang...  4.21 us
  transfers between devices with their start and end apart: 14, of which 11 were waited for; matrix products, arithmetic and copies ran while one was open for 2% of the time, Pallas kernels for 0%

profile of v5, /device:TPU:0, one launch (start us, length us, event | category | flops | bytes accessed | tf_op | source)
XLA Modules:
  0.0 85.1 jit_solution(9356464486345059645)
XLA Ops:
  0.0 0.0 copy-start
  0.0 2.3 %multiply_convert_fusion.2 = bf16[64,1024]{1,0:T(8,128)(2,1)S(1)} fusion(bf16[64,1024]{1,0:T(8,128)(2,1)} %bitcast.106, bf16[1024,2048]{1,0:T(8,128)(2,1)} %param.10), kind=kOutput, calls=%fused_computation.25 | convolution fusion | flops 134545408 | bytes 2359296 | tf_op jit(solution)/shard_map/dot_general | solution.py:218
  2.3 0.0 copy-start.1
  2.3 0.1 reshape_reshape.6
  2.4 0.3 constant_dynamic-slice_fusion.15
  2.7 3.0 %collective-permute-start.1 = (bf16[2,32,256]{2,1,0:T(8,128)(2,1)S(1)}, bf16[2,32,256]{2,1,0:T(8,128)(2,1)S(1)}, u32[]{:S(2)}, u32[]{:S(2)}) collective-permute-start(bf16[2,32,256]{2,1,0:T(8,128)(2,1)S(1)} %bitcast.99), channel_id=1, source_target_pairs={{0,16},{8,24},{16,0},{24,8},{1,17},{9,25},{17,1},{25,9},{2,18},{10... | collective-permute-start | bytes 98312 | tf_op jit(solution)/shard_map/ppermute | solution.py:154
  5.8 1.4 %collective-permute-start.2 = (bf16[2,32,256]{2,1,0:T(8,128)(2,1)S(1)}, bf16[2,32,256]{2,1,0:T(8,128)(2,1)S(1)}, u32[]{:S(2)}, u32[]{:S(2)}) collective-permute-start(bf16[2,32,256]{2,1,0:T(8,128)(2,1)S(1)} %bitcast.100), channel_id=1, source_target_pairs={{0,24},{8,0},{16,8},{24,16},{1,25},{9,1},{17,9},{25,17},{2,26},{10... | collective-permute-start | bytes 98312 | tf_op jit(solution)/shard_map/ppermute | solution.py:154
  7.2 0.6 collective-permute-start
  7.8 0.0 collective-permute-done.1
  7.8 1.9 %collective-permute-done.2 = bf16[2,32,256]{2,1,0:T(8,128)(2,1)S(1)} collective-permute-done((bf16[2,32,256]{2,1,0:T(8,128)(2,1)S(1)}, bf16[2,32,256]{2,1,0:T(8,128)(2,1)S(1)}, u32[]{:S(2)}, u32[]{:S(2)}) %collective-permute-start.2) | collective-permute-done | bytes 32800 | tf_op jit(solution)/shard_map/ppermute | solution.py:154
  9.7 2.3 %collective-permute-done = bf16[2,32,256]{2,1,0:T(8,128)(2,1)S(1)} collective-permute-done((bf16[2,32,256]{2,1,0:T(8,128)(2,1)S(1)}, bf16[2,32,256]{2,1,0:T(8,128)(2,1)S(1)}, u32[]{:S(2)}, u32[]{:S(2)}) %collective-permute-start) | collective-permute-done | bytes 32800 | tf_op jit(solution)/shard_map/ppermute | solution.py:154
  12.1 0.0 copy-start.2
  12.1 1.6 %collective-permute-start.3 = (bf16[4,2,32,256]{3,2,1,0:T(8,128)(2,1)S(1)}, bf16[4,2,32,256]{3,2,1,0:T(8,128)(2,1)S(1)}, u32[]{:S(2)}, u32[]{:S(2)}) collective-permute-start(bf16[4,2,32,256]{3,2,1,0:T(8,128)(2,1)S(1)} %get-tuple-element.35), channel_id=1, source_target_pairs={{0,2},{1,3},{2,4},{3,5},{4,6},{5,7},{6,0},{7,1},{8,10},{9,11},{10,... | collective-permute-start | bytes 393224 | tf_op jit(solution)/shard_map/ppermute | solution.py:171
  13.8 2.6 %collective-permute-start.4 = (bf16[4,2,32,256]{3,2,1,0:T(8,128)(2,1)S(1)}, bf16[4,2,32,256]{3,2,1,0:T(8,128)(2,1)S(1)}, u32[]{:S(2)}, u32[]{:S(2)}) collective-permute-start(bf16[4,2,32,256]{3,2,1,0:T(8,128)(2,1)S(1)} %get-tuple-element.35), channel_id=1, source_target_pairs={{0,4},{1,5},{2,6},{3,7},{4,0},{5,1},{6,2},{7,3},{8,12},{9,13},{10,... | collective-permute-start | bytes 393224 | tf_op jit(solution)/shard_map/ppermute | solution.py:171
  16.4 1.3 %collective-permute-start.5 = (bf16[4,2,32,256]{3,2,1,0:T(8,128)(2,1)S(1)}, bf16[4,2,32,256]{3,2,1,0:T(8,128)(2,1)S(1)}, u32[]{:S(2)}, u32[]{:S(2)}) collective-permute-start(bf16[4,2,32,256]{3,2,1,0:T(8,128)(2,1)S(1)} %get-tuple-element.35), channel_id=1, source_target_pairs={{0,6},{1,7},{2,0},{3,1},{4,2},{5,3},{6,4},{7,5},{8,14},{9,15},{10,... | collective-permute-start | bytes 393224 | tf_op jit(solution)/shard_map/ppermute | solution.py:171
  17.7 0.0 copy-done.1
  17.7 0.2 reduce_window_sum.11
  17.9 2.6 %collective-permute-done.3 = bf16[4,2,32,256]{3,2,1,0:T(8,128)(2,1)S(1)} collective-permute-done((bf16[4,2,32,256]{3,2,1,0:T(8,128)(2,1)S(1)}, bf16[4,2,32,256]{3,2,1,0:T(8,128)(2,1)S(1)}, u32[]{:S(2)}, u32[]{:S(2)}) %collective-permute-start.3) | collective-permute-done | bytes 131104 | tf_op jit(solution)/shard_map/ppermute | solution.py:171
  20.5 3.1 %collective-permute-done.4 = bf16[4,2,32,256]{3,2,1,0:T(8,128)(2,1)S(1)} collective-permute-done((bf16[4,2,32,256]{3,2,1,0:T(8,128)(2,1)S(1)}, bf16[4,2,32,256]{3,2,1,0:T(8,128)(2,1)S(1)}, u32[]{:S(2)}, u32[]{:S(2)}) %collective-permute-start.4) | collective-permute-done | bytes 131104 | tf_op jit(solution)/shard_map/ppermute | solution.py:171
  23.6 0.0 collective-permute-done.5
  23.6 0.1 pad_maximum_fusion
  23.7 0.1 fusion.29
  23.8 0.1 collective-permute-start.6
  24.0 0.1 copy.23
  24.1 0.6 reshape.61.user_ref
  24.7 0.0 copy-done.2
  24.7 1.2 %minimum_multiply_fusion = (s32[128]{0:T(128)}, s32[]{:T(128)}) fusion(s32[128]{0:T(128)S(1)} %copy-done.2), kind=kLoop, calls=%fused_computation.76 | loop fusion | flops 1663 | bytes 1028 | tf_op jit(solution)/shard_map/mul | solution.py:238
  25.9 0.1 collective-permute-done.6
  26.0 1.4 %fusion.5 = f32[4,2,4,2,32,256]{5,4,3,2,0,1:T(8,128)S(1)} fusion(bf16[4,1,4,2,32,256]{5,4,3,2,0,1:T(8,128)(2,1)} %bitcast.18, bf16[4,1,4,2,32,256]{5,4,3,2,0,1:T(8,128)(2,1)S(1)} %get-tuple-element.18, pred[]{:T(512)S(6)} %eq.29), kind=kLoop, calls=%fused_computation.7 | loop fusion | flops 2097152 | bytes 3145729 | tf_op jit(solution)/shard_map/convert_element_type | solution.py:259
  27.4 0.2 copy.28
  27.6 1.5 %copy.29 = f32[2,4,8,32,256]{4,3,2,1,0:T(8,128)} copy(f32[2,4,8,32,256]{4,3,0,1,2:T(8,128)S(1)} %bitcast.80) | data formatting | bytes 4194304 | tf_op jit(solution)/shard_map/convert_element_type | solution.py:259
  29.1 15.1 %shard_map.91 = f32[2,1024,256]{2,1,0:T(8,128)} custom-call(s32[128]{0:T(128)} %owner_ref.1, s32[128]{0:T(128)} %rank_ref.1, s32[16]{0:T(128)} %len_ref.1, s32[128]{0:T(128)} %reshape.61.user_ref, s32[1]{0:T(128)} %bitcast.4.last_ref, s32[128]{0:T(128)} %get-tuple-element.46.row_ref, f32[2,1024,256]{2,1,0:T(8,128)} %bitcast.81, bf16[16384,256]{1,0:T(8,128)(2,1)} %k_ref.1, ...), custom_call_target="tpu_custom_call" | custom-call | tf_op jit(solution)/shard_map/pallas_call | solution.py:245
  44.2 1.3 %fusion.6 = bf16[2,4,4,32,256]{4,3,2,1,0:T(8,128)(2,1)S(1)} fusion(f32[2,4,4,2,32,256]{5,4,3,2,1,0:T(8,128)} %bitcast.82, s32[]{:T(128)S(6)} %select_n.201), kind=kLoop, calls=%fused_computation.10 | loop fusion | bytes 1048580 | tf_op jit(solution)/shard_map/convert_element_type | solution.py:128
  45.5 0.5 collective-permute-start.7
  46.0 1.7 %collective-permute-done.7 = bf16[2,4,4,32,256]{4,3,2,1,0:T(8,128)(2,1)} collective-permute-done((bf16[2,4,4,32,256]{4,3,2,1,0:T(8,128)(2,1)S(1)}, bf16[2,4,4,32,256]{4,3,2,1,0:T(8,128)(2,1)}, u32[]{:S(2)}, u32[]{:S(2)}) %collective-permute-start.7) | collective-permute-done | bytes 524320 | tf_op jit(solution)/shard_map/ppermute | solution.py:127
  47.7 1.5 %bitcast_add_fusion = f32[2,4,4,32,256]{4,3,2,1,0:T(8,128)S(1)} fusion(bf16[2,4,4,32,256]{4,3,2,1,0:T(8,128)(2,1)} %collective-permute-done.7, f32[2,4,4,2,32,256]{5,4,3,2,1,0:T(8,128)} %bitcast.83, s32[]{:T(128)S(6)} %select_n.200), kind=kLoop, calls=%fused_computation.8 | loop fusion | flops 524288 | bytes 2621444 | tf_op jit(solution)/shard_map/add | solution.py:130
  49.2 0.8 fusion.19
  50.0 5.6 %collective-permute-start.10 = (bf16[2,4,32,256]{3,2,1,0:T(8,128)(2,1)}, bf16[2,4,32,256]{3,2,1,0:T(8,128)(2,1)S(1)}, u32[]{:S(2)}, u32[]{:S(2)}) collective-permute-start(bf16[2,4,32,256]{3,2,1,0:T(8,128)(2,1)} %get-tuple-element.16), channel_id=1, source_target_pairs={{0,6},{1,7},{2,0},{3,1},{4,2},{5,3},{6,4},{7,5},{8,14},{9,15},{10,... | collective-permute-start | bytes 393224 | tf_op jit(solution)/shard_map/ppermute | solution.py:140
  55.6 5.6 %collective-permute-start.8 = (bf16[2,4,32,256]{3,2,1,0:T(8,128)(2,1)}, bf16[2,4,32,256]{3,2,1,0:T(8,128)(2,1)S(1)}, u32[]{:S(2)}, u32[]{:S(2)}) collective-permute-start(bf16[2,4,32,256]{3,2,1,0:T(8,128)(2,1)} %get-tuple-element.15), channel_id=1, source_target_pairs={{0,2},{1,3},{2,4},{3,5},{4,6},{5,7},{6,0},{7,1},{8,10},{9,11},{10,... | collective-permute-start | bytes 393224 | tf_op jit(solution)/shard_map/ppermute | solution.py:140
  61.2 1.5 %collective-permute-start.9 = (bf16[2,4,32,256]{3,2,1,0:T(8,128)(2,1)}, bf16[2,4,32,256]{3,2,1,0:T(8,128)(2,1)S(1)}, u32[]{:S(2)}, u32[]{:S(2)}) collective-permute-start(bf16[2,4,32,256]{3,2,1,0:T(8,128)(2,1)} %get-tuple-element.17), channel_id=1, source_target_pairs={{0,4},{1,5},{2,6},{3,7},{4,0},{5,1},{6,2},{7,3},{8,12},{9,13},{10,... | collective-permute-start | bytes 393224 | tf_op jit(solution)/shard_map/ppermute | solution.py:140
  62.6 3.6 %collective-permute-done.10 = bf16[2,4,32,256]{3,2,1,0:T(8,128)(2,1)S(1)} collective-permute-done((bf16[2,4,32,256]{3,2,1,0:T(8,128)(2,1)}, bf16[2,4,32,256]{3,2,1,0:T(8,128)(2,1)S(1)}, u32[]{:S(2)}, u32[]{:S(2)}) %collective-permute-start.10) | collective-permute-done | bytes 131104 | tf_op jit(solution)/shard_map/ppermute | solution.py:140
  66.2 2.8 %collective-permute-done.8 = bf16[2,4,32,256]{3,2,1,0:T(8,128)(2,1)S(1)} collective-permute-done((bf16[2,4,32,256]{3,2,1,0:T(8,128)(2,1)}, bf16[2,4,32,256]{3,2,1,0:T(8,128)(2,1)S(1)}, u32[]{:S(2)}, u32[]{:S(2)}) %collective-permute-start.8) | collective-permute-done | bytes 131104 | tf_op jit(solution)/shard_map/ppermute | solution.py:140
  69.0 6.0 %collective-permute-done.9 = bf16[2,4,32,256]{3,2,1,0:T(8,128)(2,1)S(1)} collective-permute-done((bf16[2,4,32,256]{3,2,1,0:T(8,128)(2,1)}, bf16[2,4,32,256]{3,2,1,0:T(8,128)(2,1)S(1)}, u32[]{:S(2)}, u32[]{:S(2)}) %collective-permute-start.9) | collective-permute-done | bytes 131104 | tf_op jit(solution)/shard_map/ppermute | solution.py:140
  75.0 0.1 fusion.8
  75.1 0.4 collective-permute-start.11
  75.5 1.3 %collective-permute-start.12 = (f32[2,32,256]{2,1,0:T(8,128)S(1)}, f32[2,32,256]{2,1,0:T(8,128)S(1)}, u32[]{:S(2)}, u32[]{:S(2)}) collective-permute-start(f32[2,32,256]{2,1,0:T(8,128)S(1)} %get-tuple-element.32), channel_id=1, source_target_pairs={{0,16},{8,24},{16,0},{24,8},{1,17},{9,25},{17,1},{25,9},{2,18},{10... | collective-permute-start | bytes 196616 | tf_op jit(solution)/shard_map/ppermute | solution.py:192
  76.8 2.8 %collective-permute-start.13 = (f32[2,32,256]{2,1,0:T(8,128)S(1)}, f32[2,32,256]{2,1,0:T(8,128)S(1)}, u32[]{:S(2)}, u32[]{:S(2)}) collective-permute-start(f32[2,32,256]{2,1,0:T(8,128)S(1)} %get-tuple-element.31), channel_id=1, source_target_pairs={{0,24},{8,0},{16,8},{24,16},{1,25},{9,1},{17,9},{25,17},{2,26},{10... | collective-permute-start | bytes 196616 | tf_op jit(solution)/shard_map/ppermute | solution.py:192
  79.6 1.2 %collective-permute-done.11 = f32[2,32,256]{2,1,0:T(8,128)S(1)} collective-permute-done((f32[2,32,256]{2,1,0:T(8,128)S(1)}, f32[2,32,256]{2,1,0:T(8,128)S(1)}, u32[]{:S(2)}, u32[]{:S(2)}) %collective-permute-start.11) | collective-permute-done | bytes 65568 | tf_op jit(solution)/shard_map/ppermute | solution.py:192
  80.9 0.0 collective-permute-done.12
  80.9 0.7 collective-permute-done.13
  81.5 0.1 fusion.31
  81.7 0.1 div.55
  81.8 0.2 multiply_reduce_fusion
  82.0 0.0 copy-done
  82.0 3.1 %fusion.4 = bf16[64,1024]{1,0:T(8,128)(2,1)} fusion(bf16[1024,1024]{1,0:T(8,128)(2,1)S(1)} %copy-done, bf16[64,1024]{1,0:T(8,128)(2,1)} %bitcast.107, bf16[1024,2048]{1,0:T(8,128)(2,1)} %param.10, f32[64,256]{1,0:T(8,128)S(1)} %bitcast.87, f32[64,256]{1,0:T(8,128)S(1)} %bitcast.89, f32[64,256]{1,0:T(8,128)S(1)} %bitcast.91, f32[64,256]{1,0:T(8,128)S(1)} %bitcast.85, ...), kind=kOutput, calls=%fused_computation.5 | convolution fusion | flops 269484032 | bytes 4850176 | tf_op jit(solution)/shard_map/dot_general | solution.py:269
  (14 shorter events, 0.2 us)
Async XLA Ops:
  0.0 82.0 %copy-start = (bf16[1024,1024]{1,0:T(8,128)(2,1)S(1)}, bf16[1024,1024]{1,0:T(8,128)(2,1)}, u32[]{:S(2)}) copy-start(bf16[1024,1024]{1,0:T(8,128)(2,1)} %param.11) | copy-start | bytes 6291460
  2.3 15.4 %copy-start.1 = (s32[2,16]{1,0:T(2,128)S(1)}, s32[2,16]{1,0:T(2,128)}, u32[]{:S(2)}) copy-start(s32[2,16]{1,0:T(2,128)} %param.15) | copy-start | bytes 388
  2.7 5.1 %collective-permute-start.1 = (bf16[2,32,256]{2,1,0:T(8,128)(2,1)S(1)}, bf16[2,32,256]{2,1,0:T(8,128)(2,1)S(1)}, u32[]{:S(2)}, u32[]{:S(2)}) collective-permute-start(bf16[2,32,256]{2,1,0:T(8,128)(2,1)S(1)} %bitcast.99), channel_id=1, source_target_pairs={{0,16},{8,24},{16,0},{24,8},{1,17},{9,25},{17,1},{25,9},{2,18},{10... | collective-permute-start | bytes 98312 | tf_op jit(solution)/shard_map/ppermute | solution.py:154
  5.8 3.9 %collective-permute-start.2 = (bf16[2,32,256]{2,1,0:T(8,128)(2,1)S(1)}, bf16[2,32,256]{2,1,0:T(8,128)(2,1)S(1)}, u32[]{:S(2)}, u32[]{:S(2)}) collective-permute-start(bf16[2,32,256]{2,1,0:T(8,128)(2,1)S(1)} %bitcast.100), channel_id=1, source_target_pairs={{0,24},{8,0},{16,8},{24,16},{1,25},{9,1},{17,9},{25,17},{2,26},{10... | collective-permute-start | bytes 98312 | tf_op jit(solution)/shard_map/ppermute | solution.py:154
  7.2 4.8 %collective-permute-start = (bf16[2,32,256]{2,1,0:T(8,128)(2,1)S(1)}, bf16[2,32,256]{2,1,0:T(8,128)(2,1)S(1)}, u32[]{:S(2)}, u32[]{:S(2)}) collective-permute-start(bf16[2,32,256]{2,1,0:T(8,128)(2,1)S(1)} %bitcast.101), channel_id=1, source_target_pairs={{0,8},{8,16},{16,24},{24,0},{1,9},{9,17},{17,25},{25,1},{2,10},{10... | collective-permute-start | bytes 98312 | tf_op jit(solution)/shard_map/ppermute | solution.py:154
  12.1 12.6 %copy-start.2 = (s32[128]{0:T(128)S(1)}, s32[128]{0:T(128)}, u32[]{:S(2)}) copy-start(s32[128]{0:T(128)} %owner_ref.1) | copy-start | bytes 1540
  12.1 8.3 %collective-permute-start.3 = (bf16[4,2,32,256]{3,2,1,0:T(8,128)(2,1)S(1)}, bf16[4,2,32,256]{3,2,1,0:T(8,128)(2,1)S(1)}, u32[]{:S(2)}, u32[]{:S(2)}) collective-permute-start(bf16[4,2,32,256]{3,2,1,0:T(8,128)(2,1)S(1)} %get-tuple-element.35), channel_id=1, source_target_pairs={{0,2},{1,3},{2,4},{3,5},{4,6},{5,7},{6,0},{7,1},{8,10},{9,11},{10,... | collective-permute-start | bytes 393224 | tf_op jit(solution)/shard_map/ppermute | solution.py:171
  13.8 9.9 %collective-permute-start.4 = (bf16[4,2,32,256]{3,2,1,0:T(8,128)(2,1)S(1)}, bf16[4,2,32,256]{3,2,1,0:T(8,128)(2,1)S(1)}, u32[]{:S(2)}, u32[]{:S(2)}) collective-permute-start(bf16[4,2,32,256]{3,2,1,0:T(8,128)(2,1)S(1)} %get-tuple-element.35), channel_id=1, source_target_pairs={{0,4},{1,5},{2,6},{3,7},{4,0},{5,1},{6,2},{7,3},{8,12},{9,13},{10,... | collective-permute-start | bytes 393224 | tf_op jit(solution)/shard_map/ppermute | solution.py:171
  16.4 7.3 %collective-permute-start.5 = (bf16[4,2,32,256]{3,2,1,0:T(8,128)(2,1)S(1)}, bf16[4,2,32,256]{3,2,1,0:T(8,128)(2,1)S(1)}, u32[]{:S(2)}, u32[]{:S(2)}) collective-permute-start(bf16[4,2,32,256]{3,2,1,0:T(8,128)(2,1)S(1)} %get-tuple-element.35), channel_id=1, source_target_pairs={{0,6},{1,7},{2,0},{3,1},{4,2},{5,3},{6,4},{7,5},{8,14},{9,15},{10,... | collective-permute-start | bytes 393224 | tf_op jit(solution)/shard_map/ppermute | solution.py:171
  23.8 2.1 %collective-permute-start.6 = (bf16[4,4,2,32,256]{4,3,2,1,0:T(8,128)(2,1)S(1)}, bf16[4,4,2,32,256]{4,3,2,1,0:T(8,128)(2,1)}, u32[]{:S(2)}, u32[]{:S(2)}) collective-permute-start(bf16[4,4,2,32,256]{4,3,2,1,0:T(8,128)(2,1)S(1)} %get-tuple-element.19), channel_id=1, source_target_pairs={{0,1},{1,0},{2,3},{3,2},{4,5},{5,4},{6,7},{7,6},{8,9},{9,8},{10,11... | collective-permute-start | bytes 1572872 | tf_op jit(solution)/shard_map/ppermute | solution.py:179
  45.5 2.1 %collective-permute-start.7 = (bf16[2,4,4,32,256]{4,3,2,1,0:T(8,128)(2,1)S(1)}, bf16[2,4,4,32,256]{4,3,2,1,0:T(8,128)(2,1)}, u32[]{:S(2)}, u32[]{:S(2)}) collective-permute-start(bf16[2,4,4,32,256]{4,3,2,1,0:T(8,128)(2,1)S(1)} %fusion.6), channel_id=1, source_target_pairs={{0,1},{1,0},{2,3},{3,2},{4,5},{5,4},{6,7},{7,6},{8,9},{9,8},{10,11... | collective-permute-start | bytes 1572872 | tf_op jit(solution)/shard_map/ppermute | solution.py:127
  50.0 16.2 %collective-permute-start.10 = (bf16[2,4,32,256]{3,2,1,0:T(8,128)(2,1)}, bf16[2,4,32,256]{3,2,1,0:T(8,128)(2,1)S(1)}, u32[]{:S(2)}, u32[]{:S(2)}) collective-permute-start(bf16[2,4,32,256]{3,2,1,0:T(8,128)(2,1)} %get-tuple-element.16), channel_id=1, source_target_pairs={{0,6},{1,7},{2,0},{3,1},{4,2},{5,3},{6,4},{7,5},{8,14},{9,15},{10,... | collective-permute-start | bytes 393224 | tf_op jit(solution)/shard_map/ppermute | solution.py:140
  55.6 13.4 %collective-permute-start.8 = (bf16[2,4,32,256]{3,2,1,0:T(8,128)(2,1)}, bf16[2,4,32,256]{3,2,1,0:T(8,128)(2,1)S(1)}, u32[]{:S(2)}, u32[]{:S(2)}) collective-permute-start(bf16[2,4,32,256]{3,2,1,0:T(8,128)(2,1)} %get-tuple-element.15), channel_id=1, source_target_pairs={{0,2},{1,3},{2,4},{3,5},{4,6},{5,7},{6,0},{7,1},{8,10},{9,11},{10,... | collective-permute-start | bytes 393224 | tf_op jit(solution)/shard_map/ppermute | solution.py:140
  61.2 13.8 %collective-permute-start.9 = (bf16[2,4,32,256]{3,2,1,0:T(8,128)(2,1)}, bf16[2,4,32,256]{3,2,1,0:T(8,128)(2,1)S(1)}, u32[]{:S(2)}, u32[]{:S(2)}) collective-permute-start(bf16[2,4,32,256]{3,2,1,0:T(8,128)(2,1)} %get-tuple-element.17), channel_id=1, source_target_pairs={{0,4},{1,5},{2,6},{3,7},{4,0},{5,1},{6,2},{7,3},{8,12},{9,13},{10,... | collective-permute-start | bytes 393224 | tf_op jit(solution)/shard_map/ppermute | solution.py:140
  75.1 5.8 %collective-permute-start.11 = (f32[2,32,256]{2,1,0:T(8,128)S(1)}, f32[2,32,256]{2,1,0:T(8,128)S(1)}, u32[]{:S(2)}, u32[]{:S(2)}) collective-permute-start(f32[2,32,256]{2,1,0:T(8,128)S(1)} %get-tuple-element.33), channel_id=1, source_target_pairs={{0,8},{8,16},{16,24},{24,0},{1,9},{9,17},{17,25},{25,1},{2,10},{10... | collective-permute-start | bytes 196616 | tf_op jit(solution)/shard_map/ppermute | solution.py:192
  75.5 5.4 %collective-permute-start.12 = (f32[2,32,256]{2,1,0:T(8,128)S(1)}, f32[2,32,256]{2,1,0:T(8,128)S(1)}, u32[]{:S(2)}, u32[]{:S(2)}) collective-permute-start(f32[2,32,256]{2,1,0:T(8,128)S(1)} %get-tuple-element.32), channel_id=1, source_target_pairs={{0,16},{8,24},{16,0},{24,8},{1,17},{9,25},{17,1},{25,9},{2,18},{10... | collective-permute-start | bytes 196616 | tf_op jit(solution)/shard_map/ppermute | solution.py:192
  76.8 4.8 %collective-permute-start.13 = (f32[2,32,256]{2,1,0:T(8,128)S(1)}, f32[2,32,256]{2,1,0:T(8,128)S(1)}, u32[]{:S(2)}, u32[]{:S(2)}) collective-permute-start(f32[2,32,256]{2,1,0:T(8,128)S(1)} %get-tuple-element.31), channel_id=1, source_target_pairs={{0,24},{8,0},{16,8},{24,16},{1,25},{9,1},{17,9},{25,17},{2,26},{10... | collective-permute-start | bytes 196616 | tf_op jit(solution)/shard_map/ppermute | solution.py:192

commit v6 on v5

--- a/solution.py
+++ b/solution.py
@@ -41,7 +41,7 @@
                 keep = (row_ids >= user_ref[entry + 2]) & (row_ids < user_ref[entry + 3])
                 user_q[pl.ds(pl.multiple_of(user * (micro * window) + m * window, window), window), :] = jnp.where(
                     keep, rows[:window], 0.0
-                )
+                ).astype(jnp.bfloat16)
                 return carry
 
             lax.fori_loop(0, USERS, fill, 0)
@@ -59,7 +59,7 @@
             keys = jnp.where(key_ids < klen, k_ref[rows, :], 0)
             values = v_ref[rows, :]
             user_rows = pl.ds(pl.multiple_of(row_ref[slot], micro * window), micro * window)
-            queries = user_q[user_rows, :].astype(jnp.bfloat16)
+            queries = user_q[user_rows, :]
             if heads_here == 2:
                 lanes = lax.broadcasted_iota(jnp.int32, (1, 2 * HEAD_DIM), 1)
                 first = lanes < HEAD_DIM
@@ -250,7 +250,7 @@
             in_specs=[whole, tiles, tiles],
             out_specs=whole,
             scratch_shapes=[
-                pltpu.VMEM((USERS * micro * window, head_cols), jnp.float32),
+                pltpu.VMEM((USERS * micro * window, head_cols), jnp.bfloat16),
                 pltpu.VMEM((USERS * micro * window, head_cols), jnp.float32),
             ],
         ),

time: 83.7 us -> 82.4 us (0.984); the launches traced: 85.1 us -> 80.8 us
  starting transfers between devices: 28.3 us -> 17.7 us
  Pallas kernels: 15.1 us -> 22.4 us
  waiting for transfers between devices: 26 us -> 25 us
    ppermute x3, starting transfers between devices: 12.7 us -> 2.04 us  [reduce_over_hist(): total = total + lax.ppermute(send, 'hist', perm=perm).astype(jnp.float32)]
    pallas_call x1, Pallas kernels: 15.1 us -> 22.4 us  [body(): pl.pallas_call(functools.partial(attend_kernel, window=window, heads_here...]
    ppermute x3, waiting for transfers between devices: 12.4 us -> 11.4 us  [reduce_over_hist(): total = total + lax.ppermute(send, 'hist', perm=perm).astype(jnp.float32)]
  transfers between devices with their start and end apart: 14 -> 14, of which waited for: 11 -> 10; matrix products, arithmetic and copies ran while one was open for 2% -> 3% of each run, Pallas kernels for 0% -> 0%
where the time goes in v6:
time: 82.4 us; the launch traced here: 80.8 us
  waiting for transfers between devices  25 us (30%)
  Pallas kernels  22.4 us (27%)
  starting transfers between devices  17.7 us (21%)
  matrix products  5.45 us (7%)
  local copies, waits for them, and re-layouts  5.04 us (6%)
  other arithmetic  4.97 us (6%)
    pallas_call x1, Pallas kernels, body(): pl.pallas_call(functools.partial(attend_kernel, window=window, heads_here...  22.4 us
    ppermute x3, waiting for transfers between devices, reduce_over_hist(): total = total + lax.ppermute(send, 'hist', perm=perm).astype(jnp.float32)  11.4 us
    ppermute x3, waiting for transfers between devices, gather_queries(): by_offset.append(lax.ppermute(sources, 'hist', perm=perm))  5.73 us
    ppermute x3, starting transfers between devices, gather_queries(): by_offset.append(lax.ppermute(sources, 'hist', perm=perm))  5.57 us
    ppermute x3, starting transfers between devices, gather_queries(): lax.ppermute(piece, 'cand', perm=[(i, (i + shift) % n_cand) for i in rang...  5.06 us
    ppermute x3, starting transfers between devices, spread_over_cand(): lax.ppermute(piece, 'cand', perm=[(i, (i + shift) % n_cand) for i in rang...  4.5 us
    ppermute x3, waiting for transfers between devices, gather_queries(): lax.ppermute(piece, 'cand', perm=[(i, (i + shift) % n_cand) for i in rang...  4.21 us
    dot_general x1, matrix products, body(): jnp.dot(mixed_rows, out_weight, preferred_element_type=jnp.float32)  3.14 us
  transfers between devices with their start and end apart: 14, of which 10 were waited for; matrix products, arithmetic and copies ran while one was open for 3% of the time, Pallas kernels for 0%

profile of v6, /device:TPU:0, one launch (start us, length us, event | category | flops | bytes accessed | tf_op | source)
XLA Modules:
  0.0 80.8 jit_solution(10171786466154506619)
XLA Ops:
  0.0 0.0 copy-start
  0.0 2.3 %multiply_convert_fusion.2 = bf16[64,1024]{1,0:T(8,128)(2,1)S(1)} fusion(bf16[64,1024]{1,0:T(8,128)(2,1)} %bitcast.106, bf16[1024,2048]{1,0:T(8,128)(2,1)} %param.10), kind=kOutput, calls=%fused_computation.25 | convolution fusion | flops 134545408 | bytes 2359296 | tf_op jit(solution)/shard_map/dot_general | solution.py:218
  2.3 0.0 copy-start.1
  2.3 0.1 reshape_reshape.6
  2.4 0.3 constant_dynamic-slice_fusion.15
  2.7 3.0 %collective-permute-start.1 = (bf16[2,32,256]{2,1,0:T(8,128)(2,1)S(1)}, bf16[2,32,256]{2,1,0:T(8,128)(2,1)S(1)}, u32[]{:S(2)}, u32[]{:S(2)}) collective-permute-start(bf16[2,32,256]{2,1,0:T(8,128)(2,1)S(1)} %bitcast.99), channel_id=1, source_target_pairs={{0,16},{8,24},{16,0},{24,8},{1,17},{9,25},{17,1},{25,9},{2,18},{10... | collective-permute-start | bytes 98312 | tf_op jit(solution)/shard_map/ppermute | solution.py:154
  5.8 1.4 %collective-permute-start.2 = (bf16[2,32,256]{2,1,0:T(8,128)(2,1)S(1)}, bf16[2,32,256]{2,1,0:T(8,128)(2,1)S(1)}, u32[]{:S(2)}, u32[]{:S(2)}) collective-permute-start(bf16[2,32,256]{2,1,0:T(8,128)(2,1)S(1)} %bitcast.100), channel_id=1, source_target_pairs={{0,24},{8,0},{16,8},{24,16},{1,25},{9,1},{17,9},{25,17},{2,26},{10... | collective-permute-start | bytes 98312 | tf_op jit(solution)/shard_map/ppermute | solution.py:154
  7.2 0.6 collective-permute-start
  7.8 0.0 collective-permute-done.1
  7.8 1.9 %collective-permute-done.2 = bf16[2,32,256]{2,1,0:T(8,128)(2,1)S(1)} collective-permute-done((bf16[2,32,256]{2,1,0:T(8,128)(2,1)S(1)}, bf16[2,32,256]{2,1,0:T(8,128)(2,1)S(1)}, u32[]{:S(2)}, u32[]{:S(2)}) %collective-permute-start.2) | collective-permute-done | bytes 32800 | tf_op jit(solution)/shard_map/ppermute | solution.py:154
  9.7 2.3 %collective-permute-done = bf16[2,32,256]{2,1,0:T(8,128)(2,1)S(1)} collective-permute-done((bf16[2,32,256]{2,1,0:T(8,128)(2,1)S(1)}, bf16[2,32,256]{2,1,0:T(8,128)(2,1)S(1)}, u32[]{:S(2)}, u32[]{:S(2)}) %collective-permute-start) | collective-permute-done | bytes 32800 | tf_op jit(solution)/shard_map/ppermute | solution.py:154
  12.1 0.0 copy-start.2
  12.1 1.6 %collective-permute-start.3 = (bf16[4,2,32,256]{3,2,1,0:T(8,128)(2,1)S(1)}, bf16[4,2,32,256]{3,2,1,0:T(8,128)(2,1)S(1)}, u32[]{:S(2)}, u32[]{:S(2)}) collective-permute-start(bf16[4,2,32,256]{3,2,1,0:T(8,128)(2,1)S(1)} %get-tuple-element.35), channel_id=1, source_target_pairs={{0,2},{1,3},{2,4},{3,5},{4,6},{5,7},{6,0},{7,1},{8,10},{9,11},{10,... | collective-permute-start | bytes 393224 | tf_op jit(solution)/shard_map/ppermute | solution.py:171
  13.8 2.6 %collective-permute-start.4 = (bf16[4,2,32,256]{3,2,1,0:T(8,128)(2,1)S(1)}, bf16[4,2,32,256]{3,2,1,0:T(8,128)(2,1)S(1)}, u32[]{:S(2)}, u32[]{:S(2)}) collective-permute-start(bf16[4,2,32,256]{3,2,1,0:T(8,128)(2,1)S(1)} %get-tuple-element.35), channel_id=1, source_target_pairs={{0,4},{1,5},{2,6},{3,7},{4,0},{5,1},{6,2},{7,3},{8,12},{9,13},{10,... | collective-permute-start | bytes 393224 | tf_op jit(solution)/shard_map/ppermute | solution.py:171
  16.4 1.3 %collective-permute-start.5 = (bf16[4,2,32,256]{3,2,1,0:T(8,128)(2,1)S(1)}, bf16[4,2,32,256]{3,2,1,0:T(8,128)(2,1)S(1)}, u32[]{:S(2)}, u32[]{:S(2)}) collective-permute-start(bf16[4,2,32,256]{3,2,1,0:T(8,128)(2,1)S(1)} %get-tuple-element.35), channel_id=1, source_target_pairs={{0,6},{1,7},{2,0},{3,1},{4,2},{5,3},{6,4},{7,5},{8,14},{9,15},{10,... | collective-permute-start | bytes 393224 | tf_op jit(solution)/shard_map/ppermute | solution.py:171
  17.7 0.0 copy-done.1
  17.7 0.2 reduce_window_sum.11
  17.9 2.6 %collective-permute-done.3 = bf16[4,2,32,256]{3,2,1,0:T(8,128)(2,1)S(1)} collective-permute-done((bf16[4,2,32,256]{3,2,1,0:T(8,128)(2,1)S(1)}, bf16[4,2,32,256]{3,2,1,0:T(8,128)(2,1)S(1)}, u32[]{:S(2)}, u32[]{:S(2)}) %collective-permute-start.3) | collective-permute-done | bytes 131104 | tf_op jit(solution)/shard_map/ppermute | solution.py:171
  20.5 3.1 %collective-permute-done.4 = bf16[4,2,32,256]{3,2,1,0:T(8,128)(2,1)S(1)} collective-permute-done((bf16[4,2,32,256]{3,2,1,0:T(8,128)(2,1)S(1)}, bf16[4,2,32,256]{3,2,1,0:T(8,128)(2,1)S(1)}, u32[]{:S(2)}, u32[]{:S(2)}) %collective-permute-start.4) | collective-permute-done | bytes 131104 | tf_op jit(solution)/shard_map/ppermute | solution.py:171
  23.6 0.0 collective-permute-done.5
  23.6 0.1 pad_maximum_fusion
  23.7 0.1 fusion.29
  23.8 0.1 collective-permute-start.6
  24.0 0.1 copy.23
  24.1 0.6 reshape.61.user_ref
  24.7 0.0 copy-done.2
  24.7 1.2 %minimum_multiply_fusion = (s32[128]{0:T(128)}, s32[]{:T(128)}) fusion(s32[128]{0:T(128)S(1)} %copy-done.2), kind=kLoop, calls=%fused_computation.76 | loop fusion | flops 1663 | bytes 1028 | tf_op jit(solution)/shard_map/mul | solution.py:238
  25.9 0.1 collective-permute-done.6
  26.0 1.4 %fusion.5 = f32[4,2,4,2,32,256]{5,4,3,2,0,1:T(8,128)S(1)} fusion(bf16[4,1,4,2,32,256]{5,4,3,2,0,1:T(8,128)(2,1)} %bitcast.18, bf16[4,1,4,2,32,256]{5,4,3,2,0,1:T(8,128)(2,1)S(1)} %get-tuple-element.18, pred[]{:T(512)S(6)} %eq.29), kind=kLoop, calls=%fused_computation.7 | loop fusion | flops 2097152 | bytes 3145729 | tf_op jit(solution)/shard_map/convert_element_type | solution.py:259
  27.4 0.2 copy.28
  27.6 1.5 %copy.29 = f32[2,4,8,32,256]{4,3,2,1,0:T(8,128)} copy(f32[2,4,8,32,256]{4,3,0,1,2:T(8,128)S(1)} %bitcast.80) | data formatting | bytes 4194304 | tf_op jit(solution)/shard_map/convert_element_type | solution.py:259
  29.1 22.4 %shard_map.91 = f32[2,1024,256]{2,1,0:T(8,128)} custom-call(s32[128]{0:T(128)} %owner_ref.1, s32[128]{0:T(128)} %rank_ref.1, s32[16]{0:T(128)} %len_ref.1, s32[128]{0:T(128)} %reshape.61.user_ref, s32[1]{0:T(128)} %bitcast.4.last_ref, s32[128]{0:T(128)} %get-tuple-element.46.row_ref, f32[2,1024,256]{2,1,0:T(8,128)} %bitcast.81, bf16[16384,256]{1,0:T(8,128)(2,1)} %k_ref.1, ...), custom_call_target="tpu_custom_call" | custom-call | tf_op jit(solution)/shard_map/pallas_call | solution.py:245
  51.5 1.3 %fusion.6 = bf16[2,4,4,32,256]{4,3,2,1,0:T(8,128)(2,1)S(1)} fusion(f32[2,4,4,2,32,256]{5,4,3,2,1,0:T(8,128)} %bitcast.82, s32[]{:T(128)S(6)} %select_n.201), kind=kLoop, calls=%fused_computation.10 | loop fusion | bytes 1048580 | tf_op jit(solution)/shard_map/convert_element_type | solution.py:128
  52.8 0.5 collective-permute-start.7
  53.2 1.7 %collective-permute-done.7 = bf16[2,4,4,32,256]{4,3,2,1,0:T(8,128)(2,1)} collective-permute-done((bf16[2,4,4,32,256]{4,3,2,1,0:T(8,128)(2,1)S(1)}, bf16[2,4,4,32,256]{4,3,2,1,0:T(8,128)(2,1)}, u32[]{:S(2)}, u32[]{:S(2)}) %collective-permute-start.7) | collective-permute-done | bytes 524320 | tf_op jit(solution)/shard_map/ppermute | solution.py:127
  54.9 1.5 %bitcast_add_fusion = f32[2,4,4,32,256]{4,3,2,1,0:T(8,128)S(1)} fusion(bf16[2,4,4,32,256]{4,3,2,1,0:T(8,128)(2,1)} %collective-permute-done.7, f32[2,4,4,2,32,256]{5,4,3,2,1,0:T(8,128)} %bitcast.83, s32[]{:T(128)S(6)} %select_n.200), kind=kLoop, calls=%fused_computation.8 | loop fusion | flops 524288 | bytes 2621444 | tf_op jit(solution)/shard_map/add | solution.py:130
  56.5 0.8 fusion.19
  57.2 0.0 collective-permute-start.10
  57.2 2.0 %collective-permute-start.8 = (bf16[2,4,32,256]{3,2,1,0:T(8,128)(2,1)}, bf16[2,4,32,256]{3,2,1,0:T(8,128)(2,1)S(1)}, u32[]{:S(2)}, u32[]{:S(2)}) collective-permute-start(bf16[2,4,32,256]{3,2,1,0:T(8,128)(2,1)} %get-tuple-element.15), channel_id=1, source_target_pairs={{0,2},{1,3},{2,4},{3,5},{4,6},{5,7},{6,0},{7,1},{8,10},{9,11},{10,... | collective-permute-start | bytes 393224 | tf_op jit(solution)/shard_map/ppermute | solution.py:140
  59.3 0.0 collective-permute-start.9
  59.3 6.8 %collective-permute-done.10 = bf16[2,4,32,256]{3,2,1,0:T(8,128)(2,1)S(1)} collective-permute-done((bf16[2,4,32,256]{3,2,1,0:T(8,128)(2,1)}, bf16[2,4,32,256]{3,2,1,0:T(8,128)(2,1)S(1)}, u32[]{:S(2)}, u32[]{:S(2)}) %collective-permute-start.10) | collective-permute-done | bytes 131104 | tf_op jit(solution)/shard_map/ppermute | solution.py:140
  66.1 0.0 collective-permute-done.8
  66.1 4.6 %collective-permute-done.9 = bf16[2,4,32,256]{3,2,1,0:T(8,128)(2,1)S(1)} collective-permute-done((bf16[2,4,32,256]{3,2,1,0:T(8,128)(2,1)}, bf16[2,4,32,256]{3,2,1,0:T(8,128)(2,1)S(1)}, u32[]{:S(2)}, u32[]{:S(2)}) %collective-permute-start.9) | collective-permute-done | bytes 131104 | tf_op jit(solution)/shard_map/ppermute | solution.py:140
  70.7 0.1 fusion.8
  70.8 0.2 collective-permute-start.11
  71.0 1.5 %collective-permute-start.12 = (f32[2,32,256]{2,1,0:T(8,128)S(1)}, f32[2,32,256]{2,1,0:T(8,128)S(1)}, u32[]{:S(2)}, u32[]{:S(2)}) collective-permute-start(f32[2,32,256]{2,1,0:T(8,128)S(1)} %get-tuple-element.32), channel_id=1, source_target_pairs={{0,16},{8,24},{16,0},{24,8},{1,17},{9,25},{17,1},{25,9},{2,18},{10... | collective-permute-start | bytes 196616 | tf_op jit(solution)/shard_map/ppermute | solution.py:192
  72.4 2.8 %collective-permute-start.13 = (f32[2,32,256]{2,1,0:T(8,128)S(1)}, f32[2,32,256]{2,1,0:T(8,128)S(1)}, u32[]{:S(2)}, u32[]{:S(2)}) collective-permute-start(f32[2,32,256]{2,1,0:T(8,128)S(1)} %get-tuple-element.31), channel_id=1, source_target_pairs={{0,24},{8,0},{16,8},{24,16},{1,25},{9,1},{17,9},{25,17},{2,26},{10... | collective-permute-start | bytes 196616 | tf_op jit(solution)/shard_map/ppermute | solution.py:192
  75.3 1.1 %collective-permute-done.11 = f32[2,32,256]{2,1,0:T(8,128)S(1)} collective-permute-done((f32[2,32,256]{2,1,0:T(8,128)S(1)}, f32[2,32,256]{2,1,0:T(8,128)S(1)}, u32[]{:S(2)}, u32[]{:S(2)}) %collective-permute-start.11) | collective-permute-done | bytes 65568 | tf_op jit(solution)/shard_map/ppermute | solution.py:192
  76.4 0.0 collective-permute-done.12
  76.4 0.8 collective-permute-done.13
  77.2 0.1 fusion.31
  77.4 0.1 div.55
  77.4 0.2 multiply_reduce_fusion
  77.6 0.0 copy-done
  77.7 3.1 %fusion.4 = bf16[64,1024]{1,0:T(8,128)(2,1)} fusion(bf16[1024,1024]{1,0:T(8,128)(2,1)S(1)} %copy-done, bf16[64,1024]{1,0:T(8,128)(2,1)} %bitcast.107, bf16[1024,2048]{1,0:T(8,128)(2,1)} %param.10, f32[64,256]{1,0:T(8,128)S(1)} %bitcast.87, f32[64,256]{1,0:T(8,128)S(1)} %bitcast.89, f32[64,256]{1,0:T(8,128)S(1)} %bitcast.91, f32[64,256]{1,0:T(8,128)S(1)} %bitcast.85, ...), kind=kOutput, calls=%fused_computation.5 | convolution fusion | flops 269484032 | bytes 4850176 | tf_op jit(solution)/shard_map/dot_general | solution.py:269
  (14 shorter events, 0.2 us)
Async XLA Ops:
  0.0 77.6 %copy-start = (bf16[1024,1024]{1,0:T(8,128)(2,1)S(1)}, bf16[1024,1024]{1,0:T(8,128)(2,1)}, u32[]{:S(2)}) copy-start(bf16[1024,1024]{1,0:T(8,128)(2,1)} %param.11) | copy-start | bytes 6291460
  2.3 15.4 %copy-start.1 = (s32[2,16]{1,0:T(2,128)S(1)}, s32[2,16]{1,0:T(2,128)}, u32[]{:S(2)}) copy-start(s32[2,16]{1,0:T(2,128)} %param.15) | copy-start | bytes 388
  2.7 5.1 %collective-permute-start.1 = (bf16[2,32,256]{2,1,0:T(8,128)(2,1)S(1)}, bf16[2,32,256]{2,1,0:T(8,128)(2,1)S(1)}, u32[]{:S(2)}, u32[]{:S(2)}) collective-permute-start(bf16[2,32,256]{2,1,0:T(8,128)(2,1)S(1)} %bitcast.99), channel_id=1, source_target_pairs={{0,16},{8,24},{16,0},{24,8},{1,17},{9,25},{17,1},{25,9},{2,18},{10... | collective-permute-start | bytes 98312 | tf_op jit(solution)/shard_map/ppermute | solution.py:154
  5.8 3.9 %collective-permute-start.2 = (bf16[2,32,256]{2,1,0:T(8,128)(2,1)S(1)}, bf16[2,32,256]{2,1,0:T(8,128)(2,1)S(1)}, u32[]{:S(2)}, u32[]{:S(2)}) collective-permute-start(bf16[2,32,256]{2,1,0:T(8,128)(2,1)S(1)} %bitcast.100), channel_id=1, source_target_pairs={{0,24},{8,0},{16,8},{24,16},{1,25},{9,1},{17,9},{25,17},{2,26},{10... | collective-permute-start | bytes 98312 | tf_op jit(solution)/shard_map/ppermute | solution.py:154
  7.2 4.8 %collective-permute-start = (bf16[2,32,256]{2,1,0:T(8,128)(2,1)S(1)}, bf16[2,32,256]{2,1,0:T(8,128)(2,1)S(1)}, u32[]{:S(2)}, u32[]{:S(2)}) collective-permute-start(bf16[2,32,256]{2,1,0:T(8,128)(2,1)S(1)} %bitcast.101), channel_id=1, source_target_pairs={{0,8},{8,16},{16,24},{24,0},{1,9},{9,17},{17,25},{25,1},{2,10},{10... | collective-permute-start | bytes 98312 | tf_op jit(solution)/shard_map/ppermute | solution.py:154
  12.1 12.6 %copy-start.2 = (s32[128]{0:T(128)S(1)}, s32[128]{0:T(128)}, u32[]{:S(2)}) copy-start(s32[128]{0:T(128)} %owner_ref.1) | copy-start | bytes 1540
  12.1 8.3 %collective-permute-start.3 = (bf16[4,2,32,256]{3,2,1,0:T(8,128)(2,1)S(1)}, bf16[4,2,32,256]{3,2,1,0:T(8,128)(2,1)S(1)}, u32[]{:S(2)}, u32[]{:S(2)}) collective-permute-start(bf16[4,2,32,256]{3,2,1,0:T(8,128)(2,1)S(1)} %get-tuple-element.35), channel_id=1, source_target_pairs={{0,2},{1,3},{2,4},{3,5},{4,6},{5,7},{6,0},{7,1},{8,10},{9,11},{10,... | collective-permute-start | bytes 393224 | tf_op jit(solution)/shard_map/ppermute | solution.py:171
  13.8 9.9 %collective-permute-start.4 = (bf16[4,2,32,256]{3,2,1,0:T(8,128)(2,1)S(1)}, bf16[4,2,32,256]{3,2,1,0:T(8,128)(2,1)S(1)}, u32[]{:S(2)}, u32[]{:S(2)}) collective-permute-start(bf16[4,2,32,256]{3,2,1,0:T(8,128)(2,1)S(1)} %get-tuple-element.35), channel_id=1, source_target_pairs={{0,4},{1,5},{2,6},{3,7},{4,0},{5,1},{6,2},{7,3},{8,12},{9,13},{10,... | collective-permute-start | bytes 393224 | tf_op jit(solution)/shard_map/ppermute | solution.py:171
  16.4 7.3 %collective-permute-start.5 = (bf16[4,2,32,256]{3,2,1,0:T(8,128)(2,1)S(1)}, bf16[4,2,32,256]{3,2,1,0:T(8,128)(2,1)S(1)}, u32[]{:S(2)}, u32[]{:S(2)}) collective-permute-start(bf16[4,2,32,256]{3,2,1,0:T(8,128)(2,1)S(1)} %get-tuple-element.35), channel_id=1, source_target_pairs={{0,6},{1,7},{2,0},{3,1},{4,2},{5,3},{6,4},{7,5},{8,14},{9,15},{10,... | collective-permute-start | bytes 393224 | tf_op jit(solution)/shard_map/ppermute | solution.py:171
  23.8 2.1 %collective-permute-start.6 = (bf16[4,4,2,32,256]{4,3,2,1,0:T(8,128)(2,1)S(1)}, bf16[4,4,2,32,256]{4,3,2,1,0:T(8,128)(2,1)}, u32[]{:S(2)}, u32[]{:S(2)}) collective-permute-start(bf16[4,4,2,32,256]{4,3,2,1,0:T(8,128)(2,1)S(1)} %get-tuple-element.19), channel_id=1, source_target_pairs={{0,1},{1,0},{2,3},{3,2},{4,5},{5,4},{6,7},{7,6},{8,9},{9,8},{10,11... | collective-permute-start | bytes 1572872 | tf_op jit(solution)/shard_map/ppermute | solution.py:179
  52.8 2.1 %collective-permute-start.7 = (bf16[2,4,4,32,256]{4,3,2,1,0:T(8,128)(2,1)S(1)}, bf16[2,4,4,32,256]{4,3,2,1,0:T(8,128)(2,1)}, u32[]{:S(2)}, u32[]{:S(2)}) collective-permute-start(bf16[2,4,4,32,256]{4,3,2,1,0:T(8,128)(2,1)S(1)} %fusion.6), channel_id=1, source_target_pairs={{0,1},{1,0},{2,3},{3,2},{4,5},{5,4},{6,7},{7,6},{8,9},{9,8},{10,11... | collective-permute-start | bytes 1572872 | tf_op jit(solution)/shard_map/ppermute | solution.py:127
  57.2 8.9 %collective-permute-start.10 = (bf16[2,4,32,256]{3,2,1,0:T(8,128)(2,1)}, bf16[2,4,32,256]{3,2,1,0:T(8,128)(2,1)S(1)}, u32[]{:S(2)}, u32[]{:S(2)}) collective-permute-start(bf16[2,4,32,256]{3,2,1,0:T(8,128)(2,1)} %get-tuple-element.16), channel_id=1, source_target_pairs={{0,6},{1,7},{2,0},{3,1},{4,2},{5,3},{6,4},{7,5},{8,14},{9,15},{10,... | collective-permute-start | bytes 393224 | tf_op jit(solution)/shard_map/ppermute | solution.py:140
  57.2 8.9 %collective-permute-start.8 = (bf16[2,4,32,256]{3,2,1,0:T(8,128)(2,1)}, bf16[2,4,32,256]{3,2,1,0:T(8,128)(2,1)S(1)}, u32[]{:S(2)}, u32[]{:S(2)}) collective-permute-start(bf16[2,4,32,256]{3,2,1,0:T(8,128)(2,1)} %get-tuple-element.15), channel_id=1, source_target_pairs={{0,2},{1,3},{2,4},{3,5},{4,6},{5,7},{6,0},{7,1},{8,10},{9,11},{10,... | collective-permute-start | bytes 393224 | tf_op jit(solution)/shard_map/ppermute | solution.py:140
  59.3 11.4 %collective-permute-start.9 = (bf16[2,4,32,256]{3,2,1,0:T(8,128)(2,1)}, bf16[2,4,32,256]{3,2,1,0:T(8,128)(2,1)S(1)}, u32[]{:S(2)}, u32[]{:S(2)}) collective-permute-start(bf16[2,4,32,256]{3,2,1,0:T(8,128)(2,1)} %get-tuple-element.17), channel_id=1, source_target_pairs={{0,4},{1,5},{2,6},{3,7},{4,0},{5,1},{6,2},{7,3},{8,12},{9,13},{10,... | collective-permute-start | bytes 393224 | tf_op jit(solution)/shard_map/ppermute | solution.py:140
  70.8 5.6 %collective-permute-start.11 = (f32[2,32,256]{2,1,0:T(8,128)S(1)}, f32[2,32,256]{2,1,0:T(8,128)S(1)}, u32[]{:S(2)}, u32[]{:S(2)}) collective-permute-start(f32[2,32,256]{2,1,0:T(8,128)S(1)} %get-tuple-element.33), channel_id=1, source_target_pairs={{0,8},{8,16},{16,24},{24,0},{1,9},{9,17},{17,25},{25,1},{2,10},{10... | collective-permute-start | bytes 196616 | tf_op jit(solution)/shard_map/ppermute | solution.py:192
  71.0 5.5 %collective-permute-start.12 = (f32[2,32,256]{2,1,0:T(8,128)S(1)}, f32[2,32,256]{2,1,0:T(8,128)S(1)}, u32[]{:S(2)}, u32[]{:S(2)}) collective-permute-start(f32[2,32,256]{2,1,0:T(8,128)S(1)} %get-tuple-element.32), channel_id=1, source_target_pairs={{0,16},{8,24},{16,0},{24,8},{1,17},{9,25},{17,1},{25,9},{2,18},{10... | collective-permute-start | bytes 196616 | tf_op jit(solution)/shard_map/ppermute | solution.py:192
  72.4 4.8 %collective-permute-start.13 = (f32[2,32,256]{2,1,0:T(8,128)S(1)}, f32[2,32,256]{2,1,0:T(8,128)S(1)}, u32[]{:S(2)}, u32[]{:S(2)}) collective-permute-start(f32[2,32,256]{2,1,0:T(8,128)S(1)} %get-tuple-element.31), channel_id=1, source_target_pairs={{0,24},{8,0},{16,8},{24,16},{1,25},{9,1},{17,9},{25,17},{2,26},{10... | collective-permute-start | bytes 196616 | tf_op jit(solution)/shard_map/ppermute | solution.py:192

commit v7 on v6

--- a/solution.py
+++ b/solution.py
@@ -27,7 +27,7 @@
 ):
     block = pl.program_id(0)
     row_ids = lax.broadcasted_iota(jnp.int32, (window, 1), 0)
-    pad = jnp.zeros((8, out_ref.shape[2]), jnp.float32)
+    pad = jnp.zeros((16, out_ref.shape[2]), jnp.float32)
 
     @pl.when(block == 0)
     def _():
@@ -35,9 +35,10 @@
         for m in range(micro):
             def fill(user, carry):
                 entry = (m * USERS + user) * 4
-                span = pl.ds(pl.multiple_of(user_ref[entry], 8), window + 8)
+                span = pl.ds(pl.multiple_of(user_ref[entry], 16), window + 16)
                 shift = user_ref[entry + 1]
-                rows = pltpu.roll(q_ref[m, span, :], (window + 8 - shift) % (window + 8), 0)
+                rows = q_ref[m, span, :].astype(jnp.float32)
+                rows = pltpu.roll(rows, (window + 16 - shift) % (window + 16), 0)
                 keep = (row_ids >= user_ref[entry + 2]) & (row_ids < user_ref[entry + 3])
                 user_q[pl.ds(pl.multiple_of(user * (micro * window) + m * window, window), window), :] = jnp.where(
                     keep, rows[:window], 0.0
@@ -107,7 +108,7 @@
         for m in range(micro):
             def place(user, carry):
                 entry = (m * USERS + user) * 4
-                span = pl.ds(pl.multiple_of(user_ref[entry], 8), window + 8)
+                span = pl.ds(pl.multiple_of(user_ref[entry], 16), window + 16)
                 first = pl.multiple_of(user * (micro * window) + m * window, window)
                 sums = jnp.concatenate([user_acc[pl.ds(first, window), :], pad])
                 out_ref[m, span, :] += pltpu.roll(sums, user_ref[entry + 1], 0)
@@ -227,7 +228,7 @@
 
     starts = jnp.cumsum(cand_count, axis=1) - cand_count
     offsets = jnp.minimum(starts, all_cands - window)
-    base_rows = jnp.minimum(offsets // 8 * 8, all_cands - window - 8)
+    base_rows = jnp.minimum(offsets // 16 * 16, all_cands - window - 16)
     shifts = offsets - base_rows
     lows = starts - offsets
     highs = lows + cand_count
@@ -256,7 +257,7 @@
         ),
         out_shape=jax.ShapeDtypeStruct((micro, all_cands, head_cols), jnp.float32),
         compiler_params=pltpu.CompilerParams(dimension_semantics=("arbitrary",)),
-    )(tile_user, tile_rank, hist_len, user_info, last_block, first_rows, queries_all.astype(jnp.float32), k_cache, v_cache)
+    )(tile_user, tile_rank, hist_len, user_info, last_block, first_rows, queries_all, k_cache, v_cache)
 
     reduced = reduce_over_hist(partial_value.reshape(micro, n_cand, n_hist, local_rows, head_cols))
     attended = spread_over_cand(reduced)

time: 82.4 us -> 80.9 us (0.982)
  Pallas kernels: 22.4 us -> 19.3 us
  starting transfers between devices: 17.7 us -> 20.2 us
    pallas_call x1, Pallas kernels: 22.4 us -> 19.3 us  [body(): pl.pallas_call(functools.partial(attend_kernel, window=window, heads_here...]
    ppermute x3, starting transfers between devices: 2.04 us -> 4.57 us  [reduce_over_hist(): total = total + lax.ppermute(send, 'hist', perm=perm).astype(jnp.float32)]
    convert_element_type x2 -> x0, local copies, waits for them, and re-layouts: 1.69 us -> none  [body(): queries_all.astype(jnp.float32)]
    convert_element_type x1 -> x0, other arithmetic: 1.42 us -> none  [body(): queries_all.astype(jnp.float32)]
    select_n x0 -> x1, other arithmetic: none -> 1.38 us  [gather_queries(): jnp.where(core == 0, jnp.stack([mine, theirs], axis=1), jnp.stack([theirs...]
    transpose x0 -> x1, local copies, waits for them, and re-layouts: none -> 1.1 us  [gather_queries(): jnp.transpose(both, (2, 1, 0, 3, 4))]
  transfers between devices with their start and end apart: 14 -> 14, of which waited for: 10 -> 11; matrix products, arithmetic and copies ran while one was open for 3% -> 3% of each run, Pallas kernels for 0% -> 0%
where the time goes in v7:
time: 80.9 us; the launch traced here: 79.7 us
  waiting for transfers between devices  25.1 us (31%)
  starting transfers between devices  20.2 us (25%)
  Pallas kernels  19.3 us (24%)
  matrix products  5.46 us (7%)
  other arithmetic  4.9 us (6%)
  local copies, waits for them, and re-layouts  4.55 us (6%)
    pallas_call x1, Pallas kernels, body(): pl.pallas_call(functools.partial(attend_kernel, window=window, heads_here...  19.3 us
    ppermute x3, waiting for transfers between devices, reduce_over_hist(): total = total + lax.ppermute(send, 'hist', perm=perm).astype(jnp.float32)  11.4 us
    ppermute x3, waiting for transfers between devices, gather_queries(): by_offset.append(lax.ppermute(sources, 'hist', perm=perm))  5.73 us
    ppermute x3, starting transfers between devices, gather_queries(): by_offset.append(lax.ppermute(sources, 'hist', perm=perm))  5.57 us
    ppermute x3, starting transfers between devices, gather_queries(): lax.ppermute(piece, 'cand', perm=[(i, (i + shift) % n_cand) for i in rang...  5.06 us
    ppermute x3, starting transfers between devices, reduce_over_hist(): total = total + lax.ppermute(send, 'hist', perm=perm).astype(jnp.float32)  4.57 us
    ppermute x3, starting transfers between devices, spread_over_cand(): lax.ppermute(piece, 'cand', perm=[(i, (i + shift) % n_cand) for i in rang...  4.5 us
    ppermute x3, waiting for transfers between devices, gather_queries(): lax.ppermute(piece, 'cand', perm=[(i, (i + shift) % n_cand) for i in rang...  4.21 us
  transfers between devices with their start and end apart: 14, of which 11 were waited for; matrix products, arithmetic and copies ran while one was open for 3% of the time, Pallas kernels for 0%

profile of v7, /device:TPU:0, one launch (start us, length us, event | category | flops | bytes accessed | tf_op | source)
XLA Modules:
  0.0 79.7 jit_solution(3860264363959628606)
XLA Ops:
  0.0 0.0 copy-start
  0.0 2.3 %multiply_convert_fusion.2 = bf16[64,1024]{1,0:T(8,128)(2,1)S(1)} fusion(bf16[64,1024]{1,0:T(8,128)(2,1)} %bitcast.106, bf16[1024,2048]{1,0:T(8,128)(2,1)} %param.10), kind=kOutput, calls=%fused_computation.24 | convolution fusion | flops 134545408 | bytes 2359296 | tf_op jit(solution)/shard_map/dot_general | solution.py:219
  2.3 0.0 copy-start.1
  2.3 0.1 reshape_reshape.6
  2.4 0.3 constant_dynamic-slice_fusion.15
  2.7 3.0 %collective-permute-start.1 = (bf16[2,32,256]{2,1,0:T(8,128)(2,1)S(1)}, bf16[2,32,256]{2,1,0:T(8,128)(2,1)S(1)}, u32[]{:S(2)}, u32[]{:S(2)}) collective-permute-start(bf16[2,32,256]{2,1,0:T(8,128)(2,1)S(1)} %bitcast.99), channel_id=1, source_target_pairs={{0,16},{8,24},{16,0},{24,8},{1,17},{9,25},{17,1},{25,9},{2,18},{10... | collective-permute-start | bytes 98312 | tf_op jit(solution)/shard_map/ppermute | solution.py:155
  5.8 1.4 %collective-permute-start.2 = (bf16[2,32,256]{2,1,0:T(8,128)(2,1)S(1)}, bf16[2,32,256]{2,1,0:T(8,128)(2,1)S(1)}, u32[]{:S(2)}, u32[]{:S(2)}) collective-permute-start(bf16[2,32,256]{2,1,0:T(8,128)(2,1)S(1)} %bitcast.100), channel_id=1, source_target_pairs={{0,24},{8,0},{16,8},{24,16},{1,25},{9,1},{17,9},{25,17},{2,26},{10... | collective-permute-start | bytes 98312 | tf_op jit(solution)/shard_map/ppermute | solution.py:155
  7.2 0.6 collective-permute-start
  7.8 0.0 collective-permute-done.1
  7.8 1.9 %collective-permute-done.2 = bf16[2,32,256]{2,1,0:T(8,128)(2,1)S(1)} collective-permute-done((bf16[2,32,256]{2,1,0:T(8,128)(2,1)S(1)}, bf16[2,32,256]{2,1,0:T(8,128)(2,1)S(1)}, u32[]{:S(2)}, u32[]{:S(2)}) %collective-permute-start.2) | collective-permute-done | bytes 32800 | tf_op jit(solution)/shard_map/ppermute | solution.py:155
  9.7 2.3 %collective-permute-done = bf16[2,32,256]{2,1,0:T(8,128)(2,1)S(1)} collective-permute-done((bf16[2,32,256]{2,1,0:T(8,128)(2,1)S(1)}, bf16[2,32,256]{2,1,0:T(8,128)(2,1)S(1)}, u32[]{:S(2)}, u32[]{:S(2)}) %collective-permute-start) | collective-permute-done | bytes 32800 | tf_op jit(solution)/shard_map/ppermute | solution.py:155
  12.1 0.0 copy-start.2
  12.1 1.6 %collective-permute-start.3 = (bf16[4,2,32,256]{3,2,1,0:T(8,128)(2,1)S(1)}, bf16[4,2,32,256]{3,2,1,0:T(8,128)(2,1)S(1)}, u32[]{:S(2)}, u32[]{:S(2)}) collective-permute-start(bf16[4,2,32,256]{3,2,1,0:T(8,128)(2,1)S(1)} %get-tuple-element.35), channel_id=1, source_target_pairs={{0,2},{1,3},{2,4},{3,5},{4,6},{5,7},{6,0},{7,1},{8,10},{9,11},{10,... | collective-permute-start | bytes 393224 | tf_op jit(solution)/shard_map/ppermute | solution.py:172
  13.8 2.6 %collective-permute-start.4 = (bf16[4,2,32,256]{3,2,1,0:T(8,128)(2,1)S(1)}, bf16[4,2,32,256]{3,2,1,0:T(8,128)(2,1)S(1)}, u32[]{:S(2)}, u32[]{:S(2)}) collective-permute-start(bf16[4,2,32,256]{3,2,1,0:T(8,128)(2,1)S(1)} %get-tuple-element.35), channel_id=1, source_target_pairs={{0,4},{1,5},{2,6},{3,7},{4,0},{5,1},{6,2},{7,3},{8,12},{9,13},{10,... | collective-permute-start | bytes 393224 | tf_op jit(solution)/shard_map/ppermute | solution.py:172
  16.4 1.3 %collective-permute-start.5 = (bf16[4,2,32,256]{3,2,1,0:T(8,128)(2,1)S(1)}, bf16[4,2,32,256]{3,2,1,0:T(8,128)(2,1)S(1)}, u32[]{:S(2)}, u32[]{:S(2)}) collective-permute-start(bf16[4,2,32,256]{3,2,1,0:T(8,128)(2,1)S(1)} %get-tuple-element.35), channel_id=1, source_target_pairs={{0,6},{1,7},{2,0},{3,1},{4,2},{5,3},{6,4},{7,5},{8,14},{9,15},{10,... | collective-permute-start | bytes 393224 | tf_op jit(solution)/shard_map/ppermute | solution.py:172
  17.7 0.0 copy-done.1
  17.7 0.2 reduce_window_sum.11
  17.9 2.6 %collective-permute-done.3 = bf16[4,2,32,256]{3,2,1,0:T(8,128)(2,1)S(1)} collective-permute-done((bf16[4,2,32,256]{3,2,1,0:T(8,128)(2,1)S(1)}, bf16[4,2,32,256]{3,2,1,0:T(8,128)(2,1)S(1)}, u32[]{:S(2)}, u32[]{:S(2)}) %collective-permute-start.3) | collective-permute-done | bytes 131104 | tf_op jit(solution)/shard_map/ppermute | solution.py:172
  20.5 3.1 %collective-permute-done.4 = bf16[4,2,32,256]{3,2,1,0:T(8,128)(2,1)S(1)} collective-permute-done((bf16[4,2,32,256]{3,2,1,0:T(8,128)(2,1)S(1)}, bf16[4,2,32,256]{3,2,1,0:T(8,128)(2,1)S(1)}, u32[]{:S(2)}, u32[]{:S(2)}) %collective-permute-start.4) | collective-permute-done | bytes 131104 | tf_op jit(solution)/shard_map/ppermute | solution.py:172
  23.6 0.0 collective-permute-done.5
  23.6 0.1 pad_maximum_fusion
  23.7 0.1 fusion.28
  23.8 0.1 collective-permute-start.6
  24.0 0.1 copy.23
  24.1 0.6 reshape.59.user_ref
  24.7 0.0 copy-done.2
  24.7 1.1 %minimum_multiply_fusion = (s32[128]{0:T(128)}, s32[]{:T(128)}) fusion(s32[128]{0:T(128)S(1)} %copy-done.2), kind=kLoop, calls=%fused_computation.75 | loop fusion | flops 1663 | bytes 1028 | tf_op jit(solution)/shard_map/mul | solution.py:239
  25.8 0.1 collective-permute-done.6
  26.0 1.4 %maximum_select_fusion = bf16[4,2,4,2,32,256]{5,4,3,2,0,1:T(8,128)(2,1)S(1)} fusion(bf16[4,1,4,2,32,256]{5,4,3,2,0,1:T(8,128)(2,1)} %bitcast.18, bf16[4,1,4,2,32,256]{5,4,3,2,0,1:T(8,128)(2,1)S(1)} %get-tuple-element.18, pred[]{:T(512)S(6)} %eq.29), kind=kLoop, calls=%fused_computation.6 | loop fusion | flops 1572864 | bytes 2097153 | tf_op jit(solution)/shard_map/jit(_where)/select_n | solution.py:181
  27.3 0.1 copy.28
  27.5 1.1 %copy.29 = bf16[2,4,8,32,256]{4,3,2,1,0:T(8,128)(2,1)} copy(bf16[2,4,8,32,256]{4,3,0,1,2:T(8,128)(2,1)S(1)} %bitcast.82) | data formatting | bytes 2097152 | tf_op jit(solution)/shard_map/transpose | solution.py:183
  28.6 19.3 %shard_map.91 = f32[2,1024,256]{2,1,0:T(8,128)} custom-call(s32[128]{0:T(128)} %owner_ref.1, s32[128]{0:T(128)} %rank_ref.1, s32[16]{0:T(128)} %len_ref.1, s32[128]{0:T(128)} %reshape.59.user_ref, s32[1]{0:T(128)} %bitcast.4.last_ref, s32[128]{0:T(128)} %get-tuple-element.46.row_ref, bf16[2,1024,256]{2,1,0:T(8,128)(2,1)} %bitcast.83, ...), custom_call_target="tpu_custom_call" | custom-call | tf_op jit(solution)/shard_map/pallas_call | solution.py:246
  47.9 1.3 %fusion.5 = bf16[2,4,4,32,256]{4,3,2,1,0:T(8,128)(2,1)S(1)} fusion(f32[2,4,4,2,32,256]{5,4,3,2,1,0:T(8,128)} %bitcast.80, s32[]{:T(128)S(6)} %select_n.204), kind=kLoop, calls=%fused_computation.9 | loop fusion | bytes 1048580 | tf_op jit(solution)/shard_map/convert_element_type | solution.py:129
  49.2 0.4 collective-permute-start.7
  49.6 1.7 %collective-permute-done.7 = bf16[2,4,4,32,256]{4,3,2,1,0:T(8,128)(2,1)} collective-permute-done((bf16[2,4,4,32,256]{4,3,2,1,0:T(8,128)(2,1)S(1)}, bf16[2,4,4,32,256]{4,3,2,1,0:T(8,128)(2,1)}, u32[]{:S(2)}, u32[]{:S(2)}) %collective-permute-start.7) | collective-permute-done | bytes 524320 | tf_op jit(solution)/shard_map/ppermute | solution.py:128
  51.3 1.5 %bitcast_add_fusion = f32[2,4,4,32,256]{4,3,2,1,0:T(8,128)S(1)} fusion(bf16[2,4,4,32,256]{4,3,2,1,0:T(8,128)(2,1)} %collective-permute-done.7, f32[2,4,4,2,32,256]{5,4,3,2,1,0:T(8,128)} %bitcast.81, s32[]{:T(128)S(6)} %select_n.203), kind=kLoop, calls=%fused_computation.7 | loop fusion | flops 524288 | bytes 2621444 | tf_op jit(solution)/shard_map/add | solution.py:131
  52.9 0.8 fusion.18
  53.6 4.0 %collective-permute-start.10 = (bf16[2,4,32,256]{3,2,1,0:T(8,128)(2,1)}, bf16[2,4,32,256]{3,2,1,0:T(8,128)(2,1)S(1)}, u32[]{:S(2)}, u32[]{:S(2)}) collective-permute-start(bf16[2,4,32,256]{3,2,1,0:T(8,128)(2,1)} %get-tuple-element.16), channel_id=1, source_target_pairs={{0,6},{1,7},{2,0},{3,1},{4,2},{5,3},{6,4},{7,5},{8,14},{9,15},{10,... | collective-permute-start | bytes 393224 | tf_op jit(solution)/shard_map/ppermute | solution.py:141
  57.6 0.0 collective-permute-start.8
  57.6 0.6 collective-permute-start.9
  58.2 3.7 %collective-permute-done.10 = bf16[2,4,32,256]{3,2,1,0:T(8,128)(2,1)S(1)} collective-permute-done((bf16[2,4,32,256]{3,2,1,0:T(8,128)(2,1)}, bf16[2,4,32,256]{3,2,1,0:T(8,128)(2,1)S(1)}, u32[]{:S(2)}, u32[]{:S(2)}) %collective-permute-start.10) | collective-permute-done | bytes 131104 | tf_op jit(solution)/shard_map/ppermute | solution.py:141
  61.8 4.2 %collective-permute-done.8 = bf16[2,4,32,256]{3,2,1,0:T(8,128)(2,1)S(1)} collective-permute-done((bf16[2,4,32,256]{3,2,1,0:T(8,128)(2,1)}, bf16[2,4,32,256]{3,2,1,0:T(8,128)(2,1)S(1)}, u32[]{:S(2)}, u32[]{:S(2)}) %collective-permute-start.8) | collective-permute-done | bytes 131104 | tf_op jit(solution)/shard_map/ppermute | solution.py:141
  66.1 3.5 %collective-permute-done.9 = bf16[2,4,32,256]{3,2,1,0:T(8,128)(2,1)S(1)} collective-permute-done((bf16[2,4,32,256]{3,2,1,0:T(8,128)(2,1)}, bf16[2,4,32,256]{3,2,1,0:T(8,128)(2,1)S(1)}, u32[]{:S(2)}, u32[]{:S(2)}) %collective-permute-start.9) | collective-permute-done | bytes 131104 | tf_op jit(solution)/shard_map/ppermute | solution.py:141
  69.6 0.1 fusion.7
  69.7 0.4 collective-permute-start.11
  70.1 1.3 %collective-permute-start.12 = (f32[2,32,256]{2,1,0:T(8,128)S(1)}, f32[2,32,256]{2,1,0:T(8,128)S(1)}, u32[]{:S(2)}, u32[]{:S(2)}) collective-permute-start(f32[2,32,256]{2,1,0:T(8,128)S(1)} %get-tuple-element.32), channel_id=1, source_target_pairs={{0,16},{8,24},{16,0},{24,8},{1,17},{9,25},{17,1},{25,9},{2,18},{10... | collective-permute-start | bytes 196616 | tf_op jit(solution)/shard_map/ppermute | solution.py:193
  71.4 2.8 %collective-permute-start.13 = (f32[2,32,256]{2,1,0:T(8,128)S(1)}, f32[2,32,256]{2,1,0:T(8,128)S(1)}, u32[]{:S(2)}, u32[]{:S(2)}) collective-permute-start(f32[2,32,256]{2,1,0:T(8,128)S(1)} %get-tuple-element.31), channel_id=1, source_target_pairs={{0,24},{8,0},{16,8},{24,16},{1,25},{9,1},{17,9},{25,17},{2,26},{10... | collective-permute-start | bytes 196616 | tf_op jit(solution)/shard_map/ppermute | solution.py:193
  74.2 0.9 %collective-permute-done.11 = f32[2,32,256]{2,1,0:T(8,128)S(1)} collective-permute-done((f32[2,32,256]{2,1,0:T(8,128)S(1)}, f32[2,32,256]{2,1,0:T(8,128)S(1)}, u32[]{:S(2)}, u32[]{:S(2)}) %collective-permute-start.11) | collective-permute-done | bytes 65568 | tf_op jit(solution)/shard_map/ppermute | solution.py:193
  75.1 0.0 collective-permute-done.12
  75.1 1.0 %collective-permute-done.13 = f32[2,32,256]{2,1,0:T(8,128)S(1)} collective-permute-done((f32[2,32,256]{2,1,0:T(8,128)S(1)}, f32[2,32,256]{2,1,0:T(8,128)S(1)}, u32[]{:S(2)}, u32[]{:S(2)}) %collective-permute-start.13) | collective-permute-done | bytes 65568 | tf_op jit(solution)/shard_map/ppermute | solution.py:193
  76.1 0.1 fusion.30
  76.3 0.1 div.55
  76.4 0.2 multiply_reduce_fusion
  76.6 0.0 copy-done
  76.6 3.1 %fusion.4 = bf16[64,1024]{1,0:T(8,128)(2,1)} fusion(bf16[1024,1024]{1,0:T(8,128)(2,1)S(1)} %copy-done, bf16[64,1024]{1,0:T(8,128)(2,1)} %bitcast.107, bf16[1024,2048]{1,0:T(8,128)(2,1)} %param.10, f32[64,256]{1,0:T(8,128)S(1)} %bitcast.87, f32[64,256]{1,0:T(8,128)S(1)} %bitcast.89, f32[64,256]{1,0:T(8,128)S(1)} %bitcast.91, f32[64,256]{1,0:T(8,128)S(1)} %bitcast.85, ...), kind=kOutput, calls=%fused_computation.5 | convolution fusion | flops 269484032 | bytes 4850176 | tf_op jit(solution)/shard_map/dot_general | solution.py:270
  (14 shorter events, 0.2 us)
Async XLA Ops:
  0.0 76.6 %copy-start = (bf16[1024,1024]{1,0:T(8,128)(2,1)S(1)}, bf16[1024,1024]{1,0:T(8,128)(2,1)}, u32[]{:S(2)}) copy-start(bf16[1024,1024]{1,0:T(8,128)(2,1)} %param.11) | copy-start | bytes 6291460
  2.3 15.4 %copy-start.1 = (s32[2,16]{1,0:T(2,128)S(1)}, s32[2,16]{1,0:T(2,128)}, u32[]{:S(2)}) copy-start(s32[2,16]{1,0:T(2,128)} %param.15) | copy-start | bytes 388
  2.7 5.1 %collective-permute-start.1 = (bf16[2,32,256]{2,1,0:T(8,128)(2,1)S(1)}, bf16[2,32,256]{2,1,0:T(8,128)(2,1)S(1)}, u32[]{:S(2)}, u32[]{:S(2)}) collective-permute-start(bf16[2,32,256]{2,1,0:T(8,128)(2,1)S(1)} %bitcast.99), channel_id=1, source_target_pairs={{0,16},{8,24},{16,0},{24,8},{1,17},{9,25},{17,1},{25,9},{2,18},{10... | collective-permute-start | bytes 98312 | tf_op jit(solution)/shard_map/ppermute | solution.py:155
  5.8 3.9 %collective-permute-start.2 = (bf16[2,32,256]{2,1,0:T(8,128)(2,1)S(1)}, bf16[2,32,256]{2,1,0:T(8,128)(2,1)S(1)}, u32[]{:S(2)}, u32[]{:S(2)}) collective-permute-start(bf16[2,32,256]{2,1,0:T(8,128)(2,1)S(1)} %bitcast.100), channel_id=1, source_target_pairs={{0,24},{8,0},{16,8},{24,16},{1,25},{9,1},{17,9},{25,17},{2,26},{10... | collective-permute-start | bytes 98312 | tf_op jit(solution)/shard_map/ppermute | solution.py:155
  7.2 4.8 %collective-permute-start = (bf16[2,32,256]{2,1,0:T(8,128)(2,1)S(1)}, bf16[2,32,256]{2,1,0:T(8,128)(2,1)S(1)}, u32[]{:S(2)}, u32[]{:S(2)}) collective-permute-start(bf16[2,32,256]{2,1,0:T(8,128)(2,1)S(1)} %bitcast.101), channel_id=1, source_target_pairs={{0,8},{8,16},{16,24},{24,0},{1,9},{9,17},{17,25},{25,1},{2,10},{10... | collective-permute-start | bytes 98312 | tf_op jit(solution)/shard_map/ppermute | solution.py:155
  12.1 12.6 %copy-start.2 = (s32[128]{0:T(128)S(1)}, s32[128]{0:T(128)}, u32[]{:S(2)}) copy-start(s32[128]{0:T(128)} %owner_ref.1) | copy-start | bytes 1540
  12.1 8.3 %collective-permute-start.3 = (bf16[4,2,32,256]{3,2,1,0:T(8,128)(2,1)S(1)}, bf16[4,2,32,256]{3,2,1,0:T(8,128)(2,1)S(1)}, u32[]{:S(2)}, u32[]{:S(2)}) collective-permute-start(bf16[4,2,32,256]{3,2,1,0:T(8,128)(2,1)S(1)} %get-tuple-element.35), channel_id=1, source_target_pairs={{0,2},{1,3},{2,4},{3,5},{4,6},{5,7},{6,0},{7,1},{8,10},{9,11},{10,... | collective-permute-start | bytes 393224 | tf_op jit(solution)/shard_map/ppermute | solution.py:172
  13.8 9.9 %collective-permute-start.4 = (bf16[4,2,32,256]{3,2,1,0:T(8,128)(2,1)S(1)}, bf16[4,2,32,256]{3,2,1,0:T(8,128)(2,1)S(1)}, u32[]{:S(2)}, u32[]{:S(2)}) collective-permute-start(bf16[4,2,32,256]{3,2,1,0:T(8,128)(2,1)S(1)} %get-tuple-element.35), channel_id=1, source_target_pairs={{0,4},{1,5},{2,6},{3,7},{4,0},{5,1},{6,2},{7,3},{8,12},{9,13},{10,... | collective-permute-start | bytes 393224 | tf_op jit(solution)/shard_map/ppermute | solution.py:172
  16.4 7.3 %collective-permute-start.5 = (bf16[4,2,32,256]{3,2,1,0:T(8,128)(2,1)S(1)}, bf16[4,2,32,256]{3,2,1,0:T(8,128)(2,1)S(1)}, u32[]{:S(2)}, u32[]{:S(2)}) collective-permute-start(bf16[4,2,32,256]{3,2,1,0:T(8,128)(2,1)S(1)} %get-tuple-element.35), channel_id=1, source_target_pairs={{0,6},{1,7},{2,0},{3,1},{4,2},{5,3},{6,4},{7,5},{8,14},{9,15},{10,... | collective-permute-start | bytes 393224 | tf_op jit(solution)/shard_map/ppermute | solution.py:172
  23.8 2.1 %collective-permute-start.6 = (bf16[4,4,2,32,256]{4,3,2,1,0:T(8,128)(2,1)S(1)}, bf16[4,4,2,32,256]{4,3,2,1,0:T(8,128)(2,1)}, u32[]{:S(2)}, u32[]{:S(2)}) collective-permute-start(bf16[4,4,2,32,256]{4,3,2,1,0:T(8,128)(2,1)S(1)} %get-tuple-element.19), channel_id=1, source_target_pairs={{0,1},{1,0},{2,3},{3,2},{4,5},{5,4},{6,7},{7,6},{8,9},{9,8},{10,11... | collective-permute-start | bytes 1572872 | tf_op jit(solution)/shard_map/ppermute | solution.py:180
  49.2 2.1 %collective-permute-start.7 = (bf16[2,4,4,32,256]{4,3,2,1,0:T(8,128)(2,1)S(1)}, bf16[2,4,4,32,256]{4,3,2,1,0:T(8,128)(2,1)}, u32[]{:S(2)}, u32[]{:S(2)}) collective-permute-start(bf16[2,4,4,32,256]{4,3,2,1,0:T(8,128)(2,1)S(1)} %fusion.5), channel_id=1, source_target_pairs={{0,1},{1,0},{2,3},{3,2},{4,5},{5,4},{6,7},{7,6},{8,9},{9,8},{10,11... | collective-permute-start | bytes 1572872 | tf_op jit(solution)/shard_map/ppermute | solution.py:128
  53.6 8.2 %collective-permute-start.10 = (bf16[2,4,32,256]{3,2,1,0:T(8,128)(2,1)}, bf16[2,4,32,256]{3,2,1,0:T(8,128)(2,1)S(1)}, u32[]{:S(2)}, u32[]{:S(2)}) collective-permute-start(bf16[2,4,32,256]{3,2,1,0:T(8,128)(2,1)} %get-tuple-element.16), channel_id=1, source_target_pairs={{0,6},{1,7},{2,0},{3,1},{4,2},{5,3},{6,4},{7,5},{8,14},{9,15},{10,... | collective-permute-start | bytes 393224 | tf_op jit(solution)/shard_map/ppermute | solution.py:141
  57.6 8.4 %collective-permute-start.8 = (bf16[2,4,32,256]{3,2,1,0:T(8,128)(2,1)}, bf16[2,4,32,256]{3,2,1,0:T(8,128)(2,1)S(1)}, u32[]{:S(2)}, u32[]{:S(2)}) collective-permute-start(bf16[2,4,32,256]{3,2,1,0:T(8,128)(2,1)} %get-tuple-element.15), channel_id=1, source_target_pairs={{0,2},{1,3},{2,4},{3,5},{4,6},{5,7},{6,0},{7,1},{8,10},{9,11},{10,... | collective-permute-start | bytes 393224 | tf_op jit(solution)/shard_map/ppermute | solution.py:141
  57.6 12.0 %collective-permute-start.9 = (bf16[2,4,32,256]{3,2,1,0:T(8,128)(2,1)}, bf16[2,4,32,256]{3,2,1,0:T(8,128)(2,1)S(1)}, u32[]{:S(2)}, u32[]{:S(2)}) collective-permute-start(bf16[2,4,32,256]{3,2,1,0:T(8,128)(2,1)} %get-tuple-element.17), channel_id=1, source_target_pairs={{0,4},{1,5},{2,6},{3,7},{4,0},{5,1},{6,2},{7,3},{8,12},{9,13},{10,... | collective-permute-start | bytes 393224 | tf_op jit(solution)/shard_map/ppermute | solution.py:141
  69.7 5.4 %collective-permute-start.11 = (f32[2,32,256]{2,1,0:T(8,128)S(1)}, f32[2,32,256]{2,1,0:T(8,128)S(1)}, u32[]{:S(2)}, u32[]{:S(2)}) collective-permute-start(f32[2,32,256]{2,1,0:T(8,128)S(1)} %get-tuple-element.33), channel_id=1, source_target_pairs={{0,8},{8,16},{16,24},{24,0},{1,9},{9,17},{17,25},{25,1},{2,10},{10... | collective-permute-start | bytes 196616 | tf_op jit(solution)/shard_map/ppermute | solution.py:193
  70.1 5.0 %collective-permute-start.12 = (f32[2,32,256]{2,1,0:T(8,128)S(1)}, f32[2,32,256]{2,1,0:T(8,128)S(1)}, u32[]{:S(2)}, u32[]{:S(2)}) collective-permute-start(f32[2,32,256]{2,1,0:T(8,128)S(1)} %get-tuple-element.32), channel_id=1, source_target_pairs={{0,16},{8,24},{16,0},{24,8},{1,17},{9,25},{17,1},{25,9},{2,18},{10... | collective-permute-start | bytes 196616 | tf_op jit(solution)/shard_map/ppermute | solution.py:193
  71.4 4.8 %collective-permute-start.13 = (f32[2,32,256]{2,1,0:T(8,128)S(1)}, f32[2,32,256]{2,1,0:T(8,128)S(1)}, u32[]{:S(2)}, u32[]{:S(2)}) collective-permute-start(f32[2,32,256]{2,1,0:T(8,128)S(1)} %get-tuple-element.31), channel_id=1, source_target_pairs={{0,24},{8,0},{16,8},{24,16},{1,25},{9,1},{17,9},{25,17},{2,26},{10... | collective-permute-start | bytes 196616 | tf_op jit(solution)/shard_map/ppermute | solution.py:193

commit v8 on v7

--- a/solution.py
+++ b/solution.py
@@ -22,16 +22,31 @@
 
 
 def attend_kernel(
-    owner_ref, rank_ref, len_ref, user_ref, last_ref, row_ref,
-    q_ref, k_ref, v_ref, out_ref, user_q, user_acc, *, window, heads_here, micro,
+    owner_ref, rank_ref, len_ref, count_ref,
+    q_ref, k_ref, v_ref, out_ref, user_q, user_acc, user_ref, *, window, heads_here, micro,
 ):
     block = pl.program_id(0)
+    all_cands = q_ref.shape[1]
     row_ids = lax.broadcasted_iota(jnp.int32, (window, 1), 0)
     pad = jnp.zeros((16, out_ref.shape[2]), jnp.float32)
 
     @pl.when(block == 0)
     def _():
         user_acc[...] = jnp.zeros_like(user_acc)
+        for m in range(micro):
+            def scan(user, start):
+                count = count_ref[m * USERS + user]
+                offset = jnp.minimum(start, all_cands - window)
+                base_row = jnp.minimum(offset // 16 * 16, all_cands - window - 16)
+                entry = (m * USERS + user) * 4
+                user_ref[entry] = base_row
+                user_ref[entry + 1] = offset - base_row
+                user_ref[entry + 2] = start - offset
+                user_ref[entry + 3] = start - offset + count
+                return start + count
+
+            lax.fori_loop(0, USERS, scan, jnp.int32(0))
+
         for m in range(micro):
             def fill(user, carry):
                 entry = (m * USERS + user) * 4
@@ -59,7 +74,8 @@
             rows = slice(j * TILE, (j + 1) * TILE)
             keys = jnp.where(key_ids < klen, k_ref[rows, :], 0)
             values = v_ref[rows, :]
-            user_rows = pl.ds(pl.multiple_of(row_ref[slot], micro * window), micro * window)
+            first_row = jnp.minimum(user, USERS - 1) * (micro * window)
+            user_rows = pl.ds(pl.multiple_of(first_row, micro * window), micro * window)
             queries = user_q[user_rows, :]
             if heads_here == 2:
                 lanes = lax.broadcasted_iota(jnp.int32, (1, 2 * HEAD_DIM), 1)
@@ -97,7 +113,11 @@
                 user_acc[user_rows, :] += jnp.concatenate(parts, axis=1) if heads_here > 1 else parts[0]
 
 
-    @pl.when(block <= last_ref[0])
+    occupied = owner_ref[block * BLOCK_TILES]
+    for j in range(1, BLOCK_TILES):
+        occupied = jnp.minimum(occupied, owner_ref[block * BLOCK_TILES + j])
+
+    @pl.when(occupied < USERS)
     def _():
         for j in range(BLOCK_TILES):
             one_tile(j)
@@ -226,38 +246,28 @@
     all_cands = queries_all.shape[1]
     window = 2 * all_cands // USERS
 
-    starts = jnp.cumsum(cand_count, axis=1) - cand_count
-    offsets = jnp.minimum(starts, all_cands - window)
-    base_rows = jnp.minimum(offsets // 16 * 16, all_cands - window - 16)
-    shifts = offsets - base_rows
-    lows = starts - offsets
-    highs = lows + cand_count
-    user_info = jnp.stack([base_rows, shifts, lows, highs], axis=2).astype(jnp.int32).reshape(-1)
-    block_ids = jnp.arange(tiles_here, dtype=jnp.int32) // BLOCK_TILES
-    last_block = jnp.max(jnp.where(tile_user < USERS, block_ids, 0)).reshape(1).astype(jnp.int32)
-
-    first_rows = (jnp.minimum(tile_user, USERS - 1) * (micro * window)).astype(jnp.int32)
     rows_per_block = BLOCK_TILES * TILE
     n_blocks = tiles_here // BLOCK_TILES
     whole = pl.BlockSpec((micro, all_cands, head_cols), lambda b, *_: (0, 0, 0))
     tiles = pl.BlockSpec(
-        (rows_per_block, head_cols), lambda b, *_: (jnp.minimum(b, _[4][0]), 0)
+        (rows_per_block, head_cols), lambda b, *_: (b, 0)
     )
     partial_value = pl.pallas_call(
         functools.partial(attend_kernel, window=window, heads_here=heads_here, micro=micro),
         grid_spec=pltpu.PrefetchScalarGridSpec(
-            num_scalar_prefetch=6,
+            num_scalar_prefetch=4,
             grid=(n_blocks,),
             in_specs=[whole, tiles, tiles],
             out_specs=whole,
             scratch_shapes=[
                 pltpu.VMEM((USERS * micro * window, head_cols), jnp.bfloat16),
                 pltpu.VMEM((USERS * micro * window, head_cols), jnp.float32),
+                pltpu.SMEM((micro * USERS * 4,), jnp.int32),
             ],
         ),
         out_shape=jax.ShapeDtypeStruct((micro, all_cands, head_cols), jnp.float32),
         compiler_params=pltpu.CompilerParams(dimension_semantics=("arbitrary",)),
-    )(tile_user, tile_rank, hist_len, user_info, last_block, first_rows, queries_all, k_cache, v_cache)
+    )(tile_user, tile_rank, hist_len, cand_count.reshape(-1), queries_all, k_cache, v_cache)
 
     reduced = reduce_over_hist(partial_value.reshape(micro, n_cand, n_hist, local_rows, head_cols))
     attended = spread_over_cand(reduced)

time: 80.9 us -> 82.2 us (1.016); the launches traced: 79.7 us -> 83.3 us
  starting transfers between devices: 20.2 us -> 24.3 us
  waiting for transfers between devices: 25.1 us -> 27.1 us
  other arithmetic: 4.9 us -> 3.52 us
  Pallas kernels: 19.3 us -> 18.2 us
    ppermute x3, starting transfers between devices: 4.57 us -> 10.3 us  [reduce_over_hist(): total = total + lax.ppermute(send, 'hist', perm=perm).astype(jnp.float32)]
    ppermute x3, waiting for transfers between devices: 1.9 us -> 3.72 us  [spread_over_cand(): lax.ppermute(piece, 'cand', perm=[(i, (i + shift) % n_cand) for i in rang...]
    ppermute x3, waiting for transfers between devices: 4.21 us -> 2.47 us  [gather_queries(): lax.ppermute(piece, 'cand', perm=[(i, (i + shift) % n_cand) for i in rang...]
    ppermute x3, starting transfers between devices: 4.5 us -> 3.19 us  [spread_over_cand(): lax.ppermute(piece, 'cand', perm=[(i, (i + shift) % n_cand) for i in rang...]
    ppermute x1, waiting for transfers between devices: 0.13 us -> 1.41 us  [gather_queries(): lax.ppermute(mine, 'hist', perm=[(i, i ^ 1) for i in range(n_hist)])]
    ppermute x3, waiting for transfers between devices: 5.73 us -> 6.93 us  [gather_queries(): by_offset.append(lax.ppermute(sources, 'hist', perm=perm))]
    pallas_call x1, Pallas kernels: 19.3 us -> 18.2 us  [body(): pl.pallas_call(functools.partial(attend_kernel, window=window, heads_here...]
    mul x1 -> x0, other arithmetic: 1.15 us -> none  [body(): jnp.minimum(tile_user, USERS - 1) * (micro * window)]
  transfers between devices with their start and end apart: 14 -> 14, of which waited for: 11 -> 11; matrix products, arithmetic and copies ran while one was open for 3% -> 1% of each run, Pallas kernels for 0% -> 0%
where the time goes in v8:
time: 82.2 us; the launch traced here: 83.3 us
  waiting for transfers between devices  27.1 us (33%)
  starting transfers between devices  24.3 us (30%)
  Pallas kernels  18.2 us (22%)
  matrix products  5.45 us (7%)
  local copies, waits for them, and re-layouts  4.41 us (5%)
  other arithmetic  3.52 us (4%)
    pallas_call x1, Pallas kernels, body(): pl.pallas_call(functools.partial(attend_kernel, window=window, heads_here...  18.2 us
    ppermute x3, waiting for transfers between devices, reduce_over_hist(): total = total + lax.ppermute(send, 'hist', perm=perm).astype(jnp.float32)  10.6 us
    ppermute x3, starting transfers between devices, reduce_over_hist(): total = total + lax.ppermute(send, 'hist', perm=perm).astype(jnp.float32)  10.3 us
    ppermute x3, waiting for transfers between devices, gather_queries(): by_offset.append(lax.ppermute(sources, 'hist', perm=perm))  6.93 us
    ppermute x3, starting transfers between devices, gather_queries(): lax.ppermute(piece, 'cand', perm=[(i, (i + shift) % n_cand) for i in rang...  5.94 us
    ppermute x3, starting transfers between devices, gather_queries(): by_offset.append(lax.ppermute(sources, 'hist', perm=perm))  4.68 us
    ppermute x3, waiting for transfers between devices, spread_over_cand(): lax.ppermute(piece, 'cand', perm=[(i, (i + shift) % n_cand) for i in rang...  3.72 us
    ppermute x3, starting transfers between devices, spread_over_cand(): lax.ppermute(piece, 'cand', perm=[(i, (i + shift) % n_cand) for i in rang...  3.19 us
  transfers between devices with their start and end apart: 14, of which 11 were waited for; matrix products, arithmetic and copies ran while one was open for 1% of the time, Pallas kernels for 0%

profile of v8, /device:TPU:0, one launch (start us, length us, event | category | flops | bytes accessed | tf_op | source)
XLA Modules:
  0.0 83.3 jit_solution(5023781870471771609)
XLA Ops:
  0.0 0.0 copy-start
  0.0 2.3 %multiply_convert_fusion.2 = bf16[64,1024]{1,0:T(8,128)(2,1)S(1)} fusion(bf16[64,1024]{1,0:T(8,128)(2,1)} %bitcast.97, bf16[1024,2048]{1,0:T(8,128)(2,1)} %param.10), kind=kOutput, calls=%fused_computation.24 | convolution fusion | flops 134545408 | bytes 2359296 | tf_op jit(solution)/shard_map/dot_general | solution.py:239
  2.3 0.1 reshape_reshape.6
  2.4 0.3 constant_dynamic-slice_fusion.15
  2.7 3.0 %collective-permute-start = (bf16[2,32,256]{2,1,0:T(8,128)(2,1)S(1)}, bf16[2,32,256]{2,1,0:T(8,128)(2,1)S(1)}, u32[]{:S(2)}, u32[]{:S(2)}) collective-permute-start(bf16[2,32,256]{2,1,0:T(8,128)(2,1)S(1)} %bitcast.91), channel_id=1, source_target_pairs={{0,8},{8,16},{16,24},{24,0},{1,9},{9,17},{17,25},{25,1},{2,10},{10... | collective-permute-start | bytes 98312 | tf_op jit(solution)/shard_map/ppermute | solution.py:175
  5.7 1.5 %collective-permute-start.1 = (bf16[2,32,256]{2,1,0:T(8,128)(2,1)S(1)}, bf16[2,32,256]{2,1,0:T(8,128)(2,1)S(1)}, u32[]{:S(2)}, u32[]{:S(2)}) collective-permute-start(bf16[2,32,256]{2,1,0:T(8,128)(2,1)S(1)} %bitcast.92), channel_id=1, source_target_pairs={{0,16},{8,24},{16,0},{24,8},{1,17},{9,25},{17,1},{25,9},{2,18},{10... | collective-permute-start | bytes 98312 | tf_op jit(solution)/shard_map/ppermute | solution.py:175
  7.3 1.4 %collective-permute-start.2 = (bf16[2,32,256]{2,1,0:T(8,128)(2,1)S(1)}, bf16[2,32,256]{2,1,0:T(8,128)(2,1)S(1)}, u32[]{:S(2)}, u32[]{:S(2)}) collective-permute-start(bf16[2,32,256]{2,1,0:T(8,128)(2,1)S(1)} %bitcast.93), channel_id=1, source_target_pairs={{0,24},{8,0},{16,8},{24,16},{1,25},{9,1},{17,9},{25,17},{2,26},{10... | collective-permute-start | bytes 98312 | tf_op jit(solution)/shard_map/ppermute | solution.py:175
  8.7 0.0 collective-permute-done
  8.7 0.9 %collective-permute-done.1 = bf16[2,32,256]{2,1,0:T(8,128)(2,1)S(1)} collective-permute-done((bf16[2,32,256]{2,1,0:T(8,128)(2,1)S(1)}, bf16[2,32,256]{2,1,0:T(8,128)(2,1)S(1)}, u32[]{:S(2)}, u32[]{:S(2)}) %collective-permute-start.1) | collective-permute-done | bytes 32800 | tf_op jit(solution)/shard_map/ppermute | solution.py:175
  9.6 1.5 %collective-permute-done.2 = bf16[2,32,256]{2,1,0:T(8,128)(2,1)S(1)} collective-permute-done((bf16[2,32,256]{2,1,0:T(8,128)(2,1)S(1)}, bf16[2,32,256]{2,1,0:T(8,128)(2,1)S(1)}, u32[]{:S(2)}, u32[]{:S(2)}) %collective-permute-start.2) | collective-permute-done | bytes 32800 | tf_op jit(solution)/shard_map/ppermute | solution.py:175
  11.2 0.0 copy-start.1
  11.3 2.7 %collective-permute-start.4 = (bf16[4,2,32,256]{3,2,1,0:T(8,128)(2,1)S(1)}, bf16[4,2,32,256]{3,2,1,0:T(8,128)(2,1)S(1)}, u32[]{:S(2)}, u32[]{:S(2)}) collective-permute-start(bf16[4,2,32,256]{3,2,1,0:T(8,128)(2,1)S(1)} %get-tuple-element.33), channel_id=1, source_target_pairs={{0,4},{1,5},{2,6},{3,7},{4,0},{5,1},{6,2},{7,3},{8,12},{9,13},{10,... | collective-permute-start | bytes 393224 | tf_op jit(solution)/shard_map/ppermute | solution.py:192
  13.9 1.3 %collective-permute-start.5 = (bf16[4,2,32,256]{3,2,1,0:T(8,128)(2,1)S(1)}, bf16[4,2,32,256]{3,2,1,0:T(8,128)(2,1)S(1)}, u32[]{:S(2)}, u32[]{:S(2)}) collective-permute-start(bf16[4,2,32,256]{3,2,1,0:T(8,128)(2,1)S(1)} %get-tuple-element.33), channel_id=1, source_target_pairs={{0,6},{1,7},{2,0},{3,1},{4,2},{5,3},{6,4},{7,5},{8,14},{9,15},{10,... | collective-permute-start | bytes 393224 | tf_op jit(solution)/shard_map/ppermute | solution.py:192
  15.3 0.7 collective-permute-start.3
  15.9 6.9 %collective-permute-done.4 = bf16[4,2,32,256]{3,2,1,0:T(8,128)(2,1)S(1)} collective-permute-done((bf16[4,2,32,256]{3,2,1,0:T(8,128)(2,1)S(1)}, bf16[4,2,32,256]{3,2,1,0:T(8,128)(2,1)S(1)}, u32[]{:S(2)}, u32[]{:S(2)}) %collective-permute-start.4) | collective-permute-done | bytes 131104 | tf_op jit(solution)/shard_map/ppermute | solution.py:192
  22.9 0.0 collective-permute-done.5
  22.9 0.0 collective-permute-done.3
  22.9 0.1 pad_maximum_fusion
  23.0 0.1 fusion.26
  23.1 0.1 collective-permute-start.6
  23.2 0.0 copy-done.1
  23.2 0.6 reshape.56.count_ref
  23.8 1.4 %collective-permute-done.6 = bf16[4,4,2,32,256]{4,3,2,1,0:T(8,128)(2,1)} collective-permute-done((bf16[4,4,2,32,256]{4,3,2,1,0:T(8,128)(2,1)S(1)}, bf16[4,4,2,32,256]{4,3,2,1,0:T(8,128)(2,1)}, u32[]{:S(2)}, u32[]{:S(2)}) %collective-permute-start.6) | collective-permute-done | bytes 524320 | tf_op jit(solution)/shard_map/ppermute | solution.py:200
  25.2 1.4 %maximum_select_fusion = bf16[4,2,4,2,32,256]{5,4,3,2,0,1:T(8,128)(2,1)S(1)} fusion(bf16[4,1,4,2,32,256]{5,4,3,2,0,1:T(8,128)(2,1)} %bitcast.13, bf16[4,1,4,2,32,256]{5,4,3,2,0,1:T(8,128)(2,1)S(1)} %get-tuple-element.16, pred[]{:T(512)S(6)} %eq.29), kind=kLoop, calls=%fused_computation.6 | loop fusion | flops 1572864 | bytes 2097153 | tf_op jit(solution)/shard_map/jit(_where)/select_n | solution.py:201
  26.6 0.1 copy.25
  26.7 1.1 %copy.26 = bf16[2,4,8,32,256]{4,3,2,1,0:T(8,128)(2,1)} copy(bf16[2,4,8,32,256]{4,3,0,1,2:T(8,128)(2,1)S(1)} %bitcast.75) | data formatting | bytes 2097152 | tf_op jit(solution)/shard_map/transpose | solution.py:203
  27.8 18.2 %shard_map.91 = f32[2,1024,256]{2,1,0:T(8,128)} custom-call(s32[128]{0:T(128)} %owner_ref.1, s32[128]{0:T(128)} %rank_ref.1, s32[16]{0:T(128)} %len_ref.1, s32[32]{0:T(128)} %reshape.56.count_ref, bf16[2,1024,256]{2,1,0:T(8,128)(2,1)} %bitcast.74, bf16[16384,256]{1,0:T(8,128)(2,1)} %k_ref.1, bf16[16384,256]{1,0:T(8,128)(2,1)} %v_ref.1), custom_call_target="tpu_custom_call" | custom-call | tf_op jit(solution)/shard_map/pallas_call | solution.py:255
  46.0 1.3 %fusion.5 = bf16[2,4,4,32,256]{4,3,2,1,0:T(8,128)(2,1)S(1)} fusion(f32[2,4,4,2,32,256]{5,4,3,2,1,0:T(8,128)} %bitcast.72, s32[]{:T(128)S(6)} %select_n.187), kind=kLoop, calls=%fused_computation.9 | loop fusion | bytes 1048580 | tf_op jit(solution)/shard_map/convert_element_type | solution.py:149
  47.3 0.1 collective-permute-start.7
  47.4 2.0 %collective-permute-done.7 = bf16[2,4,4,32,256]{4,3,2,1,0:T(8,128)(2,1)} collective-permute-done((bf16[2,4,4,32,256]{4,3,2,1,0:T(8,128)(2,1)S(1)}, bf16[2,4,4,32,256]{4,3,2,1,0:T(8,128)(2,1)}, u32[]{:S(2)}, u32[]{:S(2)}) %collective-permute-start.7) | collective-permute-done | bytes 524320 | tf_op jit(solution)/shard_map/ppermute | solution.py:148
  49.4 1.5 %bitcast_add_fusion = f32[2,4,4,32,256]{4,3,2,1,0:T(8,128)S(1)} fusion(bf16[2,4,4,32,256]{4,3,2,1,0:T(8,128)(2,1)} %collective-permute-done.7, f32[2,4,4,2,32,256]{5,4,3,2,1,0:T(8,128)} %bitcast.73, s32[]{:T(128)S(6)} %select_n.186), kind=kLoop, calls=%fused_computation.7 | loop fusion | flops 524288 | bytes 2621444 | tf_op jit(solution)/shard_map/add | solution.py:151
  50.9 0.8 fusion.18
  51.7 7.0 %collective-permute-start.10 = (bf16[2,4,32,256]{3,2,1,0:T(8,128)(2,1)}, bf16[2,4,32,256]{3,2,1,0:T(8,128)(2,1)S(1)}, u32[]{:S(2)}, u32[]{:S(2)}) collective-permute-start(bf16[2,4,32,256]{3,2,1,0:T(8,128)(2,1)} %get-tuple-element.14), channel_id=1, source_target_pairs={{0,6},{1,7},{2,0},{3,1},{4,2},{5,3},{6,4},{7,5},{8,14},{9,15},{10,... | collective-permute-start | bytes 393224 | tf_op jit(solution)/shard_map/ppermute | solution.py:161
  58.6 0.0 collective-permute-start.8
  58.6 3.4 %collective-permute-start.9 = (bf16[2,4,32,256]{3,2,1,0:T(8,128)(2,1)}, bf16[2,4,32,256]{3,2,1,0:T(8,128)(2,1)S(1)}, u32[]{:S(2)}, u32[]{:S(2)}) collective-permute-start(bf16[2,4,32,256]{3,2,1,0:T(8,128)(2,1)} %get-tuple-element.15), channel_id=1, source_target_pairs={{0,4},{1,5},{2,6},{3,7},{4,0},{5,1},{6,2},{7,3},{8,12},{9,13},{10,... | collective-permute-start | bytes 393224 | tf_op jit(solution)/shard_map/ppermute | solution.py:161
  62.0 0.8 collective-permute-done.10
  62.8 6.1 %collective-permute-done.8 = bf16[2,4,32,256]{3,2,1,0:T(8,128)(2,1)S(1)} collective-permute-done((bf16[2,4,32,256]{3,2,1,0:T(8,128)(2,1)}, bf16[2,4,32,256]{3,2,1,0:T(8,128)(2,1)S(1)}, u32[]{:S(2)}, u32[]{:S(2)}) %collective-permute-start.8) | collective-permute-done | bytes 131104 | tf_op jit(solution)/shard_map/ppermute | solution.py:161
  68.9 3.8 %collective-permute-done.9 = bf16[2,4,32,256]{3,2,1,0:T(8,128)(2,1)S(1)} collective-permute-done((bf16[2,4,32,256]{3,2,1,0:T(8,128)(2,1)}, bf16[2,4,32,256]{3,2,1,0:T(8,128)(2,1)S(1)}, u32[]{:S(2)}, u32[]{:S(2)}) %collective-permute-start.9) | collective-permute-done | bytes 131104 | tf_op jit(solution)/shard_map/ppermute | solution.py:161
  72.6 0.1 fusion.7
  72.7 1.2 %collective-permute-start.11 = (f32[2,32,256]{2,1,0:T(8,128)S(1)}, f32[2,32,256]{2,1,0:T(8,128)S(1)}, u32[]{:S(2)}, u32[]{:S(2)}) collective-permute-start(f32[2,32,256]{2,1,0:T(8,128)S(1)} %get-tuple-element.31), channel_id=1, source_target_pairs={{0,8},{8,16},{16,24},{24,0},{1,9},{9,17},{17,25},{25,1},{2,10},{10... | collective-permute-start | bytes 196616 | tf_op jit(solution)/shard_map/ppermute | solution.py:213
  74.0 1.4 %collective-permute-start.12 = (f32[2,32,256]{2,1,0:T(8,128)S(1)}, f32[2,32,256]{2,1,0:T(8,128)S(1)}, u32[]{:S(2)}, u32[]{:S(2)}) collective-permute-start(f32[2,32,256]{2,1,0:T(8,128)S(1)} %get-tuple-element.30), channel_id=1, source_target_pairs={{0,16},{8,24},{16,0},{24,8},{1,17},{9,25},{17,1},{25,9},{2,18},{10... | collective-permute-start | bytes 196616 | tf_op jit(solution)/shard_map/ppermute | solution.py:213
  75.4 0.5 collective-permute-start.13
  75.9 2.7 %collective-permute-done.11 = f32[2,32,256]{2,1,0:T(8,128)S(1)} collective-permute-done((f32[2,32,256]{2,1,0:T(8,128)S(1)}, f32[2,32,256]{2,1,0:T(8,128)S(1)}, u32[]{:S(2)}, u32[]{:S(2)}) %collective-permute-start.11) | collective-permute-done | bytes 65568 | tf_op jit(solution)/shard_map/ppermute | solution.py:213
  78.6 0.3 collective-permute-done.12
  78.9 0.8 collective-permute-done.13
  79.7 0.1 fusion.28
  79.8 0.1 div.29
  79.9 0.2 multiply_reduce_fusion
  80.1 0.0 copy-done
  80.1 3.1 %fusion.4 = bf16[64,1024]{1,0:T(8,128)(2,1)} fusion(bf16[1024,1024]{1,0:T(8,128)(2,1)S(1)} %copy-done, bf16[64,1024]{1,0:T(8,128)(2,1)} %bitcast.98, bf16[1024,2048]{1,0:T(8,128)(2,1)} %param.10, f32[64,256]{1,0:T(8,128)S(1)} %bitcast.79, f32[64,256]{1,0:T(8,128)S(1)} %bitcast.81, f32[64,256]{1,0:T(8,128)S(1)} %bitcast.83, f32[64,256]{1,0:T(8,128)S(1)} %bitcast.77, ...), kind=kOutput, calls=%fused_computation.5 | convolution fusion | flops 269484032 | bytes 4850176 | tf_op jit(solution)/shard_map/dot_general | solution.py:280
  (12 shorter events, 0.2 us)
Async XLA Ops:
  0.0 80.1 %copy-start = (bf16[1024,1024]{1,0:T(8,128)(2,1)S(1)}, bf16[1024,1024]{1,0:T(8,128)(2,1)}, u32[]{:S(2)}) copy-start(bf16[1024,1024]{1,0:T(8,128)(2,1)} %param.11) | copy-start | bytes 6291460
  2.7 6.0 %collective-permute-start = (bf16[2,32,256]{2,1,0:T(8,128)(2,1)S(1)}, bf16[2,32,256]{2,1,0:T(8,128)(2,1)S(1)}, u32[]{:S(2)}, u32[]{:S(2)}) collective-permute-start(bf16[2,32,256]{2,1,0:T(8,128)(2,1)S(1)} %bitcast.91), channel_id=1, source_target_pairs={{0,8},{8,16},{16,24},{24,0},{1,9},{9,17},{17,25},{25,1},{2,10},{10... | collective-permute-start | bytes 98312 | tf_op jit(solution)/shard_map/ppermute | solution.py:175
  5.7 3.9 %collective-permute-start.1 = (bf16[2,32,256]{2,1,0:T(8,128)(2,1)S(1)}, bf16[2,32,256]{2,1,0:T(8,128)(2,1)S(1)}, u32[]{:S(2)}, u32[]{:S(2)}) collective-permute-start(bf16[2,32,256]{2,1,0:T(8,128)(2,1)S(1)} %bitcast.92), channel_id=1, source_target_pairs={{0,16},{8,24},{16,0},{24,8},{1,17},{9,25},{17,1},{25,9},{2,18},{10... | collective-permute-start | bytes 98312 | tf_op jit(solution)/shard_map/ppermute | solution.py:175
  7.3 3.9 %collective-permute-start.2 = (bf16[2,32,256]{2,1,0:T(8,128)(2,1)S(1)}, bf16[2,32,256]{2,1,0:T(8,128)(2,1)S(1)}, u32[]{:S(2)}, u32[]{:S(2)}) collective-permute-start(bf16[2,32,256]{2,1,0:T(8,128)(2,1)S(1)} %bitcast.93), channel_id=1, source_target_pairs={{0,24},{8,0},{16,8},{24,16},{1,25},{9,1},{17,9},{25,17},{2,26},{10... | collective-permute-start | bytes 98312 | tf_op jit(solution)/shard_map/ppermute | solution.py:175
  11.2 12.0 %copy-start.1 = (s32[2,16]{1,0:T(2,128)S(1)}, s32[2,16]{1,0:T(2,128)}, u32[]{:S(2)}) copy-start(s32[2,16]{1,0:T(2,128)} %param.15) | copy-start | bytes 388
  11.3 11.6 %collective-permute-start.4 = (bf16[4,2,32,256]{3,2,1,0:T(8,128)(2,1)S(1)}, bf16[4,2,32,256]{3,2,1,0:T(8,128)(2,1)S(1)}, u32[]{:S(2)}, u32[]{:S(2)}) collective-permute-start(bf16[4,2,32,256]{3,2,1,0:T(8,128)(2,1)S(1)} %get-tuple-element.33), channel_id=1, source_target_pairs={{0,4},{1,5},{2,6},{3,7},{4,0},{5,1},{6,2},{7,3},{8,12},{9,13},{10,... | collective-permute-start | bytes 393224 | tf_op jit(solution)/shard_map/ppermute | solution.py:192
  13.9 9.0 %collective-permute-start.5 = (bf16[4,2,32,256]{3,2,1,0:T(8,128)(2,1)S(1)}, bf16[4,2,32,256]{3,2,1,0:T(8,128)(2,1)S(1)}, u32[]{:S(2)}, u32[]{:S(2)}) collective-permute-start(bf16[4,2,32,256]{3,2,1,0:T(8,128)(2,1)S(1)} %get-tuple-element.33), channel_id=1, source_target_pairs={{0,6},{1,7},{2,0},{3,1},{4,2},{5,3},{6,4},{7,5},{8,14},{9,15},{10,... | collective-permute-start | bytes 393224 | tf_op jit(solution)/shard_map/ppermute | solution.py:192
  15.3 7.6 %collective-permute-start.3 = (bf16[4,2,32,256]{3,2,1,0:T(8,128)(2,1)S(1)}, bf16[4,2,32,256]{3,2,1,0:T(8,128)(2,1)S(1)}, u32[]{:S(2)}, u32[]{:S(2)}) collective-permute-start(bf16[4,2,32,256]{3,2,1,0:T(8,128)(2,1)S(1)} %get-tuple-element.33), channel_id=1, source_target_pairs={{0,2},{1,3},{2,4},{3,5},{4,6},{5,7},{6,0},{7,1},{8,10},{9,11},{10,... | collective-permute-start | bytes 393224 | tf_op jit(solution)/shard_map/ppermute | solution.py:192
  23.1 2.1 %collective-permute-start.6 = (bf16[4,4,2,32,256]{4,3,2,1,0:T(8,128)(2,1)S(1)}, bf16[4,4,2,32,256]{4,3,2,1,0:T(8,128)(2,1)}, u32[]{:S(2)}, u32[]{:S(2)}) collective-permute-start(bf16[4,4,2,32,256]{4,3,2,1,0:T(8,128)(2,1)S(1)} %get-tuple-element.17), channel_id=1, source_target_pairs={{0,1},{1,0},{2,3},{3,2},{4,5},{5,4},{6,7},{7,6},{8,9},{9,8},{10,11... | collective-permute-start | bytes 1572872 | tf_op jit(solution)/shard_map/ppermute | solution.py:200
  47.3 2.1 %collective-permute-start.7 = (bf16[2,4,4,32,256]{4,3,2,1,0:T(8,128)(2,1)S(1)}, bf16[2,4,4,32,256]{4,3,2,1,0:T(8,128)(2,1)}, u32[]{:S(2)}, u32[]{:S(2)}) collective-permute-start(bf16[2,4,4,32,256]{4,3,2,1,0:T(8,128)(2,1)S(1)} %fusion.5), channel_id=1, source_target_pairs={{0,1},{1,0},{2,3},{3,2},{4,5},{5,4},{6,7},{7,6},{8,9},{9,8},{10,11... | collective-permute-start | bytes 1572872 | tf_op jit(solution)/shard_map/ppermute | solution.py:148
  51.7 11.1 %collective-permute-start.10 = (bf16[2,4,32,256]{3,2,1,0:T(8,128)(2,1)}, bf16[2,4,32,256]{3,2,1,0:T(8,128)(2,1)S(1)}, u32[]{:S(2)}, u32[]{:S(2)}) collective-permute-start(bf16[2,4,32,256]{3,2,1,0:T(8,128)(2,1)} %get-tuple-element.14), channel_id=1, source_target_pairs={{0,6},{1,7},{2,0},{3,1},{4,2},{5,3},{6,4},{7,5},{8,14},{9,15},{10,... | collective-permute-start | bytes 393224 | tf_op jit(solution)/shard_map/ppermute | solution.py:161
  58.6 10.2 %collective-permute-start.8 = (bf16[2,4,32,256]{3,2,1,0:T(8,128)(2,1)}, bf16[2,4,32,256]{3,2,1,0:T(8,128)(2,1)S(1)}, u32[]{:S(2)}, u32[]{:S(2)}) collective-permute-start(bf16[2,4,32,256]{3,2,1,0:T(8,128)(2,1)} %get-tuple-element.13), channel_id=1, source_target_pairs={{0,2},{1,3},{2,4},{3,5},{4,6},{5,7},{6,0},{7,1},{8,10},{9,11},{10,... | collective-permute-start | bytes 393224 | tf_op jit(solution)/shard_map/ppermute | solution.py:161
  58.6 14.0 %collective-permute-start.9 = (bf16[2,4,32,256]{3,2,1,0:T(8,128)(2,1)}, bf16[2,4,32,256]{3,2,1,0:T(8,128)(2,1)S(1)}, u32[]{:S(2)}, u32[]{:S(2)}) collective-permute-start(bf16[2,4,32,256]{3,2,1,0:T(8,128)(2,1)} %get-tuple-element.15), channel_id=1, source_target_pairs={{0,4},{1,5},{2,6},{3,7},{4,0},{5,1},{6,2},{7,3},{8,12},{9,13},{10,... | collective-permute-start | bytes 393224 | tf_op jit(solution)/shard_map/ppermute | solution.py:161
  72.7 5.9 %collective-permute-start.11 = (f32[2,32,256]{2,1,0:T(8,128)S(1)}, f32[2,32,256]{2,1,0:T(8,128)S(1)}, u32[]{:S(2)}, u32[]{:S(2)}) collective-permute-start(f32[2,32,256]{2,1,0:T(8,128)S(1)} %get-tuple-element.31), channel_id=1, source_target_pairs={{0,8},{8,16},{16,24},{24,0},{1,9},{9,17},{17,25},{25,1},{2,10},{10... | collective-permute-start | bytes 196616 | tf_op jit(solution)/shard_map/ppermute | solution.py:213
  74.0 4.9 %collective-permute-start.12 = (f32[2,32,256]{2,1,0:T(8,128)S(1)}, f32[2,32,256]{2,1,0:T(8,128)S(1)}, u32[]{:S(2)}, u32[]{:S(2)}) collective-permute-start(f32[2,32,256]{2,1,0:T(8,128)S(1)} %get-tuple-element.30), channel_id=1, source_target_pairs={{0,16},{8,24},{16,0},{24,8},{1,17},{9,25},{17,1},{25,9},{2,18},{10... | collective-permute-start | bytes 196616 | tf_op jit(solution)/shard_map/ppermute | solution.py:213
  75.4 4.3 %collective-permute-start.13 = (f32[2,32,256]{2,1,0:T(8,128)S(1)}, f32[2,32,256]{2,1,0:T(8,128)S(1)}, u32[]{:S(2)}, u32[]{:S(2)}) collective-permute-start(f32[2,32,256]{2,1,0:T(8,128)S(1)} %get-tuple-element.29), channel_id=1, source_target_pairs={{0,24},{8,0},{16,8},{24,16},{1,25},{9,1},{17,9},{25,17},{2,26},{10... | collective-permute-start | bytes 196616 | tf_op jit(solution)/shard_map/ppermute | solution.py:213

commit v9 on v8

--- a/solution.py
+++ b/solution.py
@@ -11,7 +11,7 @@
 TILE = 128
 USERS = 16
 MICRO = 2
-BLOCK_TILES = 16
+BLOCK_TILES = 32
 
 
 EPSILON = 1e-06

time: 82.2 us -> 81.6 us (level); the launches traced: 83.3 us -> 81.3 us
  starting transfers between devices: 24.3 us -> 21.2 us
  waiting for transfers between devices: 27.1 us -> 28.6 us
    ppermute x3, starting transfers between devices: 10.3 us -> 7.15 us  [reduce_over_hist(): total = total + lax.ppermute(send, 'hist', perm=perm).astype(jnp.float32)]
    ppermute x3, waiting for transfers between devices: 10.6 us -> 12.1 us  [reduce_over_hist(): total = total + lax.ppermute(send, 'hist', perm=perm).astype(jnp.float32)]
where the time goes in v9:
time: 81.6 us; the launch traced here: 81.3 us
  waiting for transfers between devices  28.6 us (35%)
  starting transfers between devices  21.2 us (26%)
  Pallas kernels  17.9 us (22%)
  matrix products  5.46 us (7%)
  local copies, waits for them, and re-layouts  4.41 us (5%)
  other arithmetic  3.52 us (4%)
    pallas_call x1, Pallas kernels, body(): pl.pallas_call(functools.partial(attend_kernel, window=window, heads_here...  17.9 us
    ppermute x3, waiting for transfers between devices, reduce_over_hist(): total = total + lax.ppermute(send, 'hist', perm=perm).astype(jnp.float32)  12.1 us
    ppermute x3, starting transfers between devices, reduce_over_hist(): total = total + lax.ppermute(send, 'hist', perm=perm).astype(jnp.float32)  7.15 us
    ppermute x3, waiting for transfers between devices, gather_queries(): by_offset.append(lax.ppermute(sources, 'hist', perm=perm))  6.93 us
    ppermute x3, starting transfers between devices, gather_queries(): lax.ppermute(piece, 'cand', perm=[(i, (i + shift) % n_cand) for i in rang...  5.94 us
    ppermute x3, starting transfers between devices, gather_queries(): by_offset.append(lax.ppermute(sources, 'hist', perm=perm))  4.68 us
    ppermute x3, waiting for transfers between devices, spread_over_cand(): lax.ppermute(piece, 'cand', perm=[(i, (i + shift) % n_cand) for i in rang...  3.72 us
    ppermute x3, starting transfers between devices, spread_over_cand(): lax.ppermute(piece, 'cand', perm=[(i, (i + shift) % n_cand) for i in rang...  3.19 us
  transfers between devices with their start and end apart: 14, of which 11 were waited for; matrix products, arithmetic and copies ran while one was open for 1% of the time, Pallas kernels for 0%

profile of v9, /device:TPU:0, one launch (start us, length us, event | category | flops | bytes accessed | tf_op | source)
XLA Modules:
  0.0 81.3 jit_solution(9540008622074485654)
XLA Ops:
  0.0 0.0 copy-start
  0.0 2.3 %multiply_convert_fusion.2 = bf16[64,1024]{1,0:T(8,128)(2,1)S(1)} fusion(bf16[64,1024]{1,0:T(8,128)(2,1)} %bitcast.97, bf16[1024,2048]{1,0:T(8,128)(2,1)} %param.10), kind=kOutput, calls=%fused_computation.24 | convolution fusion | flops 134545408 | bytes 2359296 | tf_op jit(solution)/shard_map/dot_general | solution.py:239
  2.3 0.1 reshape_reshape.6
  2.4 0.3 constant_dynamic-slice_fusion.15
  2.7 3.0 %collective-permute-start = (bf16[2,32,256]{2,1,0:T(8,128)(2,1)S(1)}, bf16[2,32,256]{2,1,0:T(8,128)(2,1)S(1)}, u32[]{:S(2)}, u32[]{:S(2)}) collective-permute-start(bf16[2,32,256]{2,1,0:T(8,128)(2,1)S(1)} %bitcast.91), channel_id=1, source_target_pairs={{0,8},{8,16},{16,24},{24,0},{1,9},{9,17},{17,25},{25,1},{2,10},{10... | collective-permute-start | bytes 98312 | tf_op jit(solution)/shard_map/ppermute | solution.py:175
  5.7 1.5 %collective-permute-start.1 = (bf16[2,32,256]{2,1,0:T(8,128)(2,1)S(1)}, bf16[2,32,256]{2,1,0:T(8,128)(2,1)S(1)}, u32[]{:S(2)}, u32[]{:S(2)}) collective-permute-start(bf16[2,32,256]{2,1,0:T(8,128)(2,1)S(1)} %bitcast.92), channel_id=1, source_target_pairs={{0,16},{8,24},{16,0},{24,8},{1,17},{9,25},{17,1},{25,9},{2,18},{10... | collective-permute-start | bytes 98312 | tf_op jit(solution)/shard_map/ppermute | solution.py:175
  7.3 1.4 %collective-permute-start.2 = (bf16[2,32,256]{2,1,0:T(8,128)(2,1)S(1)}, bf16[2,32,256]{2,1,0:T(8,128)(2,1)S(1)}, u32[]{:S(2)}, u32[]{:S(2)}) collective-permute-start(bf16[2,32,256]{2,1,0:T(8,128)(2,1)S(1)} %bitcast.93), channel_id=1, source_target_pairs={{0,24},{8,0},{16,8},{24,16},{1,25},{9,1},{17,9},{25,17},{2,26},{10... | collective-permute-start | bytes 98312 | tf_op jit(solution)/shard_map/ppermute | solution.py:175
  8.7 0.0 collective-permute-done
  8.7 0.9 %collective-permute-done.1 = bf16[2,32,256]{2,1,0:T(8,128)(2,1)S(1)} collective-permute-done((bf16[2,32,256]{2,1,0:T(8,128)(2,1)S(1)}, bf16[2,32,256]{2,1,0:T(8,128)(2,1)S(1)}, u32[]{:S(2)}, u32[]{:S(2)}) %collective-permute-start.1) | collective-permute-done | bytes 32800 | tf_op jit(solution)/shard_map/ppermute | solution.py:175
  9.6 1.5 %collective-permute-done.2 = bf16[2,32,256]{2,1,0:T(8,128)(2,1)S(1)} collective-permute-done((bf16[2,32,256]{2,1,0:T(8,128)(2,1)S(1)}, bf16[2,32,256]{2,1,0:T(8,128)(2,1)S(1)}, u32[]{:S(2)}, u32[]{:S(2)}) %collective-permute-start.2) | collective-permute-done | bytes 32800 | tf_op jit(solution)/shard_map/ppermute | solution.py:175
  11.2 0.0 copy-start.1
  11.3 2.7 %collective-permute-start.4 = (bf16[4,2,32,256]{3,2,1,0:T(8,128)(2,1)S(1)}, bf16[4,2,32,256]{3,2,1,0:T(8,128)(2,1)S(1)}, u32[]{:S(2)}, u32[]{:S(2)}) collective-permute-start(bf16[4,2,32,256]{3,2,1,0:T(8,128)(2,1)S(1)} %get-tuple-element.33), channel_id=1, source_target_pairs={{0,4},{1,5},{2,6},{3,7},{4,0},{5,1},{6,2},{7,3},{8,12},{9,13},{10,... | collective-permute-start | bytes 393224 | tf_op jit(solution)/shard_map/ppermute | solution.py:192
  13.9 1.3 %collective-permute-start.5 = (bf16[4,2,32,256]{3,2,1,0:T(8,128)(2,1)S(1)}, bf16[4,2,32,256]{3,2,1,0:T(8,128)(2,1)S(1)}, u32[]{:S(2)}, u32[]{:S(2)}) collective-permute-start(bf16[4,2,32,256]{3,2,1,0:T(8,128)(2,1)S(1)} %get-tuple-element.33), channel_id=1, source_target_pairs={{0,6},{1,7},{2,0},{3,1},{4,2},{5,3},{6,4},{7,5},{8,14},{9,15},{10,... | collective-permute-start | bytes 393224 | tf_op jit(solution)/shard_map/ppermute | solution.py:192
  15.3 0.7 collective-permute-start.3
  15.9 6.9 %collective-permute-done.4 = bf16[4,2,32,256]{3,2,1,0:T(8,128)(2,1)S(1)} collective-permute-done((bf16[4,2,32,256]{3,2,1,0:T(8,128)(2,1)S(1)}, bf16[4,2,32,256]{3,2,1,0:T(8,128)(2,1)S(1)}, u32[]{:S(2)}, u32[]{:S(2)}) %collective-permute-start.4) | collective-permute-done | bytes 131104 | tf_op jit(solution)/shard_map/ppermute | solution.py:192
  22.9 0.0 collective-permute-done.5
  22.9 0.0 collective-permute-done.3
  22.9 0.1 pad_maximum_fusion
  23.0 0.1 fusion.26
  23.1 0.1 collective-permute-start.6
  23.2 0.0 copy-done.1
  23.2 0.6 reshape.56.count_ref
  23.8 1.4 %collective-permute-done.6 = bf16[4,4,2,32,256]{4,3,2,1,0:T(8,128)(2,1)} collective-permute-done((bf16[4,4,2,32,256]{4,3,2,1,0:T(8,128)(2,1)S(1)}, bf16[4,4,2,32,256]{4,3,2,1,0:T(8,128)(2,1)}, u32[]{:S(2)}, u32[]{:S(2)}) %collective-permute-start.6) | collective-permute-done | bytes 524320 | tf_op jit(solution)/shard_map/ppermute | solution.py:200
  25.2 1.4 %maximum_select_fusion = bf16[4,2,4,2,32,256]{5,4,3,2,0,1:T(8,128)(2,1)S(1)} fusion(bf16[4,1,4,2,32,256]{5,4,3,2,0,1:T(8,128)(2,1)} %bitcast.13, bf16[4,1,4,2,32,256]{5,4,3,2,0,1:T(8,128)(2,1)S(1)} %get-tuple-element.16, pred[]{:T(512)S(6)} %eq.29), kind=kLoop, calls=%fused_computation.6 | loop fusion | flops 1572864 | bytes 2097153 | tf_op jit(solution)/shard_map/jit(_where)/select_n | solution.py:201
  26.6 0.1 copy.25
  26.7 1.1 %copy.26 = bf16[2,4,8,32,256]{4,3,2,1,0:T(8,128)(2,1)} copy(bf16[2,4,8,32,256]{4,3,0,1,2:T(8,128)(2,1)S(1)} %bitcast.75) | data formatting | bytes 2097152 | tf_op jit(solution)/shard_map/transpose | solution.py:203
  27.8 17.9 %shard_map.91 = f32[2,1024,256]{2,1,0:T(8,128)} custom-call(s32[128]{0:T(128)} %owner_ref.1, s32[128]{0:T(128)} %rank_ref.1, s32[16]{0:T(128)} %len_ref.1, s32[32]{0:T(128)} %reshape.56.count_ref, bf16[2,1024,256]{2,1,0:T(8,128)(2,1)} %bitcast.74, bf16[16384,256]{1,0:T(8,128)(2,1)} %k_ref.1, bf16[16384,256]{1,0:T(8,128)(2,1)} %v_ref.1), custom_call_target="tpu_custom_call" | custom-call | tf_op jit(solution)/shard_map/pallas_call | solution.py:255
  45.7 1.3 %fusion.5 = bf16[2,4,4,32,256]{4,3,2,1,0:T(8,128)(2,1)S(1)} fusion(f32[2,4,4,2,32,256]{5,4,3,2,1,0:T(8,128)} %bitcast.72, s32[]{:T(128)S(6)} %select_n.187), kind=kLoop, calls=%fused_computation.9 | loop fusion | bytes 1048580 | tf_op jit(solution)/shard_map/convert_element_type | solution.py:149
  47.0 0.2 collective-permute-start.7
  47.2 1.9 %collective-permute-done.7 = bf16[2,4,4,32,256]{4,3,2,1,0:T(8,128)(2,1)} collective-permute-done((bf16[2,4,4,32,256]{4,3,2,1,0:T(8,128)(2,1)S(1)}, bf16[2,4,4,32,256]{4,3,2,1,0:T(8,128)(2,1)}, u32[]{:S(2)}, u32[]{:S(2)}) %collective-permute-start.7) | collective-permute-done | bytes 524320 | tf_op jit(solution)/shard_map/ppermute | solution.py:148
  49.1 1.5 %bitcast_add_fusion = f32[2,4,4,32,256]{4,3,2,1,0:T(8,128)S(1)} fusion(bf16[2,4,4,32,256]{4,3,2,1,0:T(8,128)(2,1)} %collective-permute-done.7, f32[2,4,4,2,32,256]{5,4,3,2,1,0:T(8,128)} %bitcast.73, s32[]{:T(128)S(6)} %select_n.186), kind=kLoop, calls=%fused_computation.7 | loop fusion | flops 524288 | bytes 2621444 | tf_op jit(solution)/shard_map/add | solution.py:151
  50.6 0.8 fusion.18
  51.4 6.0 %collective-permute-start.10 = (bf16[2,4,32,256]{3,2,1,0:T(8,128)(2,1)}, bf16[2,4,32,256]{3,2,1,0:T(8,128)(2,1)S(1)}, u32[]{:S(2)}, u32[]{:S(2)}) collective-permute-start(bf16[2,4,32,256]{3,2,1,0:T(8,128)(2,1)} %get-tuple-element.14), channel_id=1, source_target_pairs={{0,6},{1,7},{2,0},{3,1},{4,2},{5,3},{6,4},{7,5},{8,14},{9,15},{10,... | collective-permute-start | bytes 393224 | tf_op jit(solution)/shard_map/ppermute | solution.py:161
  57.4 0.0 collective-permute-start.8
  57.4 1.1 %collective-permute-start.9 = (bf16[2,4,32,256]{3,2,1,0:T(8,128)(2,1)}, bf16[2,4,32,256]{3,2,1,0:T(8,128)(2,1)S(1)}, u32[]{:S(2)}, u32[]{:S(2)}) collective-permute-start(bf16[2,4,32,256]{3,2,1,0:T(8,128)(2,1)} %get-tuple-element.15), channel_id=1, source_target_pairs={{0,4},{1,5},{2,6},{3,7},{4,0},{5,1},{6,2},{7,3},{8,12},{9,13},{10,... | collective-permute-start | bytes 393224 | tf_op jit(solution)/shard_map/ppermute | solution.py:161
  58.5 3.1 %collective-permute-done.10 = bf16[2,4,32,256]{3,2,1,0:T(8,128)(2,1)S(1)} collective-permute-done((bf16[2,4,32,256]{3,2,1,0:T(8,128)(2,1)}, bf16[2,4,32,256]{3,2,1,0:T(8,128)(2,1)S(1)}, u32[]{:S(2)}, u32[]{:S(2)}) %collective-permute-start.10) | collective-permute-done | bytes 131104 | tf_op jit(solution)/shard_map/ppermute | solution.py:161
  61.6 4.2 %collective-permute-done.8 = bf16[2,4,32,256]{3,2,1,0:T(8,128)(2,1)S(1)} collective-permute-done((bf16[2,4,32,256]{3,2,1,0:T(8,128)(2,1)}, bf16[2,4,32,256]{3,2,1,0:T(8,128)(2,1)S(1)}, u32[]{:S(2)}, u32[]{:S(2)}) %collective-permute-start.8) | collective-permute-done | bytes 131104 | tf_op jit(solution)/shard_map/ppermute | solution.py:161
  65.9 4.8 %collective-permute-done.9 = bf16[2,4,32,256]{3,2,1,0:T(8,128)(2,1)S(1)} collective-permute-done((bf16[2,4,32,256]{3,2,1,0:T(8,128)(2,1)}, bf16[2,4,32,256]{3,2,1,0:T(8,128)(2,1)S(1)}, u32[]{:S(2)}, u32[]{:S(2)}) %collective-permute-start.9) | collective-permute-done | bytes 131104 | tf_op jit(solution)/shard_map/ppermute | solution.py:161
  70.7 0.1 fusion.7
  70.8 1.2 %collective-permute-start.11 = (f32[2,32,256]{2,1,0:T(8,128)S(1)}, f32[2,32,256]{2,1,0:T(8,128)S(1)}, u32[]{:S(2)}, u32[]{:S(2)}) collective-permute-start(f32[2,32,256]{2,1,0:T(8,128)S(1)} %get-tuple-element.31), channel_id=1, source_target_pairs={{0,8},{8,16},{16,24},{24,0},{1,9},{9,17},{17,25},{25,1},{2,10},{10... | collective-permute-start | bytes 196616 | tf_op jit(solution)/shard_map/ppermute | solution.py:213
  72.0 1.4 %collective-permute-start.12 = (f32[2,32,256]{2,1,0:T(8,128)S(1)}, f32[2,32,256]{2,1,0:T(8,128)S(1)}, u32[]{:S(2)}, u32[]{:S(2)}) collective-permute-start(f32[2,32,256]{2,1,0:T(8,128)S(1)} %get-tuple-element.30), channel_id=1, source_target_pairs={{0,16},{8,24},{16,0},{24,8},{1,17},{9,25},{17,1},{25,9},{2,18},{10... | collective-permute-start | bytes 196616 | tf_op jit(solution)/shard_map/ppermute | solution.py:213
  73.4 0.5 collective-permute-start.13
  74.0 2.4 %collective-permute-done.11 = f32[2,32,256]{2,1,0:T(8,128)S(1)} collective-permute-done((f32[2,32,256]{2,1,0:T(8,128)S(1)}, f32[2,32,256]{2,1,0:T(8,128)S(1)}, u32[]{:S(2)}, u32[]{:S(2)}) %collective-permute-start.11) | collective-permute-done | bytes 65568 | tf_op jit(solution)/shard_map/ppermute | solution.py:213
  76.3 0.5 collective-permute-done.12
  76.8 0.9 %collective-permute-done.13 = f32[2,32,256]{2,1,0:T(8,128)S(1)} collective-permute-done((f32[2,32,256]{2,1,0:T(8,128)S(1)}, f32[2,32,256]{2,1,0:T(8,128)S(1)}, u32[]{:S(2)}, u32[]{:S(2)}) %collective-permute-start.13) | collective-permute-done | bytes 65568 | tf_op jit(solution)/shard_map/ppermute | solution.py:213
  77.7 0.1 fusion.28
  77.9 0.1 div.29
  78.0 0.2 multiply_reduce_fusion
  78.2 0.0 copy-done
  78.2 3.1 %fusion.4 = bf16[64,1024]{1,0:T(8,128)(2,1)} fusion(bf16[1024,1024]{1,0:T(8,128)(2,1)S(1)} %copy-done, bf16[64,1024]{1,0:T(8,128)(2,1)} %bitcast.98, bf16[1024,2048]{1,0:T(8,128)(2,1)} %param.10, f32[64,256]{1,0:T(8,128)S(1)} %bitcast.79, f32[64,256]{1,0:T(8,128)S(1)} %bitcast.81, f32[64,256]{1,0:T(8,128)S(1)} %bitcast.83, f32[64,256]{1,0:T(8,128)S(1)} %bitcast.77, ...), kind=kOutput, calls=%fused_computation.5 | convolution fusion | flops 269484032 | bytes 4850176 | tf_op jit(solution)/shard_map/dot_general | solution.py:280
  (12 shorter events, 0.2 us)
Async XLA Ops:
  0.0 78.2 %copy-start = (bf16[1024,1024]{1,0:T(8,128)(2,1)S(1)}, bf16[1024,1024]{1,0:T(8,128)(2,1)}, u32[]{:S(2)}) copy-start(bf16[1024,1024]{1,0:T(8,128)(2,1)} %param.11) | copy-start | bytes 6291460
  2.7 6.0 %collective-permute-start = (bf16[2,32,256]{2,1,0:T(8,128)(2,1)S(1)}, bf16[2,32,256]{2,1,0:T(8,128)(2,1)S(1)}, u32[]{:S(2)}, u32[]{:S(2)}) collective-permute-start(bf16[2,32,256]{2,1,0:T(8,128)(2,1)S(1)} %bitcast.91), channel_id=1, source_target_pairs={{0,8},{8,16},{16,24},{24,0},{1,9},{9,17},{17,25},{25,1},{2,10},{10... | collective-permute-start | bytes 98312 | tf_op jit(solution)/shard_map/ppermute | solution.py:175
  5.7 3.9 %collective-permute-start.1 = (bf16[2,32,256]{2,1,0:T(8,128)(2,1)S(1)}, bf16[2,32,256]{2,1,0:T(8,128)(2,1)S(1)}, u32[]{:S(2)}, u32[]{:S(2)}) collective-permute-start(bf16[2,32,256]{2,1,0:T(8,128)(2,1)S(1)} %bitcast.92), channel_id=1, source_target_pairs={{0,16},{8,24},{16,0},{24,8},{1,17},{9,25},{17,1},{25,9},{2,18},{10... | collective-permute-start | bytes 98312 | tf_op jit(solution)/shard_map/ppermute | solution.py:175
  7.3 3.9 %collective-permute-start.2 = (bf16[2,32,256]{2,1,0:T(8,128)(2,1)S(1)}, bf16[2,32,256]{2,1,0:T(8,128)(2,1)S(1)}, u32[]{:S(2)}, u32[]{:S(2)}) collective-permute-start(bf16[2,32,256]{2,1,0:T(8,128)(2,1)S(1)} %bitcast.93), channel_id=1, source_target_pairs={{0,24},{8,0},{16,8},{24,16},{1,25},{9,1},{17,9},{25,17},{2,26},{10... | collective-permute-start | bytes 98312 | tf_op jit(solution)/shard_map/ppermute | solution.py:175
  11.2 12.0 %copy-start.1 = (s32[2,16]{1,0:T(2,128)S(1)}, s32[2,16]{1,0:T(2,128)}, u32[]{:S(2)}) copy-start(s32[2,16]{1,0:T(2,128)} %param.15) | copy-start | bytes 388
  11.3 11.6 %collective-permute-start.4 = (bf16[4,2,32,256]{3,2,1,0:T(8,128)(2,1)S(1)}, bf16[4,2,32,256]{3,2,1,0:T(8,128)(2,1)S(1)}, u32[]{:S(2)}, u32[]{:S(2)}) collective-permute-start(bf16[4,2,32,256]{3,2,1,0:T(8,128)(2,1)S(1)} %get-tuple-element.33), channel_id=1, source_target_pairs={{0,4},{1,5},{2,6},{3,7},{4,0},{5,1},{6,2},{7,3},{8,12},{9,13},{10,... | collective-permute-start | bytes 393224 | tf_op jit(solution)/shard_map/ppermute | solution.py:192
  13.9 9.0 %collective-permute-start.5 = (bf16[4,2,32,256]{3,2,1,0:T(8,128)(2,1)S(1)}, bf16[4,2,32,256]{3,2,1,0:T(8,128)(2,1)S(1)}, u32[]{:S(2)}, u32[]{:S(2)}) collective-permute-start(bf16[4,2,32,256]{3,2,1,0:T(8,128)(2,1)S(1)} %get-tuple-element.33), channel_id=1, source_target_pairs={{0,6},{1,7},{2,0},{3,1},{4,2},{5,3},{6,4},{7,5},{8,14},{9,15},{10,... | collective-permute-start | bytes 393224 | tf_op jit(solution)/shard_map/ppermute | solution.py:192
  15.3 7.6 %collective-permute-start.3 = (bf16[4,2,32,256]{3,2,1,0:T(8,128)(2,1)S(1)}, bf16[4,2,32,256]{3,2,1,0:T(8,128)(2,1)S(1)}, u32[]{:S(2)}, u32[]{:S(2)}) collective-permute-start(bf16[4,2,32,256]{3,2,1,0:T(8,128)(2,1)S(1)} %get-tuple-element.33), channel_id=1, source_target_pairs={{0,2},{1,3},{2,4},{3,5},{4,6},{5,7},{6,0},{7,1},{8,10},{9,11},{10,... | collective-permute-start | bytes 393224 | tf_op jit(solution)/shard_map/ppermute | solution.py:192
  23.1 2.1 %collective-permute-start.6 = (bf16[4,4,2,32,256]{4,3,2,1,0:T(8,128)(2,1)S(1)}, bf16[4,4,2,32,256]{4,3,2,1,0:T(8,128)(2,1)}, u32[]{:S(2)}, u32[]{:S(2)}) collective-permute-start(bf16[4,4,2,32,256]{4,3,2,1,0:T(8,128)(2,1)S(1)} %get-tuple-element.17), channel_id=1, source_target_pairs={{0,1},{1,0},{2,3},{3,2},{4,5},{5,4},{6,7},{7,6},{8,9},{9,8},{10,11... | collective-permute-start | bytes 1572872 | tf_op jit(solution)/shard_map/ppermute | solution.py:200
  47.0 2.1 %collective-permute-start.7 = (bf16[2,4,4,32,256]{4,3,2,1,0:T(8,128)(2,1)S(1)}, bf16[2,4,4,32,256]{4,3,2,1,0:T(8,128)(2,1)}, u32[]{:S(2)}, u32[]{:S(2)}) collective-permute-start(bf16[2,4,4,32,256]{4,3,2,1,0:T(8,128)(2,1)S(1)} %fusion.5), channel_id=1, source_target_pairs={{0,1},{1,0},{2,3},{3,2},{4,5},{5,4},{6,7},{7,6},{8,9},{9,8},{10,11... | collective-permute-start | bytes 1572872 | tf_op jit(solution)/shard_map/ppermute | solution.py:148
  51.4 10.2 %collective-permute-start.10 = (bf16[2,4,32,256]{3,2,1,0:T(8,128)(2,1)}, bf16[2,4,32,256]{3,2,1,0:T(8,128)(2,1)S(1)}, u32[]{:S(2)}, u32[]{:S(2)}) collective-permute-start(bf16[2,4,32,256]{3,2,1,0:T(8,128)(2,1)} %get-tuple-element.14), channel_id=1, source_target_pairs={{0,6},{1,7},{2,0},{3,1},{4,2},{5,3},{6,4},{7,5},{8,14},{9,15},{10,... | collective-permute-start | bytes 393224 | tf_op jit(solution)/shard_map/ppermute | solution.py:161
  57.4 8.4 %collective-permute-start.8 = (bf16[2,4,32,256]{3,2,1,0:T(8,128)(2,1)}, bf16[2,4,32,256]{3,2,1,0:T(8,128)(2,1)S(1)}, u32[]{:S(2)}, u32[]{:S(2)}) collective-permute-start(bf16[2,4,32,256]{3,2,1,0:T(8,128)(2,1)} %get-tuple-element.13), channel_id=1, source_target_pairs={{0,2},{1,3},{2,4},{3,5},{4,6},{5,7},{6,0},{7,1},{8,10},{9,11},{10,... | collective-permute-start | bytes 393224 | tf_op jit(solution)/shard_map/ppermute | solution.py:161
  57.4 13.3 %collective-permute-start.9 = (bf16[2,4,32,256]{3,2,1,0:T(8,128)(2,1)}, bf16[2,4,32,256]{3,2,1,0:T(8,128)(2,1)S(1)}, u32[]{:S(2)}, u32[]{:S(2)}) collective-permute-start(bf16[2,4,32,256]{3,2,1,0:T(8,128)(2,1)} %get-tuple-element.15), channel_id=1, source_target_pairs={{0,4},{1,5},{2,6},{3,7},{4,0},{5,1},{6,2},{7,3},{8,12},{9,13},{10,... | collective-permute-start | bytes 393224 | tf_op jit(solution)/shard_map/ppermute | solution.py:161
  70.8 5.6 %collective-permute-start.11 = (f32[2,32,256]{2,1,0:T(8,128)S(1)}, f32[2,32,256]{2,1,0:T(8,128)S(1)}, u32[]{:S(2)}, u32[]{:S(2)}) collective-permute-start(f32[2,32,256]{2,1,0:T(8,128)S(1)} %get-tuple-element.31), channel_id=1, source_target_pairs={{0,8},{8,16},{16,24},{24,0},{1,9},{9,17},{17,25},{25,1},{2,10},{10... | collective-permute-start | bytes 196616 | tf_op jit(solution)/shard_map/ppermute | solution.py:213
  72.0 4.8 %collective-permute-start.12 = (f32[2,32,256]{2,1,0:T(8,128)S(1)}, f32[2,32,256]{2,1,0:T(8,128)S(1)}, u32[]{:S(2)}, u32[]{:S(2)}) collective-permute-start(f32[2,32,256]{2,1,0:T(8,128)S(1)} %get-tuple-element.30), channel_id=1, source_target_pairs={{0,16},{8,24},{16,0},{24,8},{1,17},{9,25},{17,1},{25,9},{2,18},{10... | collective-permute-start | bytes 196616 | tf_op jit(solution)/shard_map/ppermute | solution.py:213
  73.4 4.3 %collective-permute-start.13 = (f32[2,32,256]{2,1,0:T(8,128)S(1)}, f32[2,32,256]{2,1,0:T(8,128)S(1)}, u32[]{:S(2)}, u32[]{:S(2)}) collective-permute-start(f32[2,32,256]{2,1,0:T(8,128)S(1)} %get-tuple-element.29), channel_id=1, source_target_pairs={{0,24},{8,0},{16,8},{24,16},{1,25},{9,1},{17,9},{25,17},{2,26},{10... | collective-permute-start | bytes 196616 | tf_op jit(solution)/shard_map/ppermute | solution.py:213

commit v10 on v9

--- a/solution.py
+++ b/solution.py
@@ -235,13 +235,9 @@
     tiles_here = k_cache.shape[0] // TILE
 
     cand_rows = cand_x.reshape(micro * local_rows, model_width)
-    queries = jax.nn.silu(
-        jnp.dot(cand_rows, qu_weight[:, :model_width], preferred_element_type=jnp.float32)
-    )
-    queries = queries.astype(jnp.bfloat16).reshape(micro, local_rows, model_width)
-    gate_vals = jax.nn.silu(
-        jnp.dot(cand_rows, qu_weight[:, model_width:], preferred_element_type=jnp.float32)
-    ).astype(jnp.bfloat16)
+    projected = jax.nn.silu(jnp.dot(cand_rows, qu_weight, preferred_element_type=jnp.float32))
+    queries = projected[:, :model_width].astype(jnp.bfloat16).reshape(micro, local_rows, model_width)
+    gate_vals = projected[:, model_width:].astype(jnp.bfloat16)
     queries_all = gather_queries(queries, n_cand, n_hist)
     all_cands = queries_all.shape[1]
     window = 2 * all_cands // USERS

time: 81.6 us -> 81.7 us (level)
  starting transfers between devices: 21.2 us -> 17.7 us
  Pallas kernels: 17.9 us -> 21.3 us
  other arithmetic: 3.52 us -> 4.54 us
  matrix products: 5.46 us -> 4.46 us
    ppermute x3, starting transfers between devices: 7.15 us -> 3.77 us  [reduce_over_hist(): total = total + lax.ppermute(send, 'hist', perm=perm).astype(jnp.float32)]
    pallas_call x1, Pallas kernels: 17.9 us -> 21.3 us  [body(): pl.pallas_call(functools.partial(attend_kernel, window=window, heads_here...]
    dot_general x1, matrix products: 3.14 us -> 1.19 us  [body(): jnp.dot(mixed_rows, out_weight, preferred_element_type=jnp.float32)]
    add x1, other arithmetic: 0.06 us -> 1.09 us  [reduce_over_hist(): total = total + lax.ppermute(send, 'hist', perm=perm).astype(jnp.float32)]
    dot_general x1, matrix products: 2.31 us -> 3.27 us  [body(): jnp.dot(cand_rows, qu_weight, preferred_element_type=jnp.float32)]
where the time goes in v10:
time: 81.7 us; the launch traced here: 81.5 us
  waiting for transfers between devices  28.8 us (35%)
  Pallas kernels  21.3 us (26%)
  starting transfers between devices  17.7 us (22%)
  other arithmetic  4.54 us (6%)
  matrix products  4.46 us (5%)
  local copies, waits for them, and re-layouts  4.45 us (5%)
    pallas_call x1, Pallas kernels, body(): pl.pallas_call(functools.partial(attend_kernel, window=window, heads_here...  21.3 us
    ppermute x3, waiting for transfers between devices, reduce_over_hist(): total = total + lax.ppermute(send, 'hist', perm=perm).astype(jnp.float32)  12.2 us
    ppermute x3, waiting for transfers between devices, gather_queries(): by_offset.append(lax.ppermute(sources, 'hist', perm=perm))  6.94 us
    ppermute x3, starting transfers between devices, gather_queries(): lax.ppermute(piece, 'cand', perm=[(i, (i + shift) % n_cand) for i in rang...  5.94 us
    ppermute x3, starting transfers between devices, gather_queries(): by_offset.append(lax.ppermute(sources, 'hist', perm=perm))  4.68 us
    ppermute x3, starting transfers between devices, reduce_over_hist(): total = total + lax.ppermute(send, 'hist', perm=perm).astype(jnp.float32)  3.77 us
    ppermute x3, waiting for transfers between devices, spread_over_cand(): lax.ppermute(piece, 'cand', perm=[(i, (i + shift) % n_cand) for i in rang...  3.73 us
    dot_general x1, matrix products, body(): jnp.dot(cand_rows, qu_weight, preferred_element_type=jnp.float32)  3.27 us
  transfers between devices with their start and end apart: 14, of which 11 were waited for; matrix products, arithmetic and copies ran while one was open for 1% of the time, Pallas kernels for 0%

profile of v10, /device:TPU:0, one launch (start us, length us, event | category | flops | bytes accessed | tf_op | source)
XLA Modules:
  0.0 81.5 jit_solution(5885631895528821839)
XLA Ops:
  0.0 0.0 copy-start
  0.0 3.3 %multiply_convert_fusion = bf16[64,2048]{1,0:T(8,128)(2,1)S(1)} fusion(bf16[64,1024]{1,0:T(8,128)(2,1)} %bitcast.84, bf16[1024,2048]{1,0:T(8,128)(2,1)} %param.10), kind=kOutput, calls=%fused_computation.8 | convolution fusion | flops 269090816 | bytes 4587520 | tf_op jit(solution)/shard_map/dot_general | solution.py:238
  3.3 0.1 reshape_reshape.6
  3.4 0.3 constant_dynamic-slice_fusion.15
  3.7 3.0 %collective-permute-start = (bf16[2,32,256]{2,1,0:T(8,128)(2,1)S(1)}, bf16[2,32,256]{2,1,0:T(8,128)(2,1)S(1)}, u32[]{:S(2)}, u32[]{:S(2)}) collective-permute-start(bf16[2,32,256]{2,1,0:T(8,128)(2,1)S(1)} %bitcast.93), channel_id=1, source_target_pairs={{0,8},{8,16},{16,24},{24,0},{1,9},{9,17},{17,25},{25,1},{2,10},{10... | collective-permute-start | bytes 98312 | tf_op jit(solution)/shard_map/ppermute | solution.py:175
  6.7 1.5 %collective-permute-start.1 = (bf16[2,32,256]{2,1,0:T(8,128)(2,1)S(1)}, bf16[2,32,256]{2,1,0:T(8,128)(2,1)S(1)}, u32[]{:S(2)}, u32[]{:S(2)}) collective-permute-start(bf16[2,32,256]{2,1,0:T(8,128)(2,1)S(1)} %bitcast.94), channel_id=1, source_target_pairs={{0,16},{8,24},{16,0},{24,8},{1,17},{9,25},{17,1},{25,9},{2,18},{10... | collective-permute-start | bytes 98312 | tf_op jit(solution)/shard_map/ppermute | solution.py:175
  8.2 1.4 %collective-permute-start.2 = (bf16[2,32,256]{2,1,0:T(8,128)(2,1)S(1)}, bf16[2,32,256]{2,1,0:T(8,128)(2,1)S(1)}, u32[]{:S(2)}, u32[]{:S(2)}) collective-permute-start(bf16[2,32,256]{2,1,0:T(8,128)(2,1)S(1)} %bitcast.95), channel_id=1, source_target_pairs={{0,24},{8,0},{16,8},{24,16},{1,25},{9,1},{17,9},{25,17},{2,26},{10... | collective-permute-start | bytes 98312 | tf_op jit(solution)/shard_map/ppermute | solution.py:175
  9.7 0.0 collective-permute-done
  9.7 0.9 %collective-permute-done.1 = bf16[2,32,256]{2,1,0:T(8,128)(2,1)S(1)} collective-permute-done((bf16[2,32,256]{2,1,0:T(8,128)(2,1)S(1)}, bf16[2,32,256]{2,1,0:T(8,128)(2,1)S(1)}, u32[]{:S(2)}, u32[]{:S(2)}) %collective-permute-start.1) | collective-permute-done | bytes 32800 | tf_op jit(solution)/shard_map/ppermute | solution.py:175
  10.6 1.5 %collective-permute-done.2 = bf16[2,32,256]{2,1,0:T(8,128)(2,1)S(1)} collective-permute-done((bf16[2,32,256]{2,1,0:T(8,128)(2,1)S(1)}, bf16[2,32,256]{2,1,0:T(8,128)(2,1)S(1)}, u32[]{:S(2)}, u32[]{:S(2)}) %collective-permute-start.2) | collective-permute-done | bytes 32800 | tf_op jit(solution)/shard_map/ppermute | solution.py:175
  12.2 0.0 copy-start.2
  12.2 2.7 %collective-permute-start.4 = (bf16[4,2,32,256]{3,2,1,0:T(8,128)(2,1)S(1)}, bf16[4,2,32,256]{3,2,1,0:T(8,128)(2,1)S(1)}, u32[]{:S(2)}, u32[]{:S(2)}) collective-permute-start(bf16[4,2,32,256]{3,2,1,0:T(8,128)(2,1)S(1)} %get-tuple-element.33), channel_id=1, source_target_pairs={{0,4},{1,5},{2,6},{3,7},{4,0},{5,1},{6,2},{7,3},{8,12},{9,13},{10,... | collective-permute-start | bytes 393224 | tf_op jit(solution)/shard_map/ppermute | solution.py:192
  14.9 1.3 %collective-permute-start.5 = (bf16[4,2,32,256]{3,2,1,0:T(8,128)(2,1)S(1)}, bf16[4,2,32,256]{3,2,1,0:T(8,128)(2,1)S(1)}, u32[]{:S(2)}, u32[]{:S(2)}) collective-permute-start(bf16[4,2,32,256]{3,2,1,0:T(8,128)(2,1)S(1)} %get-tuple-element.33), channel_id=1, source_target_pairs={{0,6},{1,7},{2,0},{3,1},{4,2},{5,3},{6,4},{7,5},{8,14},{9,15},{10,... | collective-permute-start | bytes 393224 | tf_op jit(solution)/shard_map/ppermute | solution.py:192
  16.2 0.7 collective-permute-start.3
  16.9 6.9 %collective-permute-done.4 = bf16[4,2,32,256]{3,2,1,0:T(8,128)(2,1)S(1)} collective-permute-done((bf16[4,2,32,256]{3,2,1,0:T(8,128)(2,1)S(1)}, bf16[4,2,32,256]{3,2,1,0:T(8,128)(2,1)S(1)}, u32[]{:S(2)}, u32[]{:S(2)}) %collective-permute-start.4) | collective-permute-done | bytes 131104 | tf_op jit(solution)/shard_map/ppermute | solution.py:192
  23.9 0.0 collective-permute-done.5
  23.9 0.0 collective-permute-done.3
  23.9 0.1 pad_maximum_fusion
  24.0 0.1 fusion.12
  24.1 0.1 collective-permute-start.6
  24.2 0.0 copy-done.2
  24.2 0.6 reshape.56.count_ref
  24.8 1.4 %collective-permute-done.6 = bf16[4,4,2,32,256]{4,3,2,1,0:T(8,128)(2,1)} collective-permute-done((bf16[4,4,2,32,256]{4,3,2,1,0:T(8,128)(2,1)S(1)}, bf16[4,4,2,32,256]{4,3,2,1,0:T(8,128)(2,1)}, u32[]{:S(2)}, u32[]{:S(2)}) %collective-permute-start.6) | collective-permute-done | bytes 524320 | tf_op jit(solution)/shard_map/ppermute | solution.py:200
  26.2 1.4 %maximum_select_fusion = bf16[4,2,4,2,32,256]{5,4,3,2,0,1:T(8,128)(2,1)S(1)} fusion(bf16[4,1,4,2,32,256]{5,4,3,2,0,1:T(8,128)(2,1)} %bitcast.13, bf16[4,1,4,2,32,256]{5,4,3,2,0,1:T(8,128)(2,1)S(1)} %get-tuple-element.16, pred[]{:T(512)S(6)} %eq.29), kind=kLoop, calls=%fused_computation.2 | loop fusion | flops 1572864 | bytes 2097153 | tf_op jit(solution)/shard_map/jit(_where)/select_n | solution.py:201
  27.6 0.1 copy.25
  27.7 1.1 %copy.26 = bf16[2,4,8,32,256]{4,3,2,1,0:T(8,128)(2,1)} copy(bf16[2,4,8,32,256]{4,3,0,1,2:T(8,128)(2,1)S(1)} %bitcast.75) | data formatting | bytes 2097152 | tf_op jit(solution)/shard_map/transpose | solution.py:203
  28.8 21.3 %shard_map.91 = f32[2,1024,256]{2,1,0:T(8,128)} custom-call(s32[128]{0:T(128)} %owner_ref.1, s32[128]{0:T(128)} %rank_ref.1, s32[16]{0:T(128)} %len_ref.1, s32[32]{0:T(128)} %reshape.56.count_ref, bf16[2,1024,256]{2,1,0:T(8,128)(2,1)} %bitcast.74, bf16[16384,256]{1,0:T(8,128)(2,1)} %k_ref.1, bf16[16384,256]{1,0:T(8,128)(2,1)} %v_ref.1), custom_call_target="tpu_custom_call" | custom-call | tf_op jit(solution)/shard_map/pallas_call | solution.py:251
  50.0 1.3 %fusion.1 = bf16[2,4,4,32,256]{4,3,2,1,0:T(8,128)(2,1)S(1)} fusion(f32[2,4,4,2,32,256]{5,4,3,2,1,0:T(8,128)} %bitcast.72, s32[]{:T(128)S(6)} %select_n.187), kind=kLoop, calls=%fused_computation.5 | loop fusion | bytes 1048580 | tf_op jit(solution)/shard_map/convert_element_type | solution.py:149
  51.3 0.1 collective-permute-start.7
  51.5 2.0 %collective-permute-done.7 = bf16[2,4,4,32,256]{4,3,2,1,0:T(8,128)(2,1)} collective-permute-done((bf16[2,4,4,32,256]{4,3,2,1,0:T(8,128)(2,1)S(1)}, bf16[2,4,4,32,256]{4,3,2,1,0:T(8,128)(2,1)}, u32[]{:S(2)}, u32[]{:S(2)}) %collective-permute-start.7) | collective-permute-done | bytes 524320 | tf_op jit(solution)/shard_map/ppermute | solution.py:148
  53.4 1.5 %bitcast_add_fusion = f32[2,4,4,32,256]{4,3,2,1,0:T(8,128)S(1)} fusion(bf16[2,4,4,32,256]{4,3,2,1,0:T(8,128)(2,1)} %collective-permute-done.7, f32[2,4,4,2,32,256]{5,4,3,2,1,0:T(8,128)} %bitcast.73, s32[]{:T(128)S(6)} %select_n.186), kind=kLoop, calls=%fused_computation.3 | loop fusion | flops 524288 | bytes 2621444 | tf_op jit(solution)/shard_map/add | solution.py:151
  55.0 0.0 copy-start.1
  55.0 0.8 fusion.5
  55.8 2.4 %collective-permute-start.10 = (bf16[2,4,32,256]{3,2,1,0:T(8,128)(2,1)}, bf16[2,4,32,256]{3,2,1,0:T(8,128)(2,1)}, u32[]{:S(2)}, u32[]{:S(2)}) collective-permute-start(bf16[2,4,32,256]{3,2,1,0:T(8,128)(2,1)} %get-tuple-element.14), channel_id=1, source_target_pairs={{0,6},{1,7},{2,0},{3,1},{4,2},{5,3},{6,4},{7,5},{8,14},{9,15},{10,... | collective-permute-start | bytes 393224 | tf_op jit(solution)/shard_map/ppermute | solution.py:161
  58.2 0.0 collective-permute-start.8
  58.2 1.3 %collective-permute-start.9 = (bf16[2,4,32,256]{3,2,1,0:T(8,128)(2,1)}, bf16[2,4,32,256]{3,2,1,0:T(8,128)(2,1)}, u32[]{:S(2)}, u32[]{:S(2)}) collective-permute-start(bf16[2,4,32,256]{3,2,1,0:T(8,128)(2,1)} %get-tuple-element.15), channel_id=1, source_target_pairs={{0,4},{1,5},{2,6},{3,7},{4,0},{5,1},{6,2},{7,3},{8,12},{9,13},{10,... | collective-permute-start | bytes 393224 | tf_op jit(solution)/shard_map/ppermute | solution.py:161
  59.6 2.8 %collective-permute-done.10 = bf16[2,4,32,256]{3,2,1,0:T(8,128)(2,1)} collective-permute-done((bf16[2,4,32,256]{3,2,1,0:T(8,128)(2,1)}, bf16[2,4,32,256]{3,2,1,0:T(8,128)(2,1)}, u32[]{:S(2)}, u32[]{:S(2)}) %collective-permute-start.10) | collective-permute-done | bytes 131104 | tf_op jit(solution)/shard_map/ppermute | solution.py:161
  62.4 4.4 %collective-permute-done.8 = bf16[2,4,32,256]{3,2,1,0:T(8,128)(2,1)} collective-permute-done((bf16[2,4,32,256]{3,2,1,0:T(8,128)(2,1)}, bf16[2,4,32,256]{3,2,1,0:T(8,128)(2,1)}, u32[]{:S(2)}, u32[]{:S(2)}) %collective-permute-start.8) | collective-permute-done | bytes 131104 | tf_op jit(solution)/shard_map/ppermute | solution.py:161
  66.8 5.0 %collective-permute-done.9 = bf16[2,4,32,256]{3,2,1,0:T(8,128)(2,1)} collective-permute-done((bf16[2,4,32,256]{3,2,1,0:T(8,128)(2,1)}, bf16[2,4,32,256]{3,2,1,0:T(8,128)(2,1)}, u32[]{:S(2)}, u32[]{:S(2)}) %collective-permute-start.9) | collective-permute-done | bytes 131104 | tf_op jit(solution)/shard_map/ppermute | solution.py:161
  71.8 1.1 %fusion.3 = f32[2,4,32,256]{3,2,1,0:T(8,128)S(1)} fusion(bf16[2,4,32,256]{3,2,1,0:T(8,128)(2,1)} %collective-permute-done.10, bf16[2,4,32,256]{3,2,1,0:T(8,128)(2,1)} %collective-permute-done.9, bf16[2,4,32,256]{3,2,1,0:T(8,128)(2,1)} %collective-permute-done.8, f32[2,4,4,32,256]{4,3,2,1,0:T(8,128)S(1)} %bitcast_add_fusion, s32[]{:T(128)S(6)} %min.13), kind=kLoop, calls=%fused_computation.15 | loop fusion | flops 393216 | bytes 917508 | tf_op jit(solution)/shard_map/add | solution.py:161
  72.9 1.2 %collective-permute-start.11 = (f32[2,32,256]{2,1,0:T(8,128)S(1)}, f32[2,32,256]{2,1,0:T(8,128)S(1)}, u32[]{:S(2)}, u32[]{:S(2)}) collective-permute-start(f32[2,32,256]{2,1,0:T(8,128)S(1)} %get-tuple-element.31), channel_id=1, source_target_pairs={{0,8},{8,16},{16,24},{24,0},{1,9},{9,17},{17,25},{25,1},{2,10},{10... | collective-permute-start | bytes 196616 | tf_op jit(solution)/shard_map/ppermute | solution.py:213
  74.2 1.4 %collective-permute-start.12 = (f32[2,32,256]{2,1,0:T(8,128)S(1)}, f32[2,32,256]{2,1,0:T(8,128)S(1)}, u32[]{:S(2)}, u32[]{:S(2)}) collective-permute-start(f32[2,32,256]{2,1,0:T(8,128)S(1)} %get-tuple-element.30), channel_id=1, source_target_pairs={{0,16},{8,24},{16,0},{24,8},{1,17},{9,25},{17,1},{25,9},{2,18},{10... | collective-permute-start | bytes 196616 | tf_op jit(solution)/shard_map/ppermute | solution.py:213
  75.6 0.5 collective-permute-start.13
  76.1 2.4 %collective-permute-done.11 = f32[2,32,256]{2,1,0:T(8,128)S(1)} collective-permute-done((f32[2,32,256]{2,1,0:T(8,128)S(1)}, f32[2,32,256]{2,1,0:T(8,128)S(1)}, u32[]{:S(2)}, u32[]{:S(2)}) %collective-permute-start.11) | collective-permute-done | bytes 65568 | tf_op jit(solution)/shard_map/ppermute | solution.py:213
  78.5 0.5 collective-permute-done.12
  79.0 0.9 %collective-permute-done.13 = f32[2,32,256]{2,1,0:T(8,128)S(1)} collective-permute-done((f32[2,32,256]{2,1,0:T(8,128)S(1)}, f32[2,32,256]{2,1,0:T(8,128)S(1)}, u32[]{:S(2)}, u32[]{:S(2)}) %collective-permute-start.13) | collective-permute-done | bytes 65568 | tf_op jit(solution)/shard_map/ppermute | solution.py:213
  79.9 0.1 fusion.14
  80.0 0.1 div.26
  80.1 0.2 multiply_reduce_fusion
  80.3 0.0 copy-done
  80.3 0.0 copy-done.1
  80.3 1.2 %fusion = bf16[64,1024]{1,0:T(8,128)(2,1)} fusion(bf16[1024,1024]{1,0:T(8,128)(2,1)S(1)} %copy-done, bf16[64,1024]{1,0:T(8,128)(2,1)S(1)} %bitcast.85, f32[64,256]{1,0:T(8,128)S(1)} %bitcast.79, f32[64,256]{1,0:T(8,128)S(1)} %bitcast.81, f32[64,256]{1,0:T(8,128)S(1)} %bitcast.83, f32[64,256]{1,0:T(8,128)S(1)} %bitcast.77, ...), kind=kOutput, calls=%fused_computation.1 | convolution fusion | flops 134938624 | bytes 2753536 | tf_op jit(solution)/shard_map/dot_general | solution.py:276
  (13 shorter events, 0.2 us)
Async XLA Ops:
  0.0 80.3 %copy-start = (bf16[1024,1024]{1,0:T(8,128)(2,1)S(1)}, bf16[1024,1024]{1,0:T(8,128)(2,1)}, u32[]{:S(2)}) copy-start(bf16[1024,1024]{1,0:T(8,128)(2,1)} %param.11) | copy-start | bytes 6291460
  3.7 6.0 %collective-permute-start = (bf16[2,32,256]{2,1,0:T(8,128)(2,1)S(1)}, bf16[2,32,256]{2,1,0:T(8,128)(2,1)S(1)}, u32[]{:S(2)}, u32[]{:S(2)}) collective-permute-start(bf16[2,32,256]{2,1,0:T(8,128)(2,1)S(1)} %bitcast.93), channel_id=1, source_target_pairs={{0,8},{8,16},{16,24},{24,0},{1,9},{9,17},{17,25},{25,1},{2,10},{10... | collective-permute-start | bytes 98312 | tf_op jit(solution)/shard_map/ppermute | solution.py:175
  6.7 3.9 %collective-permute-start.1 = (bf16[2,32,256]{2,1,0:T(8,128)(2,1)S(1)}, bf16[2,32,256]{2,1,0:T(8,128)(2,1)S(1)}, u32[]{:S(2)}, u32[]{:S(2)}) collective-permute-start(bf16[2,32,256]{2,1,0:T(8,128)(2,1)S(1)} %bitcast.94), channel_id=1, source_target_pairs={{0,16},{8,24},{16,0},{24,8},{1,17},{9,25},{17,1},{25,9},{2,18},{10... | collective-permute-start | bytes 98312 | tf_op jit(solution)/shard_map/ppermute | solution.py:175
  8.2 3.9 %collective-permute-start.2 = (bf16[2,32,256]{2,1,0:T(8,128)(2,1)S(1)}, bf16[2,32,256]{2,1,0:T(8,128)(2,1)S(1)}, u32[]{:S(2)}, u32[]{:S(2)}) collective-permute-start(bf16[2,32,256]{2,1,0:T(8,128)(2,1)S(1)} %bitcast.95), channel_id=1, source_target_pairs={{0,24},{8,0},{16,8},{24,16},{1,25},{9,1},{17,9},{25,17},{2,26},{10... | collective-permute-start | bytes 98312 | tf_op jit(solution)/shard_map/ppermute | solution.py:175
  12.2 12.0 %copy-start.2 = (s32[2,16]{1,0:T(2,128)S(1)}, s32[2,16]{1,0:T(2,128)}, u32[]{:S(2)}) copy-start(s32[2,16]{1,0:T(2,128)} %param.15) | copy-start | bytes 388
  12.2 11.6 %collective-permute-start.4 = (bf16[4,2,32,256]{3,2,1,0:T(8,128)(2,1)S(1)}, bf16[4,2,32,256]{3,2,1,0:T(8,128)(2,1)S(1)}, u32[]{:S(2)}, u32[]{:S(2)}) collective-permute-start(bf16[4,2,32,256]{3,2,1,0:T(8,128)(2,1)S(1)} %get-tuple-element.33), channel_id=1, source_target_pairs={{0,4},{1,5},{2,6},{3,7},{4,0},{5,1},{6,2},{7,3},{8,12},{9,13},{10,... | collective-permute-start | bytes 393224 | tf_op jit(solution)/shard_map/ppermute | solution.py:192
  14.9 9.0 %collective-permute-start.5 = (bf16[4,2,32,256]{3,2,1,0:T(8,128)(2,1)S(1)}, bf16[4,2,32,256]{3,2,1,0:T(8,128)(2,1)S(1)}, u32[]{:S(2)}, u32[]{:S(2)}) collective-permute-start(bf16[4,2,32,256]{3,2,1,0:T(8,128)(2,1)S(1)} %get-tuple-element.33), channel_id=1, source_target_pairs={{0,6},{1,7},{2,0},{3,1},{4,2},{5,3},{6,4},{7,5},{8,14},{9,15},{10,... | collective-permute-start | bytes 393224 | tf_op jit(solution)/shard_map/ppermute | solution.py:192
  16.2 7.6 %collective-permute-start.3 = (bf16[4,2,32,256]{3,2,1,0:T(8,128)(2,1)S(1)}, bf16[4,2,32,256]{3,2,1,0:T(8,128)(2,1)S(1)}, u32[]{:S(2)}, u32[]{:S(2)}) collective-permute-start(bf16[4,2,32,256]{3,2,1,0:T(8,128)(2,1)S(1)} %get-tuple-element.33), channel_id=1, source_target_pairs={{0,2},{1,3},{2,4},{3,5},{4,6},{5,7},{6,0},{7,1},{8,10},{9,11},{10,... | collective-permute-start | bytes 393224 | tf_op jit(solution)/shard_map/ppermute | solution.py:192
  24.1 2.1 %collective-permute-start.6 = (bf16[4,4,2,32,256]{4,3,2,1,0:T(8,128)(2,1)S(1)}, bf16[4,4,2,32,256]{4,3,2,1,0:T(8,128)(2,1)}, u32[]{:S(2)}, u32[]{:S(2)}) collective-permute-start(bf16[4,4,2,32,256]{4,3,2,1,0:T(8,128)(2,1)S(1)} %get-tuple-element.17), channel_id=1, source_target_pairs={{0,1},{1,0},{2,3},{3,2},{4,5},{5,4},{6,7},{7,6},{8,9},{9,8},{10,11... | collective-permute-start | bytes 1572872 | tf_op jit(solution)/shard_map/ppermute | solution.py:200
  51.3 2.1 %collective-permute-start.7 = (bf16[2,4,4,32,256]{4,3,2,1,0:T(8,128)(2,1)S(1)}, bf16[2,4,4,32,256]{4,3,2,1,0:T(8,128)(2,1)}, u32[]{:S(2)}, u32[]{:S(2)}) collective-permute-start(bf16[2,4,4,32,256]{4,3,2,1,0:T(8,128)(2,1)S(1)} %fusion.1), channel_id=1, source_target_pairs={{0,1},{1,0},{2,3},{3,2},{4,5},{5,4},{6,7},{7,6},{8,9},{9,8},{10,11... | collective-permute-start | bytes 1572872 | tf_op jit(solution)/shard_map/ppermute | solution.py:148
  55.0 25.3 %copy-start.1 = (bf16[2,32,1024]{2,1,0:T(8,128)(2,1)S(1)}, bf16[2,32,1024]{2,1,0:T(8,128)(2,1)}, u32[]{:S(2)}) copy-start(bf16[2,32,1024]{2,1,0:T(8,128)(2,1)} %param.9) | copy-start | bytes 393220
  55.8 6.6 %collective-permute-start.10 = (bf16[2,4,32,256]{3,2,1,0:T(8,128)(2,1)}, bf16[2,4,32,256]{3,2,1,0:T(8,128)(2,1)}, u32[]{:S(2)}, u32[]{:S(2)}) collective-permute-start(bf16[2,4,32,256]{3,2,1,0:T(8,128)(2,1)} %get-tuple-element.14), channel_id=1, source_target_pairs={{0,6},{1,7},{2,0},{3,1},{4,2},{5,3},{6,4},{7,5},{8,14},{9,15},{10,... | collective-permute-start | bytes 393224 | tf_op jit(solution)/shard_map/ppermute | solution.py:161
  58.2 8.6 %collective-permute-start.8 = (bf16[2,4,32,256]{3,2,1,0:T(8,128)(2,1)}, bf16[2,4,32,256]{3,2,1,0:T(8,128)(2,1)}, u32[]{:S(2)}, u32[]{:S(2)}) collective-permute-start(bf16[2,4,32,256]{3,2,1,0:T(8,128)(2,1)} %get-tuple-element.13), channel_id=1, source_target_pairs={{0,2},{1,3},{2,4},{3,5},{4,6},{5,7},{6,0},{7,1},{8,10},{9,11},{10,... | collective-permute-start | bytes 393224 | tf_op jit(solution)/shard_map/ppermute | solution.py:161
  58.2 13.6 %collective-permute-start.9 = (bf16[2,4,32,256]{3,2,1,0:T(8,128)(2,1)}, bf16[2,4,32,256]{3,2,1,0:T(8,128)(2,1)}, u32[]{:S(2)}, u32[]{:S(2)}) collective-permute-start(bf16[2,4,32,256]{3,2,1,0:T(8,128)(2,1)} %get-tuple-element.15), channel_id=1, source_target_pairs={{0,4},{1,5},{2,6},{3,7},{4,0},{5,1},{6,2},{7,3},{8,12},{9,13},{10,... | collective-permute-start | bytes 393224 | tf_op jit(solution)/shard_map/ppermute | solution.py:161
  72.9 5.6 %collective-permute-start.11 = (f32[2,32,256]{2,1,0:T(8,128)S(1)}, f32[2,32,256]{2,1,0:T(8,128)S(1)}, u32[]{:S(2)}, u32[]{:S(2)}) collective-permute-start(f32[2,32,256]{2,1,0:T(8,128)S(1)} %get-tuple-element.31), channel_id=1, source_target_pairs={{0,8},{8,16},{16,24},{24,0},{1,9},{9,17},{17,25},{25,1},{2,10},{10... | collective-permute-start | bytes 196616 | tf_op jit(solution)/shard_map/ppermute | solution.py:213
  74.2 4.8 %collective-permute-start.12 = (f32[2,32,256]{2,1,0:T(8,128)S(1)}, f32[2,32,256]{2,1,0:T(8,128)S(1)}, u32[]{:S(2)}, u32[]{:S(2)}) collective-permute-start(f32[2,32,256]{2,1,0:T(8,128)S(1)} %get-tuple-element.30), channel_id=1, source_target_pairs={{0,16},{8,24},{16,0},{24,8},{1,17},{9,25},{17,1},{25,9},{2,18},{10... | collective-permute-start | bytes 196616 | tf_op jit(solution)/shard_map/ppermute | solution.py:213
  75.6 4.3 %collective-permute-start.13 = (f32[2,32,256]{2,1,0:T(8,128)S(1)}, f32[2,32,256]{2,1,0:T(8,128)S(1)}, u32[]{:S(2)}, u32[]{:S(2)}) collective-permute-start(f32[2,32,256]{2,1,0:T(8,128)S(1)} %get-tuple-element.29), channel_id=1, source_target_pairs={{0,24},{8,0},{16,8},{24,16},{1,25},{9,1},{17,9},{25,17},{2,26},{10... | collective-permute-start | bytes 196616 | tf_op jit(solution)/shard_map/ppermute | solution.py:213
